TPU v7x, 512 devices: a whole 4x4x16 slice. The times are simulated.
512 devices in a mesh: span: 128 (over z, x, y_hi), head: 4 (over y_lo, core).
Axes of the slice: x: 4, y: 4 (y_hi: 2, y_lo: 2; y = y_hi * 2 + y_lo), z: 16, core: 2. Of those that a mesh axis runs over, the one named last changes fastest.
Arguments:
- embedding_activity: bfloat16 [32768, 1024], P('span', 'head'), may hold values from -6 to 6
- common_lookup_projector: bfloat16 [1024, 1024], P(None, 'head'), may hold values from -0.1875 to 0.1875
- content_projector: bfloat16 [1024, 1024], P(None, 'head'), may hold values from -0.1875 to 0.1875
- final_projector: bfloat16 [1024, 1024], P('head'), may hold values from -3 to 3
- lane_sharpness: float32 [8], P('head'), may hold values from 4 to 16
- sorted_place_per_element: int32 [2, 32768], P(None, 'span'), may hold values from 0 to 32767, as said below
- element_per_sorted_place: int32 [2, 32768], P(None, 'span'), may hold values from 0 to 32767, as said below
Outputs:
- attended: bfloat16 [32768, 1024], P(('span', 'head'))
Inputs may be any that keep to these rules, and one draw needn't show every extreme that they name: `sorted_place_per_element`: each round's row is a permutation of the tokens' sorted slots; slots d * 256 to (d + 1) * 256 - 1 belong to index d of span. In every round at most 4 tokens of one device's positions go to the slots of one device, and some device receives exactly 4 from one device. element_per_sorted_place[r] is the inverse permutation of sorted_place_per_element[r].
All inputs are finite; a program needn't handle non-finite values.
Results may differ from a plain program's by a relative error of at most 0.014.
Values may be sent and summed in bfloat16 or wider, within the bound.
No kernel may reach another device: no remote copies, remote signals or barrier semaphores. Data moves between devices by JAX's collectives and lax.ppermute only.
A program may use at most 64 MiB of HBM per device.

v0:
```python
import jax
import jax.numpy as jnp
from jax import lax
from jax.sharding import PartitionSpec as P

HEAD_DIM = 128
BLOCK = 128


epsilon = 1e-05


def passed_along(block, axis, distance):
    devices = range(lax.axis_size(axis))
    route = [((i - distance) % len(devices), i) for i in devices]
    return lax.ppermute(block, axis, route)


def layer_norm(embedding_activity):
    content_embeddings = embedding_activity.astype(jnp.float32)
    row_mean = jnp.mean(content_embeddings, axis=-1, keepdims=True)
    centred = content_embeddings - row_mean
    row_var = jnp.mean(centred * centred, axis=-1, keepdims=True)
    return (centred * lax.rsqrt(row_var + epsilon)).astype(jnp.bfloat16)


def slot_sources(positions, slot_count):
    n_rounds, row_count = positions.shape
    round_ids = jnp.arange(n_rounds)[:, None]
    row_ids = jnp.broadcast_to(
        jnp.arange(row_count, dtype=jnp.int32)[None, :], (n_rounds, row_count)
    )
    return jnp.zeros((n_rounds, slot_count), jnp.int32).at[round_ids, positions].set(row_ids)


def dispatch(payload, send_pos, recv_pos, slot_count):
    n_rounds = send_pos.shape[0]
    fill_rows = slot_sources(send_pos, slot_count)
    outgoing = jnp.take(payload, fill_rows, axis=0)
    incoming = jnp.stack(
        [
            lax.all_to_all(outgoing[round_no], "span", split_axis=0, concat_axis=0, tiled=True)
            for round_no in range(n_rounds)
        ]
    )
    return jnp.take_along_axis(incoming, recv_pos[:, :, None], axis=1)


def send_back(results, softmax_normalizers, send_pos, recv_pos, slot_count):
    n_rounds = results.shape[0]
    fill_rows = slot_sources(recv_pos, slot_count)
    back_rows = jnp.take_along_axis(results, fill_rows[:, :, None], axis=1)
    back_totals = jnp.take_along_axis(softmax_normalizers, fill_rows[:, :, None], axis=1)
    pairs = [
        (
            lax.all_to_all(back_rows[round_no], "span", split_axis=0, concat_axis=0, tiled=True),
            lax.all_to_all(
                back_totals[round_no].astype(jnp.bfloat16),
                "span",
                split_axis=0,
                concat_axis=0,
                tiled=True,
            ).astype(jnp.float32),
        )
        for round_no in range(n_rounds)
    ]
    home_rows = jnp.stack([pair[0] for pair in pairs])
    home_totals = jnp.stack([pair[1] for pair in pairs])
    token_rows = jnp.take_along_axis(home_rows, send_pos[:, :, None], axis=1)
    token_totals = jnp.take_along_axis(home_totals, send_pos[:, :, None], axis=1)
    return (token_rows, token_totals)


def shards(
    embedding_activity,
    common_lookup_projector,
    content_projector,
    final_projector,
    lane_sharpness,
    sorted_place_per_element,
    element_per_sorted_place,
):
    n_dev = lax.axis_size("span")
    rows_here = embedding_activity.shape[0]
    capacity = 2 * rows_here // n_dev
    slot_count = n_dev * capacity
    n_rounds = sorted_place_per_element.shape[0]
    head_cols = common_lookup_projector.shape[1]
    heads_here = head_cols // HEAD_DIM
    blocks_here = rows_here // BLOCK
    round_ids = jnp.arange(n_rounds)[:, None]
    peer_ids = jnp.arange(n_dev, dtype=jnp.int32)
    target = sorted_place_per_element // rows_here
    onehot = (target[:, :, None] == peer_ids[None, None, :]).astype(jnp.int32)
    earlier = jnp.cumsum(onehot, axis=1) - onehot
    send_pos = target * capacity + jnp.sum(earlier * onehot, axis=2)
    source = element_per_sorted_place // rows_here
    within = element_per_sorted_place % rows_here
    present = (
        jnp.zeros((n_rounds, n_dev, rows_here), jnp.int32).at[round_ids, source, within].set(1)
    )
    before = jnp.cumsum(present, axis=2) - present
    recv_pos = source * capacity + before[round_ids, source, within]
    full_rows = lax.all_gather(embedding_activity, "head", axis=1, tiled=True)
    normed = layer_norm(full_rows)
    joined = jnp.concatenate([common_lookup_projector, content_projector], axis=1)
    both = jnp.dot(normed, joined, preferred_element_type=jnp.float32).astype(jnp.bfloat16)
    arrived = dispatch(both, send_pos, recv_pos, slot_count)
    sorted_shared = arrived[:, :, :head_cols]
    sorted_values = arrived[:, :, head_cols:]
    spread = sorted_shared.reshape(n_rounds, rows_here, heads_here, HEAD_DIM).astype(jnp.float32)
    unitlength_address_lines = (
        spread * lax.rsqrt(jnp.sum(spread * spread, axis=-1, keepdims=True) + 1e-06)
    ).astype(jnp.bfloat16)
    unitlength_address_lines = unitlength_address_lines.reshape(n_rounds, rows_here, head_cols)
    last_block = jnp.concatenate(
        [unitlength_address_lines[:, rows_here - BLOCK :], sorted_values[:, rows_here - BLOCK :]],
        axis=2,
    )
    prior_block = passed_along(last_block, "span", 1)
    keys_cur = unitlength_address_lines.reshape(n_rounds, blocks_here, BLOCK, head_cols)
    vals_cur = sorted_values.reshape(n_rounds, blocks_here, BLOCK, head_cols)
    keys_prev = jnp.concatenate([prior_block[:, None, :, :head_cols], keys_cur[:, :-1]], axis=1)
    vals_prev = jnp.concatenate([prior_block[:, None, :, head_cols:], vals_cur[:, :-1]], axis=1)
    key_rows = jnp.concatenate([keys_prev, keys_cur], axis=2).reshape(
        n_rounds, blocks_here, 2 * BLOCK, heads_here, HEAD_DIM
    )
    content_projector_lines = jnp.concatenate([vals_prev, vals_cur], axis=2).reshape(
        n_rounds, blocks_here, 2 * BLOCK, heads_here, HEAD_DIM
    )
    queries = keys_cur.reshape(n_rounds, blocks_here, BLOCK, heads_here, HEAD_DIM)
    similarity_energies = jnp.einsum(
        "rbqhd,rbkhd->rbhqk", queries, key_rows, preferred_element_type=jnp.float32
    )
    similarity_energies = similarity_energies * lane_sharpness[None, None, :, None, None]
    allowed = jnp.arange(2 * BLOCK)[None, :] != jnp.arange(BLOCK)[:, None] + BLOCK
    exp_scores = jnp.where(allowed, jnp.exp(similarity_energies), 0.0)
    row_totals = jnp.sum(exp_scores, axis=-1)
    weights = (exp_scores / row_totals[..., None]).astype(jnp.bfloat16)
    results = jnp.einsum(
        "rbhqk,rbkhd->rbqhd", weights, content_projector_lines, preferred_element_type=jnp.float32
    )
    results = results.astype(jnp.bfloat16).reshape(n_rounds, rows_here, head_cols)
    slot_totals = jnp.transpose(row_totals, (0, 1, 3, 2)).reshape(n_rounds, rows_here, heads_here)
    token_rows, token_totals = send_back(results, slot_totals, send_pos, recv_pos, slot_count)
    round_share = token_totals / jnp.sum(token_totals, axis=0)
    token_spread = token_rows.reshape(n_rounds, rows_here, heads_here, HEAD_DIM).astype(jnp.float32)
    combined = jnp.sum(round_share[..., None] * token_spread, axis=0).astype(jnp.bfloat16)
    combined = combined.reshape(rows_here, head_cols)
    return lax.psum_scatter(
        jnp.dot(combined, final_projector, preferred_element_type=jnp.float32).astype(jnp.bfloat16),
        "head",
        scatter_dimension=0,
        tiled=True,
    )


def solution(mesh):
    placed = (
        P("span", "head"),
        P(None, "head"),
        P(None, "head"),
        P("head", None),
        P("head"),
        P(None, "span"),
        P(None, "span"),
    )
    return jax.shard_map(
        shards, mesh=mesh, in_specs=placed, out_specs=P(("span", "head"), None), check_vma=False
    )
```

profile of v0, /device:TPU:6, one launch (start us, length us, event | category | flops | bytes accessed | tf_op | source)
XLA Modules:
  0.0 319.0 jit_solution(18114358778325544793)
XLA Ops:
  6.5 0.8 and_select_fusion.2
  7.5 0.4 fusion.24
  8.1 0.3 fusion.28
  8.4 0.6 fusion.46
  9.0 24.5 %scatter_fusion.2 = s32[2,512]{1,0:T(2,128)S(1)} fusion(s32[2,512]{1,0:T(2,128)S(1)} %broadcast.147.clone, s32[512]{0:T(512)S(1)} %bitcast.130, s32[512]{0:T(512)S(1)} %bitcast.148), kind=kCustom, calls=%fused_computation.9 | custom fusion | bytes 10240 | tf_op jit(solution)/shard_map/scatter | solution.py:33
  33.5 7.4 %all_gather.3 = bf16[256,1024]{1,0:T(8,128)(2,1)S(1)} all-gather(bf16[256,256]{1,0:T(8,128)(2,1)S(1)} %copy-done.1), channel_id=1, replica_groups=mesh['span'=128,'head'=4] {'head'}, dimensions={1}, use_global_device_ids=true | all-gather | bytes 655360 | tf_op jit(solution)/shard_map/all_gather | solution.py:104
  41.1 0.3 fusion.5
  41.4 0.5 convolution_convert_fusion.1
  41.9 4.0 %gather_fusion.1 = bf16[1024,512]{1,0:T(8,128)(2,1)S(1)} fusion(bf16[256,512]{1,0:T(8,128)(2,1)S(1)} %convolution_convert_fusion.1, s32[1024]{0:T(1024)S(1)} %broadcast_clamp_fusion), kind=kCustom, calls=%fused_computation.1 | custom fusion | bytes 2101248 | tf_op jit(solution)/shard_map/jit(_take)/gather | solution.py:39
  46.2 0.9 all_to_all.32
  47.1 21.8 %all-to-all-start = ((bf16[128,4,512]{2,1,0:T(4,128)(2,1)}), bf16[128,4,512]{2,1,0:T(4,128)(2,1)S(1)}, u32[]{:S(2)}, u32[]{:S(2)}) async-start(bf16[128,4,512]{2,1,0:T(4,128)(2,1)} %all_to_all.32), calls=%async_computation | async-start | bytes 1048576 | tf_op jit(solution)/shard_map/all_to_all | solution.py:42
  69.0 0.9 all_to_all.34
  70.0 31.4 %scatter_fusion = s32[2,128,256]{2,1,0:T(8,128)S(1)} fusion(s32[2,128,256]{2,1,0:T(8,128)S(1)} %broadcast_in_dim.131, s32[512]{0:T(512)S(1)} %bitcast.131, s32[512]{0:T(512)S(1)} %broadcast.290), kind=kCustom, calls=%fused_computation.7 | custom fusion | bytes 12288 | tf_op jit(solution)/shard_map/scatter | solution.py:100
  101.7 3.1 all-to-all-done
  104.8 15.4 %all-to-all-start.1 = ((bf16[128,4,512]{2,1,0:T(4,128)(2,1)}), bf16[128,4,512]{2,1,0:T(4,128)(2,1)S(1)}, u32[]{:S(2)}, u32[]{:S(2)}) async-start(bf16[128,4,512]{2,1,0:T(4,128)(2,1)} %all_to_all.34), calls=%async_computation.1 | async-start | bytes 1048576 | tf_op jit(solution)/shard_map/all_to_all | solution.py:42
  120.7 5.3 %gather_fusion = s32[512]{0:T(512)S(1)} fusion(s32[2,128,256]{2,1,0:T(8,128)S(1)} %sub.27, s32[512]{0:T(512)S(1)} %bitcast.133), kind=kCustom, calls=%fused_computation | custom fusion | bytes 10240 | tf_op jit(solution)/shard_map/gather | solution.py:103
  126.2 24.5 %scatter_fusion.1 = s32[2,512]{1,0:T(2,128)S(1)} fusion(s32[2,512]{1,0:T(2,128)S(1)} %broadcast.147.clone.1, s32[512]{0:T(512)S(1)} %bitcast.132, s32[512]{0:T(512)S(1)} %bitcast.149), kind=kCustom, calls=%fused_computation.8 | custom fusion | bytes 10240 | tf_op jit(solution)/shard_map/scatter | solution.py:33
  150.7 0.7 iota_compare_fusion.1
  151.6 3.9 %all-to-all-done.1 = bf16[128,4,512]{2,1,0:T(4,128)(2,1)S(1)} async-done(((bf16[128,4,512]{2,1,0:T(4,128)(2,1)}), bf16[128,4,512]{2,1,0:T(4,128)(2,1)S(1)}, u32[]{:S(2)}, u32[]{:S(2)}) %all-to-all-start.1) | async-done | bytes 524320 | tf_op jit(solution)/shard_map/all_to_all | solution.py:42
  155.7 3.9 %gather_fusion.2 = bf16[512,512]{1,0:T(8,128)(2,1)S(1)} fusion(bf16[2,512,512]{2,1,0:T(8,128)(2,1)S(1)} %pad_maximum_fusion, s32[512]{0:T(512)S(1)} %bitcast.129), kind=kCustom, calls=%fused_computation.2 | custom fusion | bytes 1052672 | tf_op jit(solution)/shard_map/jit(take_along_axis)/gather | solution.py:46
  160.0 0.6 add_rsqrt_fusion
  161.1 1.9 collective-permute-start
  163.0 0.6 mul.78
  163.6 0.4 mul.81
  164.1 0.3 reshape.267
  165.3 0.2 copy-done.3
  165.8 6.0 %collective-permute-done = bf16[2,128,512]{1,2,0:T(8,128)(2,1)S(1)} collective-permute-done((bf16[2,128,512]{1,2,0:T(8,128)(2,1)S(1)}, bf16[2,128,512]{1,2,0:T(8,128)(2,1)S(1)}, u32[]{:S(2)}, u32[]{:S(2)}) %collective-permute-start) | collective-permute-done | bytes 262176 | tf_op jit(solution)/shard_map/ppermute | solution.py:16
  172.0 1.3 fusion.57
  173.5 5.8 %gather_fusion.3 = bf16[1024,2]{1,0:T(8,128)(2,1)S(1)} fusion(bf16[2,256,2]{2,1,0:T(8,128)(2,1)S(1)} %bitcast.128, s32[1024]{0:T(1024)S(1)} %bitcast.124), kind=kCustom, calls=%fused_computation.3 | custom fusion | bytes 16384 | tf_op jit(solution)/shard_map/jit(take_along_axis)/gather | solution.py:53
  179.7 0.7 copy.105
  180.4 14.8 %all-to-all-start.2 = ((bf16[128,4,2]{1,2,0:T(2,128)(2,1)}), bf16[128,4,2]{1,2,0:T(2,128)(2,1)S(1)}, u32[]{:S(2)}, u32[]{:S(2)}) async-start(bf16[128,4,2]{1,2,0:T(2,128)(2,1)} %copy.105), calls=%async_computation.2 | async-start | bytes 131072 | tf_op jit(solution)/shard_map/all_to_all | solution.py:57
  195.2 0.4 fusion.4
  195.9 5.8 %gather_fusion.5 = bf16[1024,256]{1,0:T(8,128)(2,1)S(1)} fusion(bf16[2,256,256]{2,1,0:T(8,128)(2,1)S(1)} %reshape.194, s32[1024]{0:T(1024)S(1)} %bitcast.125), kind=kCustom, calls=%fused_computation.5 | custom fusion | bytes 1056768 | tf_op jit(solution)/shard_map/jit(take_along_axis)/gather | solution.py:52
  202.1 0.7 copy.107
  202.8 8.3 %all-to-all-done.2 = bf16[128,4,2]{1,2,0:T(2,128)(2,1)S(1)} async-done(((bf16[128,4,2]{1,2,0:T(2,128)(2,1)}), bf16[128,4,2]{1,2,0:T(2,128)(2,1)S(1)}, u32[]{:S(2)}, u32[]{:S(2)}) %all-to-all-start.2) | async-done | bytes 2080 | tf_op jit(solution)/shard_map/all_to_all | solution.py:57
  211.1 10.3 %all-to-all-start.3 = ((bf16[128,4,2]{1,2,0:T(2,128)(2,1)}), bf16[128,4,2]{1,2,0:T(2,128)(2,1)S(1)}, u32[]{:S(2)}, u32[]{:S(2)}) async-start(bf16[128,4,2]{1,2,0:T(2,128)(2,1)} %copy.107), calls=%async_computation.3 | async-start | bytes 131072 | tf_op jit(solution)/shard_map/all_to_all | solution.py:57
  221.4 0.8 all_to_all.38
  222.2 15.0 %all-to-all-done.3 = bf16[128,4,2]{1,2,0:T(2,128)(2,1)S(1)} async-done(((bf16[128,4,2]{1,2,0:T(2,128)(2,1)}), bf16[128,4,2]{1,2,0:T(2,128)(2,1)S(1)}, u32[]{:S(2)}, u32[]{:S(2)}) %all-to-all-start.3) | async-done | bytes 2080 | tf_op jit(solution)/shard_map/all_to_all | solution.py:57
  237.2 6.3 %all-to-all-start.4 = ((bf16[128,4,256]{2,1,0:T(4,128)(2,1)}), bf16[128,4,256]{2,1,0:T(4,128)(2,1)S(1)}, u32[]{:S(2)}, u32[]{:S(2)}) async-start(bf16[128,4,256]{2,1,0:T(4,128)(2,1)} %all_to_all.38), calls=%async_computation.4 | async-start | bytes 524288 | tf_op jit(solution)/shard_map/all_to_all | solution.py:56
  243.6 0.8 all_to_all.40
  244.3 20.4 %all-to-all-done.4 = bf16[128,4,256]{2,1,0:T(4,128)(2,1)S(1)} async-done(((bf16[128,4,256]{2,1,0:T(4,128)(2,1)}), bf16[128,4,256]{2,1,0:T(4,128)(2,1)S(1)}, u32[]{:S(2)}, u32[]{:S(2)}) %all-to-all-start.4) | async-done | bytes 262176 | tf_op jit(solution)/shard_map/all_to_all | solution.py:56
  264.7 6.1 %all-to-all-start.5 = ((bf16[128,4,256]{2,1,0:T(4,128)(2,1)}), bf16[128,4,256]{2,1,0:T(4,128)(2,1)S(1)}, u32[]{:S(2)}, u32[]{:S(2)}) async-start(bf16[128,4,256]{2,1,0:T(4,128)(2,1)} %all_to_all.40), calls=%async_computation.5 | async-start | bytes 524288 | tf_op jit(solution)/shard_map/all_to_all | solution.py:56
  271.4 3.7 %gather_fusion.4 = f32[512,2]{1,0:T(8,128)S(1)} fusion(f32[2,512,2]{2,1,0:T(8,128)S(1)} %copy.109, s32[512]{0:T(512)S(1)} %bitcast.126), kind=kCustom, calls=%fused_computation.4 | custom fusion | bytes 12288 | tf_op jit(solution)/shard_map/jit(take_along_axis)/gather | solution.py:70
  275.4 16.3 %all-to-all-done.5 = bf16[128,4,256]{2,1,0:T(4,128)(2,1)S(1)} async-done(((bf16[128,4,256]{2,1,0:T(4,128)(2,1)}), bf16[128,4,256]{2,1,0:T(4,128)(2,1)S(1)}, u32[]{:S(2)}, u32[]{:S(2)}) %all-to-all-start.5) | async-done | bytes 262176 | tf_op jit(solution)/shard_map/all_to_all | solution.py:56
  291.8 3.2 gather_fusion.6
  295.1 1.6 multiply_reduce_fusion
  296.7 1.1 convolution_convert_fusion
  297.8 14.4 %reduce-scatter.2.cloned.1.call-done = bf16[64,1024]{1,0:T(8,128)(2,1)} async-done(((bf16[256,1024]{1,0:T(8,128)(2,1)}), bf16[64,1024]{1,0:T(8,128)(2,1)}) %reduce-scatter.2.cloned.1.call-update) | async-done | bytes 131088 | tf_op jit(solution)/shard_map/reduce_scatter | solution.py:150
  (119 shorter events, 6.5 us)
Async XLA Ops:
  6.5 290.1 %copy-start = (bf16[256,1024]{1,0:T(8,128)(2,1)S(1)}, bf16[256,1024]{1,0:T(8,128)(2,1)}, u32[]{:S(2)}) copy-start(bf16[256,1024]{1,0:T(8,128)(2,1)} %param.10) | copy-start | bytes 1572868
  6.5 1.8 copy-start.4
  9.0 24.6 %copy-start.1 = (bf16[256,256]{1,0:T(8,128)(2,1)S(1)}, bf16[256,256]{1,0:T(8,128)(2,1)}, u32[]{:S(2)}) copy-start(bf16[256,256]{1,0:T(8,128)(2,1)} %param.7) | copy-start | bytes 393220
  33.5 7.9 %copy-start.7 = (bf16[1024,256]{1,0:T(8,128)(2,1)S(1)}, bf16[1024,256]{1,0:T(8,128)(2,1)}, u32[]{:S(2)}) copy-start(bf16[1024,256]{1,0:T(8,128)(2,1)} %param.9) | copy-start | bytes 1572868
  33.5 7.9 %copy-start.8 = (bf16[1024,256]{1,0:T(8,128)(2,1)S(1)}, bf16[1024,256]{1,0:T(8,128)(2,1)}, u32[]{:S(2)}) copy-start(bf16[1024,256]{1,0:T(8,128)(2,1)} %param.8) | copy-start | bytes 1572868
  47.1 22.8 %copy-start.6 = (s32[2,256]{1,0:T(2,128)S(1)}, s32[2,256]{1,0:T(2,128)}, u32[]{:S(2)}) copy-start(s32[2,256]{1,0:T(2,128)} %param.13) | copy-start | bytes 6148
  47.1 57.6 %all-to-all-start = ((bf16[128,4,512]{2,1,0:T(4,128)(2,1)}), bf16[128,4,512]{2,1,0:T(4,128)(2,1)S(1)}, u32[]{:S(2)}, u32[]{:S(2)}) async-start(bf16[128,4,512]{2,1,0:T(4,128)(2,1)} %all_to_all.32), calls=%async_computation | async-start | bytes 1048576 | tf_op jit(solution)/shard_map/all_to_all | solution.py:42
  104.8 50.7 %all-to-all-start.1 = ((bf16[128,4,512]{2,1,0:T(4,128)(2,1)}), bf16[128,4,512]{2,1,0:T(4,128)(2,1)S(1)}, u32[]{:S(2)}, u32[]{:S(2)}) async-start(bf16[128,4,512]{2,1,0:T(4,128)(2,1)} %all_to_all.34), calls=%async_computation.1 | async-start | bytes 1048576 | tf_op jit(solution)/shard_map/all_to_all | solution.py:42
  161.1 10.7 %collective-permute-start = (bf16[2,128,512]{1,2,0:T(8,128)(2,1)S(1)}, bf16[2,128,512]{1,2,0:T(8,128)(2,1)S(1)}, u32[]{:S(2)}, u32[]{:S(2)}) collective-permute-start(bf16[2,128,512]{1,2,0:T(8,128)(2,1)S(1)} %pad_maximum_fusion.2), channel_id=1, source_target_pairs={{508,0},{0,4},{4,8},{8,12},{12,16},{16,20},{20,24},{24,28},{28,32}... | collective-permute-start | bytes 786440 | tf_op jit(solution)/shard_map/ppermute | solution.py:16
  164.9 0.7 copy-start.3
  165.3 6.7 %copy-start.2 = (pred[128,256]{1,0:T(8,128)(4,1)S(1)}, pred[128,256]{1,0:T(8,128)(4,1)}, u32[]{:S(2)}) copy-start(pred[128,256]{1,0:T(8,128)(4,1)} %iota_compare_fusion.1) | copy-start | bytes 98308
  165.3 6.7 %copy-start.9 = (f32[2]{0:T(128)S(1)}, f32[2]{0:T(128)}, u32[]{:S(2)}) copy-start(f32[2]{0:T(128)} %param.11) | copy-start | bytes 28
  173.5 21.7 %copy-start.10 = (f32[2,2,2,128,256]{4,3,2,1,0:T(8,128)S(1)}, f32[2,2,2,128,256]{4,3,2,1,0:T(8,128)}, u32[]{:S(2)}) copy-start(f32[2,2,2,128,256]{4,3,2,1,0:T(8,128)} %get-tuple-element.27) | copy-start | bytes 3145732
  180.4 30.7 %all-to-all-start.2 = ((bf16[128,4,2]{1,2,0:T(2,128)(2,1)}), bf16[128,4,2]{1,2,0:T(2,128)(2,1)S(1)}, u32[]{:S(2)}, u32[]{:S(2)}) async-start(bf16[128,4,2]{1,2,0:T(2,128)(2,1)} %copy.105), calls=%async_computation.2 | async-start | bytes 131072 | tf_op jit(solution)/shard_map/all_to_all | solution.py:57
  211.1 26.1 %all-to-all-start.3 = ((bf16[128,4,2]{1,2,0:T(2,128)(2,1)}), bf16[128,4,2]{1,2,0:T(2,128)(2,1)S(1)}, u32[]{:S(2)}, u32[]{:S(2)}) async-start(bf16[128,4,2]{1,2,0:T(2,128)(2,1)} %copy.107), calls=%async_computation.3 | async-start | bytes 131072 | tf_op jit(solution)/shard_map/all_to_all | solution.py:57
  221.4 49.5 %copy-start.5 = (s32[1,2,2,128]{3,2,1,0:T(2,128)S(1)}, s32[1,2,2,128]{3,2,1,0:T(2,128)}, u32[]{:S(2)}) copy-start(s32[1,2,2,128]{3,2,1,0:T(2,128)} %get-tuple-element.24) | copy-start | bytes 6148
  237.2 27.5 %all-to-all-start.4 = ((bf16[128,4,256]{2,1,0:T(4,128)(2,1)}), bf16[128,4,256]{2,1,0:T(4,128)(2,1)S(1)}, u32[]{:S(2)}, u32[]{:S(2)}) async-start(bf16[128,4,256]{2,1,0:T(4,128)(2,1)} %all_to_all.38), calls=%async_computation.4 | async-start | bytes 524288 | tf_op jit(solution)/shard_map/all_to_all | solution.py:56
  264.7 27.0 %all-to-all-start.5 = ((bf16[128,4,256]{2,1,0:T(4,128)(2,1)}), bf16[128,4,256]{2,1,0:T(4,128)(2,1)S(1)}, u32[]{:S(2)}, u32[]{:S(2)}) async-start(bf16[128,4,256]{2,1,0:T(4,128)(2,1)} %all_to_all.40), calls=%async_computation.5 | async-start | bytes 524288 | tf_op jit(solution)/shard_map/all_to_all | solution.py:56
  270.8 41.4 %reduce-scatter.2.cloned.1.call-start = ((), (), s32[]{:S(2)}) async-start(), calls=%async_computation.7 | async-start | bytes 655360 | tf_op jit(solution)/shard_map/reduce_scatter | solution.py:150
Sparse Core Ops, SparseCore 0:
  297.9 14.2 reduce-scatter.1
where the time goes:
time: 321 us; the launch traced here: 319 us
  local copies, waits for them, and re-layouts  123 us (38%)
  waiting for transfers between devices  87.4 us (27%)
  starting transfers between devices  76.8 us (24%)
  between operations  14.3 us (4%)
  blocking collectives  7.39 us (2%)
  other arithmetic  7.24 us (2%)
  matrix products  3.32 us (1%)
    scatter x2, local copies, waits for them, and re-layouts, slot_sources(): jnp.zeros((n_rounds, slot_count), jnp.int32).at[round_ids, positions]  49 us
    all_to_all x2, starting transfers between devices, dispatch(): lax.all_to_all(outgoing[round_no], 'span', split_axis=0, concat_axis=0, t...  37.3 us
    all_to_all x2, waiting for transfers between devices, send_back(): lax.all_to_all(back_rows[round_no], 'span', split_axis=0, concat_axis=0,...  36.6 us
    scatter x1, local copies, waits for them, and re-layouts, shards(): jnp.zeros((n_rounds, n_dev, rows_here), jnp.int32)  31.4 us
    all_to_all x2, starting transfers between devices, send_back(): lax.all_to_all(back_totals[round_no].astype(jnp.bfloat16), 'span', split_...  25.1 us
    all_to_all x2, waiting for transfers between devices, send_back(): lax.all_to_all(back_totals[round_no].astype(jnp.bfloat16), 'span', split_...  23.3 us
    reduce_scatter x1, waiting for transfers between devices, shards(): lax.psum_scatter(jnp.dot(combined, final_projector, preferred_element_typ...  14.4 us
    all_to_all x2, starting transfers between devices, send_back(): lax.all_to_all(back_rows[round_no], 'span', split_axis=0, concat_axis=0,...  12.5 us
  transfers between devices with their start and end apart: 8, of which 8 were waited for; matrix products, arithmetic and copies ran while one was open for 24% of the time, Pallas kernels for 0%

commit v1 on v0

--- a/solution.py
+++ b/solution.py
@@ -24,51 +24,16 @@
     return (centred * lax.rsqrt(row_var + epsilon)).astype(jnp.bfloat16)
 
 
-def slot_sources(positions, slot_count):
-    n_rounds, row_count = positions.shape
-    round_ids = jnp.arange(n_rounds)[:, None]
-    row_ids = jnp.broadcast_to(
-        jnp.arange(row_count, dtype=jnp.int32)[None, :], (n_rounds, row_count)
-    )
-    return jnp.zeros((n_rounds, slot_count), jnp.int32).at[round_ids, positions].set(row_ids)
+def rank_within_group(group, order):
+    same = group[:, :, None] == group[:, None, :]
+    earlier = order[:, None, :] < order[:, :, None]
+    return jnp.sum((same & earlier).astype(jnp.int32), axis=2)
 
 
-def dispatch(payload, send_pos, recv_pos, slot_count):
-    n_rounds = send_pos.shape[0]
-    fill_rows = slot_sources(send_pos, slot_count)
-    outgoing = jnp.take(payload, fill_rows, axis=0)
-    incoming = jnp.stack(
-        [
-            lax.all_to_all(outgoing[round_no], "span", split_axis=0, concat_axis=0, tiled=True)
-            for round_no in range(n_rounds)
-        ]
+def one_hot_rows(index, count):
+    return (index[:, :, None] == jnp.arange(count, dtype=jnp.int32)[None, None, :]).astype(
+        jnp.bfloat16
     )
-    return jnp.take_along_axis(incoming, recv_pos[:, :, None], axis=1)
-
-
-def send_back(results, softmax_normalizers, send_pos, recv_pos, slot_count):
-    n_rounds = results.shape[0]
-    fill_rows = slot_sources(recv_pos, slot_count)
-    back_rows = jnp.take_along_axis(results, fill_rows[:, :, None], axis=1)
-    back_totals = jnp.take_along_axis(softmax_normalizers, fill_rows[:, :, None], axis=1)
-    pairs = [
-        (
-            lax.all_to_all(back_rows[round_no], "span", split_axis=0, concat_axis=0, tiled=True),
-            lax.all_to_all(
-                back_totals[round_no].astype(jnp.bfloat16),
-                "span",
-                split_axis=0,
-                concat_axis=0,
-                tiled=True,
-            ).astype(jnp.float32),
-        )
-        for round_no in range(n_rounds)
-    ]
-    home_rows = jnp.stack([pair[0] for pair in pairs])
-    home_totals = jnp.stack([pair[1] for pair in pairs])
-    token_rows = jnp.take_along_axis(home_rows, send_pos[:, :, None], axis=1)
-    token_totals = jnp.take_along_axis(home_totals, send_pos[:, :, None], axis=1)
-    return (token_rows, token_totals)
 
 
 def shards(
@@ -83,29 +48,41 @@
     n_dev = lax.axis_size("span")
     rows_here = embedding_activity.shape[0]
     capacity = 2 * rows_here // n_dev
-    slot_count = n_dev * capacity
     n_rounds = sorted_place_per_element.shape[0]
+    per_peer = n_rounds * capacity
+    buffer_rows = n_dev * per_peer
     head_cols = common_lookup_projector.shape[1]
     heads_here = head_cols // HEAD_DIM
     blocks_here = rows_here // BLOCK
-    round_ids = jnp.arange(n_rounds)[:, None]
-    peer_ids = jnp.arange(n_dev, dtype=jnp.int32)
+    round_ids = jnp.arange(n_rounds, dtype=jnp.int32)[:, None]
+    local_ids = jnp.broadcast_to(
+        jnp.arange(rows_here, dtype=jnp.int32)[None, :], (n_rounds, rows_here)
+    )
+
     target = sorted_place_per_element // rows_here
-    onehot = (target[:, :, None] == peer_ids[None, None, :]).astype(jnp.int32)
-    earlier = jnp.cumsum(onehot, axis=1) - onehot
-    send_pos = target * capacity + jnp.sum(earlier * onehot, axis=2)
+    send_rank = rank_within_group(target, local_ids)
+    send_row = target * per_peer + round_ids * capacity + send_rank
+    send_hot = one_hot_rows(send_row, buffer_rows)
+
     source = element_per_sorted_place // rows_here
     within = element_per_sorted_place % rows_here
-    present = (
-        jnp.zeros((n_rounds, n_dev, rows_here), jnp.int32).at[round_ids, source, within].set(1)
-    )
-    before = jnp.cumsum(present, axis=2) - present
-    recv_pos = source * capacity + before[round_ids, source, within]
+    recv_rank = rank_within_group(source, within)
+    recv_row = source * per_peer + round_ids * capacity + recv_rank
+    recv_hot = one_hot_rows(recv_row, buffer_rows)
+
     full_rows = lax.all_gather(embedding_activity, "head", axis=1, tiled=True)
     normed = layer_norm(full_rows)
     joined = jnp.concatenate([common_lookup_projector, content_projector], axis=1)
     both = jnp.dot(normed, joined, preferred_element_type=jnp.float32).astype(jnp.bfloat16)
-    arrived = dispatch(both, send_pos, recv_pos, slot_count)
+
+    outgoing = jnp.einsum(
+        "rtq,tw->qw", send_hot, both, preferred_element_type=jnp.float32
+    ).astype(jnp.bfloat16)
+    incoming = lax.all_to_all(outgoing, "span", split_axis=0, concat_axis=0, tiled=True)
+    arrived = jnp.einsum(
+        "rsq,qw->rsw", recv_hot, incoming, preferred_element_type=jnp.float32
+    ).astype(jnp.bfloat16)
+
     sorted_shared = arrived[:, :, :head_cols]
     sorted_values = arrived[:, :, head_cols:]
     spread = sorted_shared.reshape(n_rounds, rows_here, heads_here, HEAD_DIM).astype(jnp.float32)
@@ -142,9 +119,22 @@
     )
     results = results.astype(jnp.bfloat16).reshape(n_rounds, rows_here, head_cols)
     slot_totals = jnp.transpose(row_totals, (0, 1, 3, 2)).reshape(n_rounds, rows_here, heads_here)
-    token_rows, token_totals = send_back(results, slot_totals, send_pos, recv_pos, slot_count)
+    totals_high = slot_totals.astype(jnp.bfloat16)
+    totals_low = (slot_totals - totals_high.astype(jnp.float32)).astype(jnp.bfloat16)
+    back_payload = jnp.concatenate([results, totals_high, totals_low], axis=2)
+
+    back = jnp.einsum(
+        "rsq,rsw->qw", recv_hot, back_payload, preferred_element_type=jnp.float32
+    ).astype(jnp.bfloat16)
+    home = lax.all_to_all(back, "span", split_axis=0, concat_axis=0, tiled=True)
+    token_all = jnp.einsum("rtq,qw->rtw", send_hot, home, preferred_element_type=jnp.float32)
+    token_rows = token_all[:, :, :head_cols]
+    token_totals = (
+        token_all[:, :, head_cols : head_cols + heads_here]
+        + token_all[:, :, head_cols + heads_here : head_cols + 2 * heads_here]
+    )
     round_share = token_totals / jnp.sum(token_totals, axis=0)
-    token_spread = token_rows.reshape(n_rounds, rows_here, heads_here, HEAD_DIM).astype(jnp.float32)
+    token_spread = token_rows.reshape(n_rounds, rows_here, heads_here, HEAD_DIM)
     combined = jnp.sum(round_share[..., None] * token_spread, axis=0).astype(jnp.bfloat16)
     combined = combined.reshape(rows_here, head_cols)
     return lax.psum_scatter(

time: 321 us -> 194 us (0.60)
  local copies, waits for them, and re-layouts: 123 us -> 3.78 us
  blocking collectives: 7.39 us -> 61.2 us
  starting transfers between devices: 76.8 us -> 23.7 us
  waiting for transfers between devices: 87.4 us -> 79.2 us
    scatter x3 -> x0, local copies, waits for them, and re-layouts: 80.4 us -> none  [the longest x2 49 us: slot_sources(): jnp.zeros((n_rounds, slot_count), jnp.int32).at[round_ids, positions]]
    all_to_all x0 -> x1, blocking collectives: none -> 53.6 us  [shards(): home = lax.all_to_all(back, 'span', split_axis=0, concat_axis=0, tiled=True)]
    all_to_all x6 -> x1, starting transfers between devices: 74.8 us -> 21.7 us  [shards(): lax.all_to_all(outgoing, 'span', split_axis=0, concat_axis=0, tiled=True)]
    gather x11 -> x0, local copies, waits for them, and re-layouts: 32.1 us -> none  [the longest x2 5.97 us: send_back(): jnp.take_along_axis(softmax_normalizers, fill_rows[:, :, None], axis=1)]
    all_to_all x6 -> x1, waiting for transfers between devices: 66.9 us -> 57 us  [shards(): lax.all_to_all(outgoing, 'span', split_axis=0, concat_axis=0, tiled=True)]
    dot_general x1 -> x4, matrix products: 0.49 us -> 3.98 us  [the longest x1 1.89 us: shards(): jnp.einsum('rtq,tw->qw', send_hot, both, preferred_element_type=jnp.float32)]
    all_to_all x6 -> x0, local copies, waits for them, and re-layouts: 3.39 us -> none  [the longest x2 1.85 us: dispatch(): lax.all_to_all(outgoing[round_no], 'span', split_axis=0, concat_axis=0, t...]
  transfers between devices with their start and end apart: 8 -> 3, of which waited for: 8 -> 3; matrix products, arithmetic and copies ran while one was open for 24% -> 1% of each run, Pallas kernels for 0% -> 0%
where the time goes in v1:
time: 194 us; the launch traced here: 192 us
  waiting for transfers between devices  79.2 us (41%)
  blocking collectives  61.2 us (32%)
  starting transfers between devices  23.7 us (12%)
  between operations  13.7 us (7%)
  matrix products  5.92 us (3%)
  other arithmetic  4.52 us (2%)
  local copies, waits for them, and re-layouts  3.78 us (2%)
    all_to_all x1, waiting for transfers between devices, shards(): lax.all_to_all(outgoing, 'span', split_axis=0, concat_axis=0, tiled=True)  57 us
    all_to_all x1, blocking collectives, shards(): home = lax.all_to_all(back, 'span', split_axis=0, concat_axis=0, tiled=True)  53.6 us
    all_to_all x1, starting transfers between devices, shards(): lax.all_to_all(outgoing, 'span', split_axis=0, concat_axis=0, tiled=True)  21.7 us
    reduce_scatter x1, waiting for transfers between devices, shards(): lax.psum_scatter(jnp.dot(combined, final_projector, preferred_element_typ...  14.6 us
    ppermute x1, waiting for transfers between devices, passed_along(): return lax.ppermute(block, axis, route)  7.63 us
    all_gather x1, blocking collectives, shards(): full_rows = lax.all_gather(embedding_activity, 'head', axis=1, tiled=True)  7.6 us
  transfers between devices with their start and end apart: 3, of which 3 were waited for; matrix products, arithmetic and copies ran while one was open for 1% of the time, Pallas kernels for 0%

profile of v1, /device:TPU:6, one launch (start us, length us, event | category | flops | bytes accessed | tf_op | source)
XLA Modules:
  0.0 192.0 jit_solution(4594289631952886897)
XLA Ops:
  6.6 0.7 and_select_fusion.2
  7.3 0.7 and_select_fusion.1
  8.0 0.0 copy-start.3
  8.0 0.0 copy-start.4
  8.0 7.6 %all_gather.3 = bf16[256,1024]{1,0:T(8,128)(2,1)S(1)} all-gather(bf16[256,256]{1,0:T(8,128)(2,1)} %param.7), channel_id=1, replica_groups=mesh['span'=128,'head'=4] {'head'}, dimensions={1}, use_global_device_ids=true | all-gather | bytes 655360 | tf_op jit(solution)/shard_map/all_gather | solution.py:73
  15.6 0.1 convert_reduce_fusion.1
  15.8 0.3 fusion.13
  16.1 0.5 convert_reduce_fusion.2
  16.6 0.1 add_add_fusion
  16.6 0.3 convert_reduce_fusion
  16.9 1.9 fusion.5
  18.8 21.7 %all-to-all-start = ((bf16[128,8,512]{2,1,0:T(8,128)(2,1)}), bf16[128,8,512]{2,1,0:T(8,128)(2,1)S(1)}, u32[]{:S(2)}, u32[]{:S(2)}) async-start(bf16[128,8,512]{2,1,0:T(8,128)(2,1)} %fusion.5), calls=%async_computation | async-start | bytes 2097152 | tf_op jit(solution)/shard_map/all_to_all | solution.py:81
  40.5 0.0 reduce-scatter.2.cloned.1.call-start
  40.6 0.7 iota_compare_fusion.12
  41.3 57.0 %all-to-all-done = bf16[128,8,512]{2,1,0:T(8,128)(2,1)S(1)} async-done(((bf16[128,8,512]{2,1,0:T(8,128)(2,1)}), bf16[128,8,512]{2,1,0:T(8,128)(2,1)S(1)}, u32[]{:S(2)}, u32[]{:S(2)}) %all-to-all-start) | async-done | bytes 1048608 | tf_op jit(solution)/shard_map/all_to_all | solution.py:81
  98.2 0.7 fusion.9
  99.1 0.1 fusion.60
  99.1 0.3 mul.82
  99.4 0.6 reduce_sum.86
  100.1 0.6 mul.83
  100.7 0.4 mul.88
  101.1 0.4 mul.84
  101.6 1.9 %collective-permute-start = (bf16[2,128,512]{2,1,0:T(8,128)(2,1)S(1)}, bf16[2,128,512]{2,1,0:T(8,128)(2,1)S(1)}, u32[]{:S(2)}, u32[]{:S(2)}) collective-permute-start(bf16[2,128,512]{2,1,0:T(8,128)(2,1)S(1)} %pad_maximum_fusion), channel_id=1, source_target_pairs={{508,0},{0,4},{4,8},{8,12},{12,16},{16,20},{20,24},{24,28},{28,32}... | collective-permute-start | bytes 786440 | tf_op jit(solution)/shard_map/ppermute | solution.py:16
  103.6 0.1 copy.79
  103.7 0.3 reshape.97
  104.0 0.1 concatenate.40
  104.1 0.1 copy.63
  104.2 0.2 copy.65
  104.4 0.1 copy.67
  104.5 0.1 copy.69
  104.6 0.0 copy-start.1
  104.7 0.0 copy-start.5
  104.7 0.2 fusion.38
  104.9 7.6 %collective-permute-done = bf16[2,128,512]{2,1,0:T(8,128)(2,1)S(1)} collective-permute-done((bf16[2,128,512]{2,1,0:T(8,128)(2,1)S(1)}, bf16[2,128,512]{2,1,0:T(8,128)(2,1)S(1)}, u32[]{:S(2)}, u32[]{:S(2)}) %collective-permute-start) | collective-permute-done | bytes 262176 | tf_op jit(solution)/shard_map/ppermute | solution.py:16
  112.5 0.1 copy.75
  112.7 0.0 copy-done.1
  112.7 0.0 copy-done.5
  112.7 0.4 fusion.62
  113.2 0.4 fusion.12
  113.6 0.3 copy.76
  113.9 0.2 reshape.102
  114.0 0.6 fusion.8
  114.7 0.4 copy.72
  115.1 53.6 %all_to_all.24 = bf16[128,8,260]{2,1,0:T(8,128)(2,1)S(1)} all-to-all(bf16[128,8,260]{2,1,0:T(8,128)(2,1)S(1)} %bitcast.42), channel_id=1, replica_groups=mesh['span'=128,'head'=4] {'span'}, dimensions={0} | all-to-all | bytes 1064960 | tf_op jit(solution)/shard_map/all_to_all | solution.py:129
  168.6 0.7 fusion.2
  169.4 1.1 convolution_convert_fusion.1
  170.5 0.0 reduce-scatter.2.cloned.1.call-update
  170.5 14.6 %reduce-scatter.2.cloned.1.call-done = bf16[64,1024]{1,0:T(8,128)(2,1)} async-done(((bf16[256,1024]{1,0:T(8,128)(2,1)}), bf16[64,1024]{1,0:T(8,128)(2,1)}) %reduce-scatter.2.cloned.1.call-update) | async-done | bytes 131088 | tf_op jit(solution)/shard_map/reduce_scatter | solution.py:140
  (25 shorter events, 0.4 us)
Async XLA Ops:
  6.5 162.9 %copy-start = (bf16[256,1024]{1,0:T(8,128)(2,1)S(1)}, bf16[256,1024]{1,0:T(8,128)(2,1)}, u32[]{:S(2)}) copy-start(bf16[256,1024]{1,0:T(8,128)(2,1)} %param.10) | copy-start | bytes 1572868
  6.5 10.0 %copy-start.2 = (s32[2,256]{1,0:T(2,128)S(1)}, s32[2,256]{1,0:T(2,128)}, u32[]{:S(2)}) copy-start(s32[2,256]{1,0:T(2,128)} %param.12) | copy-start | bytes 6148
  8.0 8.9 %copy-start.3 = (bf16[1024,256]{1,0:T(8,128)(2,1)S(1)}, bf16[1024,256]{1,0:T(8,128)(2,1)}, u32[]{:S(2)}) copy-start(bf16[1024,256]{1,0:T(8,128)(2,1)} %param.9) | copy-start | bytes 1572868
  8.0 8.9 %copy-start.4 = (bf16[1024,256]{1,0:T(8,128)(2,1)S(1)}, bf16[1024,256]{1,0:T(8,128)(2,1)}, u32[]{:S(2)}) copy-start(bf16[1024,256]{1,0:T(8,128)(2,1)} %param.8) | copy-start | bytes 1572868
  18.8 79.4 %all-to-all-start = ((bf16[128,8,512]{2,1,0:T(8,128)(2,1)}), bf16[128,8,512]{2,1,0:T(8,128)(2,1)S(1)}, u32[]{:S(2)}, u32[]{:S(2)}) async-start(bf16[128,8,512]{2,1,0:T(8,128)(2,1)} %fusion.5), calls=%async_computation | async-start | bytes 2097152 | tf_op jit(solution)/shard_map/all_to_all | solution.py:81
  40.5 144.7 %reduce-scatter.2.cloned.1.call-start = ((), (), s32[]{:S(2)}) async-start(), calls=%async_computation.3 | async-start | bytes 655360 | tf_op jit(solution)/shard_map/reduce_scatter | solution.py:140
  101.6 10.9 %collective-permute-start = (bf16[2,128,512]{2,1,0:T(8,128)(2,1)S(1)}, bf16[2,128,512]{2,1,0:T(8,128)(2,1)S(1)}, u32[]{:S(2)}, u32[]{:S(2)}) collective-permute-start(bf16[2,128,512]{2,1,0:T(8,128)(2,1)S(1)} %pad_maximum_fusion), channel_id=1, source_target_pairs={{508,0},{0,4},{4,8},{8,12},{12,16},{16,20},{20,24},{24,28},{28,32}... | collective-permute-start | bytes 786440 | tf_op jit(solution)/shard_map/ppermute | solution.py:16
  104.6 8.1 %copy-start.1 = (pred[128,256]{1,0:T(8,128)(4,1)S(1)}, pred[128,256]{1,0:T(8,128)(4,1)}, u32[]{:S(2)}) copy-start(pred[128,256]{1,0:T(8,128)(4,1)} %iota_compare_fusion.12) | copy-start | bytes 98308
  104.7 8.1 %copy-start.5 = (f32[2]{0:T(128)S(1)}, f32[2]{0:T(128)}, u32[]{:S(2)}) copy-start(f32[2]{0:T(128)} %param.11) | copy-start | bytes 28
Sparse Core Ops, SparseCore 0:
  170.7 14.4 reduce-scatter.1

commit v2 on v1

--- a/solution.py
+++ b/solution.py
@@ -70,41 +70,37 @@
     recv_row = source * per_peer + round_ids * capacity + recv_rank
     recv_hot = one_hot_rows(recv_row, buffer_rows)
 
-    full_rows = lax.all_gather(embedding_activity, "head", axis=1, tiled=True)
-    normed = layer_norm(full_rows)
-    joined = jnp.concatenate([common_lookup_projector, content_projector], axis=1)
-    both = jnp.dot(normed, joined, preferred_element_type=jnp.float32).astype(jnp.bfloat16)
-
     outgoing = jnp.einsum(
-        "rtq,tw->qw", send_hot, both, preferred_element_type=jnp.float32
+        "rtq,tf->qf", send_hot, embedding_activity, preferred_element_type=jnp.float32
     ).astype(jnp.bfloat16)
     incoming = lax.all_to_all(outgoing, "span", split_axis=0, concat_axis=0, tiled=True)
     arrived = jnp.einsum(
-        "rsq,qw->rsw", recv_hot, incoming, preferred_element_type=jnp.float32
+        "rsq,qf->rsf", recv_hot, incoming, preferred_element_type=jnp.float32
     ).astype(jnp.bfloat16)
-
-    sorted_shared = arrived[:, :, :head_cols]
-    sorted_values = arrived[:, :, head_cols:]
-    spread = sorted_shared.reshape(n_rounds, rows_here, heads_here, HEAD_DIM).astype(jnp.float32)
+    prior_block = passed_along(arrived[:, rows_here - BLOCK :], "span", 1)
+    with_prior = jnp.concatenate([prior_block, arrived], axis=1)
+    full_rows = lax.all_gather(with_prior, "head", axis=2, tiled=True)
+    normed = layer_norm(full_rows)
+    joined = jnp.concatenate([common_lookup_projector, content_projector], axis=1)
+    both = jnp.einsum(
+        "rsf,fw->rsw", normed, joined, preferred_element_type=jnp.float32
+    ).astype(jnp.bfloat16)
+    span_rows = rows_here + BLOCK
+    sorted_shared = both[:, :, :head_cols]
+    sorted_values = both[:, :, head_cols:]
+    spread = sorted_shared.reshape(n_rounds, span_rows, heads_here, HEAD_DIM).astype(jnp.float32)
     unitlength_address_lines = (
         spread * lax.rsqrt(jnp.sum(spread * spread, axis=-1, keepdims=True) + 1e-06)
     ).astype(jnp.bfloat16)
-    unitlength_address_lines = unitlength_address_lines.reshape(n_rounds, rows_here, head_cols)
-    last_block = jnp.concatenate(
-        [unitlength_address_lines[:, rows_here - BLOCK :], sorted_values[:, rows_here - BLOCK :]],
-        axis=2,
-    )
-    prior_block = passed_along(last_block, "span", 1)
-    keys_cur = unitlength_address_lines.reshape(n_rounds, blocks_here, BLOCK, head_cols)
-    vals_cur = sorted_values.reshape(n_rounds, blocks_here, BLOCK, head_cols)
-    keys_prev = jnp.concatenate([prior_block[:, None, :, :head_cols], keys_cur[:, :-1]], axis=1)
-    vals_prev = jnp.concatenate([prior_block[:, None, :, head_cols:], vals_cur[:, :-1]], axis=1)
-    key_rows = jnp.concatenate([keys_prev, keys_cur], axis=2).reshape(
-        n_rounds, blocks_here, 2 * BLOCK, heads_here, HEAD_DIM
-    )
-    content_projector_lines = jnp.concatenate([vals_prev, vals_cur], axis=2).reshape(
-        n_rounds, blocks_here, 2 * BLOCK, heads_here, HEAD_DIM
-    )
+    unitlength_address_lines = unitlength_address_lines.reshape(n_rounds, span_rows, head_cols)
+    keys_cur = unitlength_address_lines[:, BLOCK:].reshape(n_rounds, blocks_here, BLOCK, head_cols)
+    key_rows = jnp.stack(
+        [unitlength_address_lines[:, b * BLOCK : b * BLOCK + 2 * BLOCK] for b in range(blocks_here)],
+        axis=1,
+    ).reshape(n_rounds, blocks_here, 2 * BLOCK, heads_here, HEAD_DIM)
+    content_projector_lines = jnp.stack(
+        [sorted_values[:, b * BLOCK : b * BLOCK + 2 * BLOCK] for b in range(blocks_here)], axis=1
+    ).reshape(n_rounds, blocks_here, 2 * BLOCK, heads_here, HEAD_DIM)
     queries = keys_cur.reshape(n_rounds, blocks_here, BLOCK, heads_here, HEAD_DIM)
     similarity_energies = jnp.einsum(
         "rbqhd,rbkhd->rbhqk", queries, key_rows, preferred_element_type=jnp.float32

time: 194 us -> 202 us (1.041)
  blocking collectives: 61.2 us -> 123 us
  waiting for transfers between devices: 79.2 us -> 44.3 us
  starting transfers between devices: 23.7 us -> 1.96 us
  other arithmetic: 4.52 us -> 7.37 us
    all_to_all x0 -> x1, blocking collectives: none -> 57.1 us  [shards(): lax.all_to_all(outgoing, 'span', split_axis=0, concat_axis=0, tiled=True)]
    all_to_all x1 -> x0, waiting for transfers between devices: 57 us -> none  [shards(): lax.all_to_all(outgoing, 'span', split_axis=0, concat_axis=0, tiled=True)]
    all_gather x0 -> x1, waiting for transfers between devices: none -> 22.3 us  [shards(): full_rows = lax.all_gather(with_prior, 'head', axis=2, tiled=True)]
    all_to_all x1 -> x0, starting transfers between devices: 21.7 us -> none  [shards(): lax.all_to_all(outgoing, 'span', split_axis=0, concat_axis=0, tiled=True)]
    all_to_all x1, blocking collectives: 53.6 us -> 65.9 us  [shards(): home = lax.all_to_all(back, 'span', split_axis=0, concat_axis=0, tiled=True)]
    all_gather x1 -> x0, blocking collectives: 7.6 us -> none  [shards(): full_rows = lax.all_gather(embedding_activity, 'head', axis=1, tiled=True)]
  transfers between devices with their start and end apart: 3 -> 3, of which waited for: 3 -> 3; matrix products, arithmetic and copies ran while one was open for 1% -> 0% of each run, Pallas kernels for 0% -> 0%
where the time goes in v2:
time: 202 us; the launch traced here: 200 us
  blocking collectives  123 us (61%)
  waiting for transfers between devices  44.3 us (22%)
  between operations  13.7 us (7%)
  other arithmetic  7.37 us (4%)
  matrix products  6.09 us (3%)
  local copies, waits for them, and re-layouts  3.67 us (2%)
    all_to_all x1, blocking collectives, shards(): home = lax.all_to_all(back, 'span', split_axis=0, concat_axis=0, tiled=True)  65.9 us
    all_to_all x1, blocking collectives, shards(): lax.all_to_all(outgoing, 'span', split_axis=0, concat_axis=0, tiled=True)  57.1 us
    all_gather x1, waiting for transfers between devices, shards(): full_rows = lax.all_gather(with_prior, 'head', axis=2, tiled=True)  22.3 us
    reduce_scatter x1, waiting for transfers between devices, shards(): lax.psum_scatter(jnp.dot(combined, final_projector, preferred_element_typ...  14.6 us
    ppermute x1, waiting for transfers between devices, passed_along(): return lax.ppermute(block, axis, route)  7.34 us
  transfers between devices with their start and end apart: 3, of which 3 were waited for; matrix products, arithmetic and copies ran while one was open for 0% of the time, Pallas kernels for 0%

profile of v2, /device:TPU:6, one launch (start us, length us, event | category | flops | bytes accessed | tf_op | source)
XLA Modules:
  0.0 200.1 jit_solution(3799464918146375862)
XLA Ops:
  6.5 0.0 copy-start
  6.5 0.0 all-gather.2.cloned.1.call-start
  6.6 0.7 and_select_fusion.1
  7.3 0.7 and_select_fusion.2
  8.0 0.5 convert_reduce_fusion.2
  8.5 0.8 add_add_fusion
  9.2 0.3 convert_reduce_fusion.1
  9.5 1.3 fusion.19
  10.8 57.1 %all_to_all.24 = bf16[128,8,256]{2,1,0:T(8,128)(2,1)S(1)} all-to-all(bf16[128,8,256]{2,1,0:T(8,128)(2,1)S(1)} %fusion.19), channel_id=1, replica_groups=mesh['span'=128,'head'=4] {'span'}, dimensions={0} | all-to-all | bytes 1048576 | tf_op jit(solution)/shard_map/all_to_all | solution.py:76
  67.9 0.5 fusion.20
  68.4 1.9 collective-permute-start
  70.3 7.3 %collective-permute-done = bf16[2,128,256]{2,1,0:T(8,128)(2,1)S(1)} collective-permute-done((bf16[2,128,256]{2,1,0:T(8,128)(2,1)S(1)}, bf16[2,128,256]{2,1,0:T(8,128)(2,1)S(1)}, u32[]{:S(2)}, u32[]{:S(2)}) %collective-permute-start) | collective-permute-done | bytes 131104 | tf_op jit(solution)/shard_map/ppermute | solution.py:16
  77.6 0.8 pad_maximum_fusion
  78.4 0.0 all-gather.2.cloned.1.call-update
  78.4 0.0 reduce-scatter.2.cloned.1.call-start
  78.5 0.1 iota_compare_fusion.12
  78.6 22.3 %all-gather.2.cloned.1.call-done = bf16[2,384,1024]{2,1,0:T(8,128)(2,1)} async-done(((bf16[2,384,256]{2,1,0:T(8,128)(2,1)}), bf16[2,384,1024]{2,1,0:T(8,128)(2,1)}) %all-gather.2.cloned.1.call-update) | async-done | bytes 1572880 | tf_op jit(solution)/shard_map/all_gather | solution.py:82
  100.9 1.8 convert_reduce_fusion
  102.8 0.0 copy-done.1
  102.8 0.6 fusion.2
  103.4 0.0 copy-done.2
  103.4 0.0 copy-done.3
  103.4 1.0 fusion.12
  104.4 0.1 convert_multiply_fusion.1
  104.5 0.4 mul.71
  104.9 0.9 reduce_sum.86
  105.8 0.1 add_rsqrt_fusion
  105.9 1.0 mul.72
  106.8 0.6 mul.73
  107.5 0.1 fusion.27
  107.6 0.1 stack.22
  107.7 0.1 reshape_reshape.3
  107.8 0.0 copy-start.4
  107.8 0.1 stack.21
  108.0 0.1 copy.41
  108.1 0.1 copy.42
  108.2 0.2 copy-done.4
  108.5 0.4 fusion.53
  108.9 0.4 fusion.21
  109.3 0.3 copy.43
  109.6 0.2 reshape.77
  109.8 0.6 fusion.18
  110.4 0.4 copy.38
  110.8 65.9 %all_to_all.25 = bf16[128,8,260]{2,1,0:T(8,128)(2,1)S(1)} all-to-all(bf16[128,8,260]{2,1,0:T(8,128)(2,1)S(1)} %bitcast.40), channel_id=1, replica_groups=mesh['span'=128,'head'=4] {'span'}, dimensions={0} | all-to-all | bytes 1064960 | tf_op jit(solution)/shard_map/all_to_all | solution.py:125
  176.7 0.7 fusion.6
  177.5 1.1 convolution_convert_fusion
  178.6 0.0 reduce-scatter.2.cloned.1.call-update
  178.6 14.6 %reduce-scatter.2.cloned.1.call-done = bf16[64,1024]{1,0:T(8,128)(2,1)} async-done(((bf16[256,1024]{1,0:T(8,128)(2,1)}), bf16[64,1024]{1,0:T(8,128)(2,1)}) %reduce-scatter.2.cloned.1.call-update) | async-done | bytes 131088 | tf_op jit(solution)/shard_map/reduce_scatter | solution.py:136
  (18 shorter events, 0.3 us)
Async XLA Ops:
  6.5 170.9 %copy-start = (bf16[256,1024]{1,0:T(8,128)(2,1)S(1)}, bf16[256,1024]{1,0:T(8,128)(2,1)}, u32[]{:S(2)}) copy-start(bf16[256,1024]{1,0:T(8,128)(2,1)} %param.10) | copy-start | bytes 1572868
  6.5 94.4 %all-gather.2.cloned.1.call-start = ((), (), s32[]{:S(2)}) async-start(), calls=%async_computation.3 | async-start | bytes 1966080 | tf_op jit(solution)/shard_map/all_gather | solution.py:82
  68.4 9.3 %collective-permute-start = (bf16[2,128,256]{2,1,0:T(8,128)(2,1)S(1)}, bf16[2,128,256]{2,1,0:T(8,128)(2,1)S(1)}, u32[]{:S(2)}, u32[]{:S(2)}) collective-permute-start(bf16[2,128,256]{2,1,0:T(8,128)(2,1)S(1)} %slice.40), channel_id=1, source_target_pairs={{508,0},{0,4},{4,8},{8,12},{12,16},{16,20},{20,24},{24,28},{28,32}... | collective-permute-start | bytes 393224 | tf_op jit(solution)/shard_map/ppermute | solution.py:16
  78.4 114.8 %reduce-scatter.2.cloned.1.call-start = ((), (), s32[]{:S(2)}) async-start(), calls=%async_computation.4 | async-start | bytes 655360 | tf_op jit(solution)/shard_map/reduce_scatter | solution.py:136
  100.9 1.9 copy-start.1
  100.9 2.5 %copy-start.2 = (bf16[1024,256]{1,0:T(8,128)(2,1)S(1)}, bf16[1024,256]{1,0:T(8,128)(2,1)}, u32[]{:S(2)}) copy-start(bf16[1024,256]{1,0:T(8,128)(2,1)} %param.9) | copy-start | bytes 1572868
  100.9 2.5 %copy-start.3 = (bf16[1024,256]{1,0:T(8,128)(2,1)S(1)}, bf16[1024,256]{1,0:T(8,128)(2,1)}, u32[]{:S(2)}) copy-start(bf16[1024,256]{1,0:T(8,128)(2,1)} %param.8) | copy-start | bytes 1572868
  107.8 0.7 copy-start.4
Sparse Core Ops, SparseCore 0:
  78.6 22.2 all-gather.1
  178.7 14.4 reduce-scatter.1

commit v3 on v2

--- a/solution.py
+++ b/solution.py
@@ -1,13 +1,28 @@
 import jax
 import jax.numpy as jnp
 from jax import lax
-from jax.sharding import PartitionSpec as P
+from jax.sharding import Mesh, PartitionSpec as P
 
 HEAD_DIM = 128
 BLOCK = 128
 
 
 epsilon = 1e-05
+
+SPAN_FACTORS = (16, 4, 2)
+SPAN_AXES = ("span_z", "span_x", "span_y")
+
+
+def staged_all_to_all(rows, axes):
+    sizes = tuple(lax.axis_size(axis) for axis in axes)
+    count = 1
+    for size in sizes:
+        count *= size
+    per_peer = rows.shape[0] // count
+    staged = rows.reshape(sizes + (per_peer,) + rows.shape[1:])
+    for place, axis in enumerate(axes):
+        staged = lax.all_to_all(staged, axis, split_axis=place, concat_axis=place, tiled=True)
+    return staged.reshape(rows.shape)
 
 
 def passed_along(block, axis, distance):
@@ -45,7 +60,7 @@
     sorted_place_per_element,
     element_per_sorted_place,
 ):
-    n_dev = lax.axis_size("span")
+    n_dev = lax.axis_size(SPAN_AXES)
     rows_here = embedding_activity.shape[0]
     capacity = 2 * rows_here // n_dev
     n_rounds = sorted_place_per_element.shape[0]
@@ -73,11 +88,11 @@
     outgoing = jnp.einsum(
         "rtq,tf->qf", send_hot, embedding_activity, preferred_element_type=jnp.float32
     ).astype(jnp.bfloat16)
-    incoming = lax.all_to_all(outgoing, "span", split_axis=0, concat_axis=0, tiled=True)
+    incoming = staged_all_to_all(outgoing, SPAN_AXES)
     arrived = jnp.einsum(
         "rsq,qf->rsf", recv_hot, incoming, preferred_element_type=jnp.float32
     ).astype(jnp.bfloat16)
-    prior_block = passed_along(arrived[:, rows_here - BLOCK :], "span", 1)
+    prior_block = passed_along(arrived[:, rows_here - BLOCK :], SPAN_AXES, 1)
     with_prior = jnp.concatenate([prior_block, arrived], axis=1)
     full_rows = lax.all_gather(with_prior, "head", axis=2, tiled=True)
     normed = layer_norm(full_rows)
@@ -122,7 +137,7 @@
     back = jnp.einsum(
         "rsq,rsw->qw", recv_hot, back_payload, preferred_element_type=jnp.float32
     ).astype(jnp.bfloat16)
-    home = lax.all_to_all(back, "span", split_axis=0, concat_axis=0, tiled=True)
+    home = staged_all_to_all(back, SPAN_AXES)
     token_all = jnp.einsum("rtq,qw->rtw", send_hot, home, preferred_element_type=jnp.float32)
     token_rows = token_all[:, :, :head_cols]
     token_totals = (
@@ -142,15 +157,23 @@
 
 
 def solution(mesh):
+    assert mesh.shape["span"] == SPAN_FACTORS[0] * SPAN_FACTORS[1] * SPAN_FACTORS[2]
+    split_mesh = Mesh(
+        mesh.devices.reshape(SPAN_FACTORS + (mesh.shape["head"],)), SPAN_AXES + ("head",)
+    )
     placed = (
-        P("span", "head"),
+        P(SPAN_AXES, "head"),
         P(None, "head"),
         P(None, "head"),
         P("head", None),
         P("head"),
-        P(None, "span"),
-        P(None, "span"),
+        P(None, SPAN_AXES),
+        P(None, SPAN_AXES),
     )
     return jax.shard_map(
-        shards, mesh=mesh, in_specs=placed, out_specs=P(("span", "head"), None), check_vma=False
+        shards,
+        mesh=split_mesh,
+        in_specs=placed,
+        out_specs=P(SPAN_AXES + ("head",), None),
+        check_vma=False,
     )

time: 202 us -> 240 us (1.19)
  blocking collectives: 123 us -> 150 us
  waiting for transfers between devices: 44.3 us -> 55.2 us
    all_to_all x2 -> x6, blocking collectives: 123 us -> 150 us  [staged_all_to_all(): lax.all_to_all(staged, axis, split_axis=place, concat_axis=place, tiled=T...]
    reduce_scatter x1, waiting for transfers between devices: 14.6 us -> 20.7 us  [shards(): lax.psum_scatter(jnp.dot(combined, final_projector, preferred_element_typ...]
    all_gather x1, waiting for transfers between devices: 22.3 us -> 27.1 us  [shards(): full_rows = lax.all_gather(with_prior, 'head', axis=2, tiled=True)]
where the time goes in v3:
time: 240 us; the launch traced here: 238 us
  blocking collectives  150 us (62%)
  waiting for transfers between devices  55.2 us (23%)
  between operations  13.7 us (6%)
  other arithmetic  7.37 us (3%)
  matrix products  6.09 us (3%)
  local copies, waits for them, and re-layouts  4.07 us (2%)
    all_to_all x6, blocking collectives, staged_all_to_all(): lax.all_to_all(staged, axis, split_axis=place, concat_axis=place, tiled=T...  150 us
    all_gather x1, waiting for transfers between devices, shards(): full_rows = lax.all_gather(with_prior, 'head', axis=2, tiled=True)  27.1 us
    reduce_scatter x1, waiting for transfers between devices, shards(): lax.psum_scatter(jnp.dot(combined, final_projector, preferred_element_typ...  20.7 us
    ppermute x1, waiting for transfers between devices, passed_along(): return lax.ppermute(block, axis, route)  7.34 us
  transfers between devices with their start and end apart: 3, of which 3 were waited for; matrix products, arithmetic and copies ran while one was open for 0% of the time, Pallas kernels for 0%

profile of v3, /device:TPU:6, one launch (start us, length us, event | category | flops | bytes accessed | tf_op | source)
XLA Modules:
  0.0 238.3 jit_solution(15070742310931650084)
XLA Ops:
  6.6 0.7 and_select_fusion.1
  7.3 0.7 and_select_fusion.2
  8.0 0.5 convert_reduce_fusion.2
  8.5 0.8 add_add_fusion.1
  9.2 0.3 convert_reduce_fusion.1
  9.5 1.3 fusion.51
  10.8 44.1 %all_to_all.30 = bf16[16,4,2,8,256]{4,3,2,1,0:T(8,128)(2,1)S(1)} all-to-all(bf16[16,4,2,8,256]{4,3,2,1,0:T(8,128)(2,1)S(1)} %bitcast.38), channel_id=1, replica_groups=mesh['span_z'=16,'span_x'=4,'span_y'=2,'head'=4] {'span_z'}, dimensions={0} | all-to-all | bytes 1048576 | tf_op jit(solution)/shard_map/all_to_all | solution.py:24
  54.9 10.6 %all_to_all.31 = bf16[16,4,2,8,256]{4,3,2,0,1:T(8,128)(2,1)S(1)} all-to-all(bf16[16,4,2,8,256]{4,3,2,0,1:T(8,128)(2,1)S(1)} %copy.52), channel_id=1, replica_groups=mesh['span_z'=16,'span_x'=4,'span_y'=2,'head'=4] {'span_x'}, dimensions={1} | all-to-all | bytes 1048576 | tf_op jit(solution)/shard_map/all_to_all | solution.py:24
  65.5 0.1 copy.53
  65.5 13.7 %all_to_all.32 = bf16[16,4,2,8,256]{4,3,1,0,2:T(8,128)(2,1)S(1)} all-to-all(bf16[16,4,2,8,256]{4,3,1,0,2:T(8,128)(2,1)S(1)} %copy.53), channel_id=1, replica_groups=mesh['span_z'=16,'span_x'=4,'span_y'=2,'head'=4] {'span_y'}, dimensions={2} | all-to-all | bytes 1048576 | tf_op jit(solution)/shard_map/all_to_all | solution.py:24
  79.3 0.5 fusion.19
  79.9 1.9 collective-permute-start
  81.8 7.3 %collective-permute-done = bf16[2,128,256]{2,1,0:T(8,128)(2,1)S(1)} collective-permute-done((bf16[2,128,256]{2,1,0:T(8,128)(2,1)S(1)}, bf16[2,128,256]{2,1,0:T(8,128)(2,1)S(1)}, u32[]{:S(2)}, u32[]{:S(2)}) %collective-permute-start) | collective-permute-done | bytes 131104 | tf_op jit(solution)/shard_map/ppermute | solution.py:31
  89.1 0.8 pad_maximum_fusion
  89.9 0.0 reduce-scatter.2.cloned.1.call-start
  90.0 0.1 iota_compare_fusion.12
  90.1 27.1 %all-gather.2.cloned.1.call-done = bf16[2,384,1024]{2,1,0:T(8,128)(2,1)} async-done(((bf16[2,384,256]{2,1,0:T(8,128)(2,1)}), bf16[2,384,1024]{2,1,0:T(8,128)(2,1)}) %all-gather.2.cloned.1.call-update) | async-done | bytes 1572880 | tf_op jit(solution)/shard_map/all_gather | solution.py:97
  117.2 1.8 convert_reduce_fusion
  119.1 0.6 fusion.2
  119.7 1.0 fusion.12
  120.7 0.1 convert_multiply_fusion.1
  120.8 0.4 mul.71
  121.2 0.9 reduce_sum.86
  122.1 0.1 add_rsqrt_fusion
  122.2 1.0 mul.72
  123.1 0.6 mul.73
  123.8 0.1 fusion.26
  123.9 0.1 stack.22
  124.0 0.1 reshape_reshape.3
  124.1 0.1 stack.21
  124.3 0.1 copy.68
  124.4 0.1 copy.69
  124.6 0.2 copy-done.4
  124.8 0.4 fusion.50
  125.2 0.4 fusion.20
  125.6 0.3 copy.70
  125.9 0.2 reshape.89
  126.1 0.6 fusion.18
  126.7 0.4 copy.62
  127.1 52.7 %all_to_all.33 = bf16[16,4,2,8,260]{4,3,2,1,0:T(8,128)(2,1)S(1)} all-to-all(bf16[16,4,2,8,260]{4,3,2,1,0:T(8,128)(2,1)S(1)} %bitcast.37), channel_id=1, replica_groups=mesh['span_z'=16,'span_x'=4,'span_y'=2,'head'=4] {'span_z'}, dimensions={0} | all-to-all | bytes 1064960 | tf_op jit(solution)/shard_map/all_to_all | solution.py:24
  179.8 0.1 copy.63
  179.9 14.9 %all_to_all.34 = bf16[16,4,2,8,260]{4,3,2,0,1:T(8,128)(2,1)S(1)} all-to-all(bf16[16,4,2,8,260]{4,3,2,0,1:T(8,128)(2,1)S(1)} %copy.63), channel_id=1, replica_groups=mesh['span_z'=16,'span_x'=4,'span_y'=2,'head'=4] {'span_x'}, dimensions={1} | all-to-all | bytes 1064960 | tf_op jit(solution)/shard_map/all_to_all | solution.py:24
  194.8 0.1 copy.64
  194.9 13.9 %all_to_all.35 = bf16[16,4,2,8,260]{4,3,1,0,2:T(8,128)(2,1)S(1)} all-to-all(bf16[16,4,2,8,260]{4,3,1,0,2:T(8,128)(2,1)S(1)} %copy.64), channel_id=1, replica_groups=mesh['span_z'=16,'span_x'=4,'span_y'=2,'head'=4] {'span_y'}, dimensions={2} | all-to-all | bytes 1064960 | tf_op jit(solution)/shard_map/all_to_all | solution.py:24
  208.7 0.1 copy.65
  208.9 0.7 fusion.6
  209.7 1.1 convolution_convert_fusion
  210.8 20.7 %reduce-scatter.2.cloned.1.call-done = bf16[64,1024]{1,0:T(8,128)(2,1)} async-done(((bf16[256,1024]{1,0:T(8,128)(2,1)}), bf16[64,1024]{1,0:T(8,128)(2,1)}) %reduce-scatter.2.cloned.1.call-update) | async-done | bytes 131088 | tf_op jit(solution)/shard_map/reduce_scatter | solution.py:151
  (28 shorter events, 0.4 us)
Async XLA Ops:
  6.5 203.1 %copy-start = (bf16[256,1024]{1,0:T(8,128)(2,1)S(1)}, bf16[256,1024]{1,0:T(8,128)(2,1)}, u32[]{:S(2)}) copy-start(bf16[256,1024]{1,0:T(8,128)(2,1)} %param.10) | copy-start | bytes 1572868
  6.5 110.7 %all-gather.2.cloned.1.call-start = ((), (), s32[]{:S(2)}) async-start(), calls=%async_computation.7 | async-start | bytes 1966080 | tf_op jit(solution)/shard_map/all_gather | solution.py:97
  79.9 9.3 %collective-permute-start = (bf16[2,128,256]{2,1,0:T(8,128)(2,1)S(1)}, bf16[2,128,256]{2,1,0:T(8,128)(2,1)S(1)}, u32[]{:S(2)}, u32[]{:S(2)}) collective-permute-start(bf16[2,128,256]{2,1,0:T(8,128)(2,1)S(1)} %slice.40), channel_id=1, source_target_pairs={{508,0},{0,4},{4,8},{8,12},{12,16},{16,20},{20,24},{24,28},{28,32}... | collective-permute-start | bytes 393224 | tf_op jit(solution)/shard_map/ppermute | solution.py:31
  89.9 141.6 %reduce-scatter.2.cloned.1.call-start = ((), (), s32[]{:S(2)}) async-start(), calls=%async_computation.8 | async-start | bytes 655360 | tf_op jit(solution)/shard_map/reduce_scatter | solution.py:151
  117.2 1.9 copy-start.1
  117.2 2.5 %copy-start.2 = (bf16[1024,256]{1,0:T(8,128)(2,1)S(1)}, bf16[1024,256]{1,0:T(8,128)(2,1)}, u32[]{:S(2)}) copy-start(bf16[1024,256]{1,0:T(8,128)(2,1)} %param.9) | copy-start | bytes 1572868
  117.2 2.5 %copy-start.3 = (bf16[1024,256]{1,0:T(8,128)(2,1)S(1)}, bf16[1024,256]{1,0:T(8,128)(2,1)}, u32[]{:S(2)}) copy-start(bf16[1024,256]{1,0:T(8,128)(2,1)} %param.8) | copy-start | bytes 1572868
  124.1 0.7 copy-start.4
Sparse Core Ops, SparseCore 0:
  90.0 27.1 all-gather.1
  210.9 20.5 reduce-scatter.1

commit v4 on v2

--- a/solution.py
+++ b/solution.py
@@ -122,7 +122,10 @@
     back = jnp.einsum(
         "rsq,rsw->qw", recv_hot, back_payload, preferred_element_type=jnp.float32
     ).astype(jnp.bfloat16)
-    home = lax.all_to_all(back, "span", split_axis=0, concat_axis=0, tiled=True)
+    back_width = back.shape[1]
+    home = lax.all_to_all(
+        back.reshape(n_dev, per_peer * back_width), "span", split_axis=0, concat_axis=0, tiled=True
+    ).reshape(buffer_rows, back_width)
     token_all = jnp.einsum("rtq,qw->rtw", send_hot, home, preferred_element_type=jnp.float32)
     token_rows = token_all[:, :, :head_cols]
     token_totals = (

time: 202 us -> 205 us (1.015)
  blocking collectives: 123 us -> 115 us
  other arithmetic: 7.37 us -> 15 us
  local copies, waits for them, and re-layouts: 3.67 us -> 7.36 us
    all_to_all x1, blocking collectives: 65.9 us -> 58.1 us  [shards(): lax.all_to_all(back.reshape(n_dev, per_peer * back_width), 'span', split_...]
    all_to_all x0 -> x2, other arithmetic: none -> 7.63 us  [shards(): lax.all_to_all(back.reshape(n_dev, per_peer * back_width), 'span', split_...]
where the time goes in v4:
time: 205 us; the launch traced here: 203 us
  blocking collectives  115 us (56%)
  waiting for transfers between devices  43.5 us (21%)
  other arithmetic  15 us (7%)
  between operations  13.7 us (7%)
  local copies, waits for them, and re-layouts  7.36 us (4%)
  matrix products  6.08 us (3%)
  starting transfers between devices  2.15 us (1%)
    all_to_all x1, blocking collectives, shards(): lax.all_to_all(back.reshape(n_dev, per_peer * back_width), 'span', split_...  58.1 us
    all_to_all x1, blocking collectives, shards(): lax.all_to_all(outgoing, 'span', split_axis=0, concat_axis=0, tiled=True)  57.1 us
    all_gather x1, waiting for transfers between devices, shards(): full_rows = lax.all_gather(with_prior, 'head', axis=2, tiled=True)  22.1 us
    reduce_scatter x1, waiting for transfers between devices, shards(): lax.psum_scatter(jnp.dot(combined, final_projector, preferred_element_typ...  14 us
    all_to_all x2, other arithmetic, shards(): lax.all_to_all(back.reshape(n_dev, per_peer * back_width), 'span', split_...  7.63 us
    ppermute x1, waiting for transfers between devices, passed_along(): return lax.ppermute(block, axis, route)  7.34 us
  transfers between devices with their start and end apart: 3, of which 3 were waited for; matrix products, arithmetic and copies ran while one was open for 0% of the time, Pallas kernels for 0%

profile of v4, /device:TPU:6, one launch (start us, length us, event | category | flops | bytes accessed | tf_op | source)
XLA Modules:
  0.0 203.1 jit_solution(14824501153442392618)
XLA Ops:
  6.6 0.7 and_select_fusion.1
  7.3 0.7 and_select_fusion.2
  8.0 0.5 convert_reduce_fusion.2
  8.5 0.8 add_add_fusion
  9.2 0.3 convert_reduce_fusion.1
  9.5 1.3 fusion.19
  10.8 57.1 %all_to_all.22 = bf16[128,8,256]{2,1,0:T(8,128)(2,1)S(1)} all-to-all(bf16[128,8,256]{2,1,0:T(8,128)(2,1)S(1)} %fusion.19), channel_id=1, replica_groups=mesh['span'=128,'head'=4] {'span'}, dimensions={0} | all-to-all | bytes 1048576 | tf_op jit(solution)/shard_map/all_to_all | solution.py:76
  67.9 0.5 fusion.20
  68.4 1.9 collective-permute-start
  70.3 7.3 %collective-permute-done = bf16[2,128,256]{2,1,0:T(8,128)(2,1)S(1)} collective-permute-done((bf16[2,128,256]{2,1,0:T(8,128)(2,1)S(1)}, bf16[2,128,256]{2,1,0:T(8,128)(2,1)S(1)}, u32[]{:S(2)}, u32[]{:S(2)}) %collective-permute-start) | collective-permute-done | bytes 131104 | tf_op jit(solution)/shard_map/ppermute | solution.py:16
  77.6 0.8 pad_maximum_fusion
  78.4 0.2 reduce-scatter.2.cloned.1.call-start
  78.7 0.1 iota_compare_fusion.12
  78.8 22.1 %all-gather.2.cloned.1.call-done = bf16[2,384,1024]{2,1,0:T(8,128)(2,1)} async-done(((bf16[2,384,256]{2,1,0:T(8,128)(2,1)}), bf16[2,384,1024]{2,1,0:T(8,128)(2,1)}) %all-gather.2.cloned.1.call-update) | async-done | bytes 1572880 | tf_op jit(solution)/shard_map/all_gather | solution.py:82
  100.9 1.8 convert_reduce_fusion
  102.8 0.0 copy-done.1
  102.8 0.6 fusion.2
  103.4 1.0 fusion.12
  104.4 0.1 convert_multiply_fusion.1
  104.5 0.4 mul.71
  104.9 0.9 reduce_sum.86
  105.8 0.1 add_rsqrt_fusion
  105.9 1.0 mul.72
  106.8 0.6 mul.73
  107.5 0.1 fusion.27
  107.6 0.1 stack.22
  107.7 0.1 reshape_reshape.3
  107.8 0.1 stack.21
  108.0 0.1 copy.43
  108.1 0.1 copy.44
  108.3 0.2 copy-done.4
  108.5 0.4 fusion.53
  108.9 0.4 fusion.21
  109.3 0.3 copy.45
  109.6 0.2 reshape.84
  109.8 0.6 fusion.18
  110.4 0.4 copy.39
  110.8 1.1 all_to_all.19
  111.8 0.5 broadcast.101
  112.3 4.1 %reduce.2 = bf16[128,2080]{1,0:T(8,128)(2,1)S(1)} reduce(bf16[128,1,2080]{2,1,0:T(2,128)(2,1)S(1)} %all_to_all.19, bf16[]{:T(256)} %broadcast.101), dimensions={1}, to_apply=%all_to_all.19.reduce_sub_computation | reduce | bytes 1064962 | tf_op jit(solution)/shard_map/all_to_all | solution.py:126
  116.5 0.6 reshape.86
  117.1 58.1 %all_to_all.23 = bf16[128,2,1040]{2,1,0:T(2,128)(2,1)S(1)} all-to-all(bf16[128,2,1040]{2,1,0:T(2,128)(2,1)S(1)} %reshape.86), channel_id=1, replica_groups=mesh['span'=128,'head'=4] {'span'}, dimensions={0} | all-to-all | bytes 1064960 | tf_op jit(solution)/shard_map/all_to_all | solution.py:126
  175.2 0.6 reshape.87
  175.8 3.5 %reduce.1 = bf16[128,2080]{1,0:T(8,128)(2,1)S(1)} reduce(bf16[128,1,2080]{2,1,0:T(2,128)(2,1)S(1)} %reshape.87, bf16[]{:T(256)} %constant.52), dimensions={1}, to_apply=%all_to_all.18.reduce_sub_computation | reduce | bytes 1064962 | tf_op jit(solution)/shard_map/all_to_all | solution.py:126
  179.3 0.9 reshape.79
  180.3 0.7 fusion.6
  181.1 1.1 convolution_convert_fusion
  182.2 14.0 %reduce-scatter.2.cloned.1.call-done = bf16[64,1024]{1,0:T(8,128)(2,1)} async-done(((bf16[256,1024]{1,0:T(8,128)(2,1)}), bf16[64,1024]{1,0:T(8,128)(2,1)}) %reduce-scatter.2.cloned.1.call-update) | async-done | bytes 131088 | tf_op jit(solution)/shard_map/reduce_scatter | solution.py:139
  (25 shorter events, 0.3 us)
Async XLA Ops:
  6.5 174.5 %copy-start = (bf16[256,1024]{1,0:T(8,128)(2,1)S(1)}, bf16[256,1024]{1,0:T(8,128)(2,1)}, u32[]{:S(2)}) copy-start(bf16[256,1024]{1,0:T(8,128)(2,1)} %param.10) | copy-start | bytes 1572868
  6.5 94.4 %all-gather.2.cloned.1.call-start = ((), (), s32[]{:S(2)}) async-start(), calls=%async_computation.3 | async-start | bytes 1966080 | tf_op jit(solution)/shard_map/all_gather | solution.py:82
  68.4 9.3 %collective-permute-start = (bf16[2,128,256]{2,1,0:T(8,128)(2,1)S(1)}, bf16[2,128,256]{2,1,0:T(8,128)(2,1)S(1)}, u32[]{:S(2)}, u32[]{:S(2)}) collective-permute-start(bf16[2,128,256]{2,1,0:T(8,128)(2,1)S(1)} %slice.40), channel_id=1, source_target_pairs={{508,0},{0,4},{4,8},{8,12},{12,16},{16,20},{20,24},{24,28},{28,32}... | collective-permute-start | bytes 393224 | tf_op jit(solution)/shard_map/ppermute | solution.py:16
  78.4 117.8 %reduce-scatter.2.cloned.1.call-start = ((), (), s32[]{:S(2)}) async-start(), calls=%async_computation.4 | async-start | bytes 655360 | tf_op jit(solution)/shard_map/reduce_scatter | solution.py:139
  100.9 1.9 copy-start.1
  100.9 2.5 %copy-start.2 = (bf16[1024,256]{1,0:T(8,128)(2,1)S(1)}, bf16[1024,256]{1,0:T(8,128)(2,1)}, u32[]{:S(2)}) copy-start(bf16[1024,256]{1,0:T(8,128)(2,1)} %param.9) | copy-start | bytes 1572868
  100.9 2.5 %copy-start.3 = (bf16[1024,256]{1,0:T(8,128)(2,1)S(1)}, bf16[1024,256]{1,0:T(8,128)(2,1)}, u32[]{:S(2)}) copy-start(bf16[1024,256]{1,0:T(8,128)(2,1)} %param.8) | copy-start | bytes 1572868
  107.8 0.7 copy-start.4
Sparse Core Ops, SparseCore 0:
  78.6 22.2 all-gather.1
  182.3 13.8 reduce-scatter.1

commit v5 on v2

--- a/solution.py
+++ b/solution.py
@@ -70,6 +70,7 @@
     recv_row = source * per_peer + round_ids * capacity + recv_rank
     recv_hot = one_hot_rows(recv_row, buffer_rows)
 
+    full_projector = lax.all_gather(final_projector, "head", axis=0, tiled=True)
     outgoing = jnp.einsum(
         "rtq,tf->qf", send_hot, embedding_activity, preferred_element_type=jnp.float32
     ).astype(jnp.bfloat16)
@@ -133,12 +134,16 @@
     token_spread = token_rows.reshape(n_rounds, rows_here, heads_here, HEAD_DIM)
     combined = jnp.sum(round_share[..., None] * token_spread, axis=0).astype(jnp.bfloat16)
     combined = combined.reshape(rows_here, head_cols)
-    return lax.psum_scatter(
-        jnp.dot(combined, final_projector, preferred_element_type=jnp.float32).astype(jnp.bfloat16),
-        "head",
-        scatter_dimension=0,
-        tiled=True,
-    )
+    n_groups = lax.axis_size("head")
+    mine = lax.all_to_all(combined, "head", split_axis=0, concat_axis=1, tiled=True)
+    mine_rows = mine.shape[0]
+    group_parts = jnp.einsum(
+        "tgk,gkn->gtn",
+        mine.reshape(mine_rows, n_groups, head_cols),
+        full_projector.reshape(n_groups, head_cols, full_projector.shape[1]),
+        preferred_element_type=jnp.float32,
+    ).astype(jnp.bfloat16)
+    return jnp.sum(group_parts.astype(jnp.float32), axis=0).astype(jnp.bfloat16)
 
 
 def solution(mesh):

time: 202 us -> 195 us (0.965)
  waiting for transfers between devices: 44.3 us -> 34.2 us
  starting transfers between devices: 1.96 us -> 5.29 us
    reduce_scatter x1 -> x0, waiting for transfers between devices: 14.6 us -> none  [shards(): lax.psum_scatter(jnp.dot(combined, final_projector, preferred_element_typ...]
    all_to_all x0 -> x1, waiting for transfers between devices: none -> 4.57 us  [shards(): lax.all_to_all(combined, 'head', split_axis=0, concat_axis=1, tiled=True)]
    all_to_all x0 -> x1, starting transfers between devices: none -> 3.33 us  [shards(): lax.all_to_all(combined, 'head', split_axis=0, concat_axis=1, tiled=True)]
  transfers between devices with their start and end apart: 3 -> 4, of which waited for: 3 -> 3; matrix products, arithmetic and copies ran while one was open for 0% -> 6% of each run, Pallas kernels for 0% -> 0%
where the time goes in v5:
time: 195 us
  blocking collectives  123 us (63%)
  waiting for transfers between devices  34.2 us (18%)
  between operations  13.7 us (7%)
  other arithmetic  7.32 us (4%)
  matrix products  6.82 us (3%)
  starting transfers between devices  5.29 us (3%)
  local copies, waits for them, and re-layouts  4.35 us (2%)
    all_to_all x1, blocking collectives, shards(): home = lax.all_to_all(back, 'span', split_axis=0, concat_axis=0, tiled=True)  65.9 us
    all_to_all x1, blocking collectives, shards(): lax.all_to_all(outgoing, 'span', split_axis=0, concat_axis=0, tiled=True)  57.1 us
    all_gather x1, waiting for transfers between devices, shards(): full_rows = lax.all_gather(with_prior, 'head', axis=2, tiled=True)  21.6 us
    ppermute x1, waiting for transfers between devices, passed_along(): return lax.ppermute(block, axis, route)  7.34 us
    all_to_all x1, waiting for transfers between devices, shards(): lax.all_to_all(combined, 'head', split_axis=0, concat_axis=1, tiled=True)  4.57 us
  transfers between devices with their start and end apart: 4, of which 3 were waited for; matrix products, arithmetic and copies ran while one was open for 6% of the time, Pallas kernels for 0%

profile of v5, /device:TPU:6, one launch (start us, length us, event | category | flops | bytes accessed | tf_op | source)
XLA Modules:
  0.0 194.7 jit_solution(14253263947843324362)
XLA Ops:
  6.6 0.7 and_select_fusion.1
  7.3 0.7 and_select_fusion.2
  8.0 0.5 convert_reduce_fusion.2
  8.5 0.8 add_add_fusion
  9.2 0.3 convert_reduce_fusion.1
  9.5 0.0 copy-done
  9.5 0.4 fusion.19
  9.8 57.1 %all_to_all.37 = bf16[128,8,256]{2,1,0:T(8,128)(2,1)S(1)} all-to-all(bf16[128,8,256]{2,1,0:T(8,128)(2,1)S(1)} %fusion.19), channel_id=1, replica_groups=mesh['span'=128,'head'=4] {'span'}, dimensions={0} | all-to-all | bytes 1048576 | tf_op jit(solution)/shard_map/all_to_all | solution.py:77
  66.9 0.5 fusion.20
  67.5 1.9 collective-permute-start
  69.4 7.3 %collective-permute-done = bf16[2,128,256]{2,1,0:T(8,128)(2,1)S(1)} collective-permute-done((bf16[2,128,256]{2,1,0:T(8,128)(2,1)S(1)}, bf16[2,128,256]{2,1,0:T(8,128)(2,1)S(1)}, u32[]{:S(2)}, u32[]{:S(2)}) %collective-permute-start) | collective-permute-done | bytes 131104 | tf_op jit(solution)/shard_map/ppermute | solution.py:16
  76.7 0.8 pad_maximum_fusion
  77.5 0.0 all-gather.3.cloned.1.call-update
  77.5 0.0 all-gather.5.cloned.1.call-start
  77.6 0.7 all-gather.5.cloned.1.call-update
  78.3 0.1 iota_compare_fusion.12
  78.4 21.6 %all-gather.3.cloned.1.call-done = bf16[2,384,1024]{2,1,0:T(8,128)(2,1)} async-done(((bf16[2,384,256]{2,1,0:T(8,128)(2,1)}), bf16[2,384,1024]{2,1,0:T(8,128)(2,1)}) %all-gather.3.cloned.1.call-update) | async-done | bytes 1572880 | tf_op jit(solution)/shard_map/all_gather | solution.py:83
  100.0 1.8 convert_reduce_fusion
  101.8 0.1 copy-done.1
  101.9 0.6 fusion.2
  102.5 1.0 fusion.12
  103.5 0.1 convert_multiply_fusion.1
  103.6 0.4 mul.71
  104.0 0.9 reduce_sum.98
  104.9 0.1 add_rsqrt_fusion
  104.9 1.0 mul.72
  105.9 0.6 mul.73
  106.5 0.1 fusion.28
  106.7 0.1 stack.22
  106.8 0.0 copy-start.4
  106.8 0.1 reshape_reshape.3
  106.9 0.1 stack.21
  107.1 0.1 copy.43
  107.2 0.1 copy.44
  107.3 0.1 copy-done.4
  107.4 0.4 fusion.54
  107.9 0.4 fusion.22
  108.3 0.3 copy.45
  108.6 0.2 reshape.88
  108.7 0.6 fusion.18
  109.4 0.4 copy.39
  109.7 65.9 %all_to_all.38 = bf16[128,8,260]{2,1,0:T(8,128)(2,1)S(1)} all-to-all(bf16[128,8,260]{2,1,0:T(8,128)(2,1)S(1)} %bitcast.44), channel_id=1, replica_groups=mesh['span'=128,'head'=4] {'span'}, dimensions={0} | all-to-all | bytes 1064960 | tf_op jit(solution)/shard_map/all_to_all | solution.py:126
  175.7 0.7 fusion.6
  176.5 0.8 copy.41
  177.2 3.3 %all-to-all-start.2 = ((bf16[4,64,256]{2,1,0:T(8,128)(2,1)}), bf16[4,64,256]{2,1,0:T(8,128)(2,1)S(1)}, u32[]{:S(2)}, u32[]{:S(2)}) async-start(bf16[4,64,256]{2,1,0:T(8,128)(2,1)} %bitcast.15), calls=%async_computation.2 | async-start | bytes 262144 | tf_op jit(solution)/shard_map/all_to_all | solution.py:138
  180.5 0.0 all-gather.5.cloned.1.call-done
  180.6 4.6 %all-to-all-done.2 = bf16[4,64,256]{2,1,0:T(8,128)(2,1)S(1)} async-done(((bf16[4,64,256]{2,1,0:T(8,128)(2,1)}), bf16[4,64,256]{2,1,0:T(8,128)(2,1)S(1)}, u32[]{:S(2)}, u32[]{:S(2)}) %all-to-all-start.2) | async-done | bytes 131104 | tf_op jit(solution)/shard_map/all_to_all | solution.py:138
  185.1 2.8 %fusion.21 = bf16[64,1024]{1,0:T(8,128)(2,1)} fusion(bf16[4,256,1024]{2,1,0:T(8,128)(2,1)} %bitcast.45, bf16[4,64,256]{2,1,0:T(8,128)(2,1)S(1)} %all-to-all-done.2), kind=kOutput, calls=%fused_computation.27 | convolution fusion | flops 134676480 | bytes 2359296 | tf_op jit(solution)/shard_map/tgk,gkn->gtn/dot_general | solution.py:140
  (21 shorter events, 0.3 us)
Async XLA Ops:
  6.5 2.9 %copy-start = (bf16[256,256]{1,0:T(8,128)(2,1)S(1)}, bf16[256,256]{1,0:T(8,128)(2,1)}, u32[]{:S(2)}) copy-start(bf16[256,256]{1,0:T(8,128)(2,1)} %param.7) | copy-start | bytes 393220
  6.5 93.5 %all-gather.3.cloned.1.call-start = ((), (), s32[]{:S(2)}) async-start(), calls=%async_computation.3 | async-start | bytes 1966080 | tf_op jit(solution)/shard_map/all_gather | solution.py:83
  67.5 9.3 %collective-permute-start = (bf16[2,128,256]{2,1,0:T(8,128)(2,1)S(1)}, bf16[2,128,256]{2,1,0:T(8,128)(2,1)S(1)}, u32[]{:S(2)}, u32[]{:S(2)}) collective-permute-start(bf16[2,128,256]{2,1,0:T(8,128)(2,1)S(1)} %slice.40), channel_id=1, source_target_pairs={{508,0},{0,4},{4,8},{8,12},{12,16},{16,20},{20,24},{24,28},{28,32}... | collective-permute-start | bytes 393224 | tf_op jit(solution)/shard_map/ppermute | solution.py:16
  76.7 25.7 %copy-start.3 = (bf16[1024,256]{1,0:T(8,128)(2,1)S(1)}, bf16[1024,256]{1,0:T(8,128)(2,1)}, u32[]{:S(2)}) copy-start(bf16[1024,256]{1,0:T(8,128)(2,1)} %param.8) | copy-start | bytes 1572868
  77.5 25.0 %copy-start.2 = (bf16[1024,256]{1,0:T(8,128)(2,1)S(1)}, bf16[1024,256]{1,0:T(8,128)(2,1)}, u32[]{:S(2)}) copy-start(bf16[1024,256]{1,0:T(8,128)(2,1)} %param.9) | copy-start | bytes 1572868
  77.5 103.0 %all-gather.5.cloned.1.call-start = ((), (), s32[]{:S(2)}) async-start(), calls=%async_computation.4 | async-start | bytes 2621440 | tf_op jit(solution)/shard_map/all_gather | solution.py:73
  100.0 1.9 copy-start.1
  106.8 0.7 copy-start.4
  177.2 7.9 %all-to-all-start.2 = ((bf16[4,64,256]{2,1,0:T(8,128)(2,1)}), bf16[4,64,256]{2,1,0:T(8,128)(2,1)S(1)}, u32[]{:S(2)}, u32[]{:S(2)}) async-start(bf16[4,64,256]{2,1,0:T(8,128)(2,1)} %bitcast.15), calls=%async_computation.2 | async-start | bytes 262144 | tf_op jit(solution)/shard_map/all_to_all | solution.py:138
Sparse Core Ops, SparseCore 0:
  77.6 22.2 all-gather.2
  102.1 41.3 all-gather.4

commit v6 on v2

--- a/solution.py
+++ b/solution.py
@@ -79,7 +79,12 @@
     ).astype(jnp.bfloat16)
     prior_block = passed_along(arrived[:, rows_here - BLOCK :], "span", 1)
     with_prior = jnp.concatenate([prior_block, arrived], axis=1)
-    full_rows = lax.all_gather(with_prior, "head", axis=2, tiled=True)
+    n_groups = lax.axis_size("head")
+    copies = jnp.broadcast_to(with_prior[None], (n_groups,) + with_prior.shape)
+    gathered = lax.all_to_all(copies, "head", split_axis=0, concat_axis=0, tiled=True)
+    full_rows = jnp.moveaxis(gathered, 0, 2).reshape(
+        with_prior.shape[:2] + (n_groups * with_prior.shape[2],)
+    )
     normed = layer_norm(full_rows)
     joined = jnp.concatenate([common_lookup_projector, content_projector], axis=1)
     both = jnp.einsum(
@@ -133,12 +138,17 @@
     token_spread = token_rows.reshape(n_rounds, rows_here, heads_here, HEAD_DIM)
     combined = jnp.sum(round_share[..., None] * token_spread, axis=0).astype(jnp.bfloat16)
     combined = combined.reshape(rows_here, head_cols)
-    return lax.psum_scatter(
-        jnp.dot(combined, final_projector, preferred_element_type=jnp.float32).astype(jnp.bfloat16),
+    group_part = jnp.dot(
+        combined, final_projector, preferred_element_type=jnp.float32
+    ).astype(jnp.bfloat16)
+    group_parts = lax.all_to_all(
+        group_part.reshape(n_groups, rows_here // n_groups, group_part.shape[1]),
         "head",
-        scatter_dimension=0,
+        split_axis=0,
+        concat_axis=0,
         tiled=True,
     )
+    return jnp.sum(group_parts.astype(jnp.float32), axis=0).astype(jnp.bfloat16)
 
 
 def solution(mesh):

time: 202 us -> 176 us (0.87)
  waiting for transfers between devices: 44.3 us -> 27.4 us
  between operations: 13.7 us -> 0.34 us
  starting transfers between devices: 1.96 us -> 6.25 us
  local copies, waits for them, and re-layouts: 3.67 us -> 7.54 us
    all_gather x1 -> x0, waiting for transfers between devices: 22.3 us -> none  [shards(): full_rows = lax.all_gather(with_prior, 'head', axis=2, tiled=True)]
    all_to_all x0 -> x1, waiting for transfers between devices: none -> 20 us  [shards(): lax.all_to_all(copies, 'head', split_axis=0, concat_axis=0, tiled=True)]
    reduce_scatter x1 -> x0, waiting for transfers between devices: 14.6 us -> none  [shards(): lax.psum_scatter(jnp.dot(combined, final_projector, preferred_element_typ...]
    all_to_all x1, blocking collectives: 65.9 us -> 54.2 us  [shards(): home = lax.all_to_all(back, 'span', split_axis=0, concat_axis=0, tiled=True)]
    all_to_all x0 -> x1, blocking collectives: none -> 11.2 us  [shards(): lax.all_to_all(group_part.reshape(n_groups, rows_here // n_groups, group_...]
    all_to_all x0 -> x1, starting transfers between devices: none -> 4.33 us  [shards(): lax.all_to_all(copies, 'head', split_axis=0, concat_axis=0, tiled=True)]
  transfers between devices with their start and end apart: 3 -> 2, of which waited for: 3 -> 2; matrix products, arithmetic and copies ran while one was open for 0% -> 0% of each run, Pallas kernels for 0% -> 0%
where the time goes in v6:
time: 176 us; the launch traced here: 175 us
  blocking collectives  123 us (70%)
  waiting for transfers between devices  27.4 us (16%)
  local copies, waits for them, and re-layouts  7.54 us (4%)
  starting transfers between devices  6.25 us (4%)
  other arithmetic  6.08 us (3%)
  matrix products  5.25 us (3%)
    all_to_all x1, blocking collectives, shards(): lax.all_to_all(outgoing, 'span', split_axis=0, concat_axis=0, tiled=True)  57.1 us
    all_to_all x1, blocking collectives, shards(): home = lax.all_to_all(back, 'span', split_axis=0, concat_axis=0, tiled=True)  54.2 us
    all_to_all x1, waiting for transfers between devices, shards(): lax.all_to_all(copies, 'head', split_axis=0, concat_axis=0, tiled=True)  20 us
    all_to_all x1, blocking collectives, shards(): lax.all_to_all(group_part.reshape(n_groups, rows_here // n_groups, group_...  11.2 us
    ppermute x1, waiting for transfers between devices, passed_along(): return lax.ppermute(block, axis, route)  7.34 us
    all_to_all x1, starting transfers between devices, shards(): lax.all_to_all(copies, 'head', split_axis=0, concat_axis=0, tiled=True)  4.33 us
  transfers between devices with their start and end apart: 2, of which 2 were waited for; matrix products, arithmetic and copies ran while one was open for 0% of the time, Pallas kernels for 0%

profile of v6, /device:TPU:6, one launch (start us, length us, event | category | flops | bytes accessed | tf_op | source)
XLA Modules:
  0.0 175.4 jit_solution(14094101873363880144)
XLA Ops:
  0.0 0.7 and_select_fusion.1
  0.8 0.7 and_select_fusion.2
  1.5 0.5 convert_reduce_fusion.1
  1.9 0.8 add_add_fusion
  2.7 0.3 convert_reduce_fusion
  3.0 1.3 fusion.12
  4.2 57.1 %all_to_all.34 = bf16[128,8,256]{2,1,0:T(8,128)(2,1)S(1)} all-to-all(bf16[128,8,256]{2,1,0:T(8,128)(2,1)S(1)} %fusion.12), channel_id=1, replica_groups=mesh['span'=128,'head'=4] {'span'}, dimensions={0} | all-to-all | bytes 1048576 | tf_op jit(solution)/shard_map/all_to_all | solution.py:76
  61.3 0.5 fusion.13
  61.8 1.9 %collective-permute-start = (bf16[2,128,256]{2,1,0:T(8,128)(2,1)S(1)}, bf16[2,128,256]{2,1,0:T(8,128)(2,1)S(1)}, u32[]{:S(2)}, u32[]{:S(2)}) collective-permute-start(bf16[2,128,256]{2,1,0:T(8,128)(2,1)S(1)} %slice.40), channel_id=1, source_target_pairs={{508,0},{0,4},{4,8},{8,12},{12,16},{16,20},{20,24},{24,28},{28,32}... | collective-permute-start | bytes 393224 | tf_op jit(solution)/shard_map/ppermute | solution.py:16
  63.8 7.3 %collective-permute-done = bf16[2,128,256]{2,1,0:T(8,128)(2,1)S(1)} collective-permute-done((bf16[2,128,256]{2,1,0:T(8,128)(2,1)S(1)}, bf16[2,128,256]{2,1,0:T(8,128)(2,1)S(1)}, u32[]{:S(2)}, u32[]{:S(2)}) %collective-permute-start) | collective-permute-done | bytes 131104 | tf_op jit(solution)/shard_map/ppermute | solution.py:16
  71.1 1.2 broadcast_in_dim.8
  72.4 4.3 %all-to-all-start.1 = ((bf16[4,2,384,256]{3,2,1,0:T(8,128)(2,1)}), bf16[4,2,384,256]{3,2,1,0:T(8,128)(2,1)}, u32[]{:S(2)}, u32[]{:S(2)}) async-start(bf16[4,2,384,256]{3,2,1,0:T(8,128)(2,1)} %broadcast_in_dim.8), calls=%async_computation.1 | async-start | bytes 3145728 | tf_op jit(solution)/shard_map/all_to_all | solution.py:84
  76.7 0.1 iota_compare_fusion.12
  76.8 20.0 %all-to-all-done.1 = bf16[4,2,384,256]{3,2,1,0:T(8,128)(2,1)} async-done(((bf16[4,2,384,256]{3,2,1,0:T(8,128)(2,1)}), bf16[4,2,384,256]{3,2,1,0:T(8,128)(2,1)}, u32[]{:S(2)}, u32[]{:S(2)}) %all-to-all-start.1) | async-done | bytes 1572896 | tf_op jit(solution)/shard_map/all_to_all | solution.py:84
  96.9 1.9 %copy.42 = bf16[4,2,384,256]{2,3,0,1:T(8,128)(2,1)S(1)} copy(bf16[4,2,384,256]{3,2,1,0:T(8,128)(2,1)} %all-to-all-done.1) | data formatting | bytes 3145728 | tf_op jit(solution)/shard_map/all_to_all | solution.py:84
  98.8 0.3 bitcast_reduce_fusion
  99.0 0.4 fusion.3
  99.5 0.0 copy-start.1
  99.5 0.0 copy-start.2
  99.5 0.4 fusion.1
  99.9 0.6 copy-done.1
  100.5 0.2 copy-done.2
  100.7 1.0 convolution_convert_fusion
  101.7 0.1 convert_multiply_fusion.1
  101.8 0.4 mul.72
  102.2 0.9 reduce_sum.98
  103.1 0.1 add_rsqrt_fusion
  103.1 1.0 mul.73
  104.1 0.6 mul.74
  104.7 0.1 fusion.20
  104.9 0.1 stack.22
  105.0 0.1 reshape_reshape.3
  105.1 0.0 copy-start.3
  105.1 0.1 stack.21
  105.2 0.1 copy.55
  105.4 0.1 copy.56
  105.5 0.2 copy-done.3
  105.7 0.4 fusion.46
  106.2 0.4 fusion.14
  106.6 0.3 copy.57
  106.9 0.2 reshape.86
  107.0 0.6 fusion.11
  107.7 0.4 copy.51
  108.1 54.2 %all_to_all.35 = bf16[128,8,260]{2,1,0:T(8,128)(2,1)S(1)} all-to-all(bf16[128,8,260]{2,1,0:T(8,128)(2,1)S(1)} %bitcast.56), channel_id=1, replica_groups=mesh['span'=128,'head'=4] {'span'}, dimensions={0} | all-to-all | bytes 1064960 | tf_op jit(solution)/shard_map/all_to_all | solution.py:130
  162.3 0.7 fusion.6
  163.1 0.3 convolution_convert_fusion.1
  163.4 11.2 %all_to_all.36 = bf16[4,64,1024]{2,1,0:T(8,128)(2,1)S(1)} all-to-all(bf16[4,64,1024]{2,1,0:T(8,128)(2,1)S(1)} %bitcast.57), channel_id=1, replica_groups=mesh['span'=128,'head'=4] {'head'}, dimensions={0} | all-to-all | bytes 1048576 | tf_op jit(solution)/shard_map/all_to_all | solution.py:144
  174.6 0.7 reduce_sum.102
  (17 shorter events, 0.3 us)
Async XLA Ops:
  0.0 163.1 %copy-start = (bf16[256,1024]{1,0:T(8,128)(2,1)S(1)}, bf16[256,1024]{1,0:T(8,128)(2,1)}, u32[]{:S(2)}) copy-start(bf16[256,1024]{1,0:T(8,128)(2,1)} %param.10) | copy-start | bytes 1572868
  61.8 9.3 %collective-permute-start = (bf16[2,128,256]{2,1,0:T(8,128)(2,1)S(1)}, bf16[2,128,256]{2,1,0:T(8,128)(2,1)S(1)}, u32[]{:S(2)}, u32[]{:S(2)}) collective-permute-start(bf16[2,128,256]{2,1,0:T(8,128)(2,1)S(1)} %slice.40), channel_id=1, source_target_pairs={{508,0},{0,4},{4,8},{8,12},{12,16},{16,20},{20,24},{24,28},{28,32}... | collective-permute-start | bytes 393224 | tf_op jit(solution)/shard_map/ppermute | solution.py:16
  72.4 24.5 %all-to-all-start.1 = ((bf16[4,2,384,256]{3,2,1,0:T(8,128)(2,1)}), bf16[4,2,384,256]{3,2,1,0:T(8,128)(2,1)}, u32[]{:S(2)}, u32[]{:S(2)}) async-start(bf16[4,2,384,256]{3,2,1,0:T(8,128)(2,1)} %broadcast_in_dim.8), calls=%async_computation.1 | async-start | bytes 3145728 | tf_op jit(solution)/shard_map/all_to_all | solution.py:84
  99.5 1.0 copy-start.1
  99.5 1.2 copy-start.2
  105.1 0.7 copy-start.3

commit v7 on v6

--- a/solution.py
+++ b/solution.py
@@ -78,26 +78,34 @@
         "rsq,qf->rsf", recv_hot, incoming, preferred_element_type=jnp.float32
     ).astype(jnp.bfloat16)
     prior_block = passed_along(arrived[:, rows_here - BLOCK :], "span", 1)
-    with_prior = jnp.concatenate([prior_block, arrived], axis=1)
     n_groups = lax.axis_size("head")
-    copies = jnp.broadcast_to(with_prior[None], (n_groups,) + with_prior.shape)
-    gathered = lax.all_to_all(copies, "head", split_axis=0, concat_axis=0, tiled=True)
-    full_rows = jnp.moveaxis(gathered, 0, 2).reshape(
-        with_prior.shape[:2] + (n_groups * with_prior.shape[2],)
-    )
-    normed = layer_norm(full_rows)
     joined = jnp.concatenate([common_lookup_projector, content_projector], axis=1)
-    both = jnp.einsum(
-        "rsf,fw->rsw", normed, joined, preferred_element_type=jnp.float32
-    ).astype(jnp.bfloat16)
-    span_rows = rows_here + BLOCK
-    sorted_shared = both[:, :, :head_cols]
-    sorted_values = both[:, :, head_cols:]
-    spread = sorted_shared.reshape(n_rounds, span_rows, heads_here, HEAD_DIM).astype(jnp.float32)
-    unitlength_address_lines = (
-        spread * lax.rsqrt(jnp.sum(spread * spread, axis=-1, keepdims=True) + 1e-06)
-    ).astype(jnp.bfloat16)
-    unitlength_address_lines = unitlength_address_lines.reshape(n_rounds, span_rows, head_cols)
+
+    def gather_features(rows):
+        copies = jnp.broadcast_to(rows[None], (n_groups,) + rows.shape)
+        return lax.all_to_all(copies, "head", split_axis=0, concat_axis=0, tiled=True)
+
+    def keys_and_values(gathered):
+        rows_shape = gathered.shape[1:3]
+        full_rows = jnp.moveaxis(gathered, 0, 2).reshape(rows_shape + (-1,))
+        normed = layer_norm(full_rows)
+        both = jnp.einsum(
+            "rsf,fw->rsw", normed, joined, preferred_element_type=jnp.float32
+        ).astype(jnp.bfloat16)
+        spread = both[:, :, :head_cols].reshape(rows_shape + (heads_here, HEAD_DIM))
+        spread = spread.astype(jnp.float32)
+        unit = (
+            spread * lax.rsqrt(jnp.sum(spread * spread, axis=-1, keepdims=True) + 1e-06)
+        ).astype(jnp.bfloat16)
+        return unit.reshape(rows_shape + (head_cols,)), both[:, :, head_cols:]
+
+    gathered_here = gather_features(arrived)
+    prior_block, gathered_here = lax.optimization_barrier((prior_block, gathered_here))
+    gathered_prior = gather_features(prior_block)
+    keys_here, values_here = keys_and_values(gathered_here)
+    keys_prior, values_prior = keys_and_values(gathered_prior)
+    unitlength_address_lines = jnp.concatenate([keys_prior, keys_here], axis=1)
+    sorted_values = jnp.concatenate([values_prior, values_here], axis=1)
     keys_cur = unitlength_address_lines[:, BLOCK:].reshape(n_rounds, blocks_here, BLOCK, head_cols)
     key_rows = jnp.stack(
         [unitlength_address_lines[:, b * BLOCK : b * BLOCK + 2 * BLOCK] for b in range(blocks_here)],

time: 176 us -> 175 us (level)
  waiting for transfers between devices: 27.4 us -> 18.4 us
  starting transfers between devices: 6.25 us -> 9.08 us
  local copies, waits for them, and re-layouts: 7.54 us -> 9.82 us
    all_to_all x1 -> x2, waiting for transfers between devices: 20 us -> 5.99 us  [gather_features(): lax.all_to_all(copies, 'head', split_axis=0, concat_axis=0, tiled=True)]
    ppermute x1, waiting for transfers between devices: 7.34 us -> 12.5 us  [passed_along(): return lax.ppermute(block, axis, route)]
    all_to_all x1 -> x2, starting transfers between devices: 4.33 us -> 7.16 us  [gather_features(): lax.all_to_all(copies, 'head', split_axis=0, concat_axis=0, tiled=True)]
  transfers between devices with their start and end apart: 2 -> 3, of which waited for: 2 -> 2; matrix products, arithmetic and copies ran while one was open for 0% -> 2% of each run, Pallas kernels for 0% -> 0%
where the time goes in v7:
time: 175 us; the launch traced here: 174 us
  blocking collectives  124 us (71%)
  waiting for transfers between devices  18.4 us (11%)
  local copies, waits for them, and re-layouts  9.82 us (6%)
  starting transfers between devices  9.08 us (5%)
  other arithmetic  7.15 us (4%)
  matrix products  5.53 us (3%)
    all_to_all x1, blocking collectives, shards(): lax.all_to_all(outgoing, 'span', split_axis=0, concat_axis=0, tiled=True)  57.1 us
    all_to_all x1, blocking collectives, shards(): home = lax.all_to_all(back, 'span', split_axis=0, concat_axis=0, tiled=True)  55.2 us
    ppermute x1, waiting for transfers between devices, passed_along(): return lax.ppermute(block, axis, route)  12.5 us
    all_to_all x1, blocking collectives, shards(): lax.all_to_all(group_part.reshape(n_groups, rows_here // n_groups, group_...  11.2 us
    all_to_all x2, starting transfers between devices, gather_features(): lax.all_to_all(copies, 'head', split_axis=0, concat_axis=0, tiled=True)  7.16 us
    all_to_all x2, waiting for transfers between devices, gather_features(): lax.all_to_all(copies, 'head', split_axis=0, concat_axis=0, tiled=True)  5.99 us
  transfers between devices with their start and end apart: 3, of which 2 were waited for; matrix products, arithmetic and copies ran while one was open for 2% of the time, Pallas kernels for 0%

profile of v7, /device:TPU:6, one launch (start us, length us, event | category | flops | bytes accessed | tf_op | source)
XLA Modules:
  0.0 174.0 jit_solution(6725835185179044618)
XLA Ops:
  0.0 0.7 and_select_fusion.2
  0.8 0.7 and_select_fusion.1
  1.5 0.5 convert_reduce_fusion.1
  1.9 0.8 add_add_fusion
  2.7 0.3 convert_reduce_fusion
  3.0 1.3 fusion.12
  4.2 57.1 %all_to_all.39 = bf16[128,8,256]{2,1,0:T(8,128)(2,1)S(1)} all-to-all(bf16[128,8,256]{2,1,0:T(8,128)(2,1)S(1)} %fusion.12), channel_id=1, replica_groups=mesh['span'=128,'head'=4] {'span'}, dimensions={0} | all-to-all | bytes 1048576 | tf_op jit(solution)/shard_map/all_to_all | solution.py:76
  61.3 0.5 fusion.13
  61.8 1.1 broadcast_in_dim.10
  62.9 3.5 %all-to-all-start.1 = ((bf16[4,2,256,256]{3,2,1,0:T(8,128)(2,1)}), bf16[4,2,256,256]{3,2,1,0:T(8,128)(2,1)S(1)}, u32[]{:S(2)}, u32[]{:S(2)}) async-start(bf16[4,2,256,256]{3,2,1,0:T(8,128)(2,1)} %broadcast_in_dim.10), calls=%async_computation.1 | async-start | bytes 2097152 | tf_op jit(solution)/shard_map/all_to_all | solution.py:86
  66.4 1.9 %collective-permute-start = (bf16[2,128,256]{2,1,0:T(8,128)(2,1)S(1)}, bf16[2,128,256]{2,1,0:T(8,128)(2,1)S(1)}, u32[]{:S(2)}, u32[]{:S(2)}) collective-permute-start(bf16[2,128,256]{2,1,0:T(8,128)(2,1)S(1)} %slice.40), channel_id=1, source_target_pairs={{508,0},{0,4},{4,8},{8,12},{12,16},{16,20},{20,24},{24,28},{28,32}... | collective-permute-start | bytes 393224 | tf_op jit(solution)/shard_map/ppermute | solution.py:16
  68.4 0.7 iota_compare_fusion.12
  69.1 12.5 %collective-permute-done = bf16[2,128,256]{2,1,0:T(8,128)(2,1)S(1)} collective-permute-done((bf16[2,128,256]{2,1,0:T(8,128)(2,1)S(1)}, bf16[2,128,256]{2,1,0:T(8,128)(2,1)S(1)}, u32[]{:S(2)}, u32[]{:S(2)}) %collective-permute-start) | collective-permute-done | bytes 131104 | tf_op jit(solution)/shard_map/ppermute | solution.py:16
  81.5 0.5 copy.54
  82.0 0.2 bitcast_reduce_fusion
  82.2 0.3 fusion.3
  82.6 0.3 fusion.1
  82.8 0.7 copy-done.4
  83.6 0.2 copy-done.6
  83.7 0.7 convolution_convert_fusion.2
  84.6 0.3 reshape.141
  84.9 1.0 reshape.140
  85.9 0.8 broadcast_in_dim.11
  86.8 3.6 %all-to-all-start.2 = ((bf16[4,2,128,256]{3,2,1,0:T(8,128)(2,1)}), bf16[4,2,128,256]{3,2,1,0:T(8,128)(2,1)S(1)}, u32[]{:S(2)}, u32[]{:S(2)}) async-start(bf16[4,2,128,256]{3,2,1,0:T(8,128)(2,1)} %broadcast_in_dim.11), calls=%async_computation.2 | async-start | bytes 1048576 | tf_op jit(solution)/shard_map/all_to_all | solution.py:86
  90.4 0.3 mul.121
  90.7 0.6 reduce_sum.127
  91.6 0.6 mul.129
  92.2 0.4 mul.130
  92.8 0.2 fusion.31
  93.1 6.0 %all-to-all-done.2 = bf16[4,2,128,256]{3,2,1,0:T(8,128)(2,1)S(1)} async-done(((bf16[4,2,128,256]{3,2,1,0:T(8,128)(2,1)}), bf16[4,2,128,256]{3,2,1,0:T(8,128)(2,1)S(1)}, u32[]{:S(2)}, u32[]{:S(2)}) %all-to-all-start.2) | async-done | bytes 524320 | tf_op jit(solution)/shard_map/all_to_all | solution.py:86
  99.0 0.3 copy.52
  99.8 0.5 copy-done.5
  100.5 0.5 convolution_convert_fusion.3
  101.2 0.3 reduce_sum.128
  101.6 0.3 mul.126
  101.9 0.2 mul.127
  102.3 0.7 slice-done
  103.3 0.5 fusion.52
  103.8 0.4 fusion.14
  104.2 0.3 copy.72
  104.5 0.2 reshape.146
  104.7 0.6 fusion.11
  105.3 0.4 copy.65
  105.7 55.2 %all_to_all.40 = bf16[128,8,260]{2,1,0:T(8,128)(2,1)S(1)} all-to-all(bf16[128,8,260]{2,1,0:T(8,128)(2,1)S(1)} %bitcast.74), channel_id=1, replica_groups=mesh['span'=128,'head'=4] {'span'}, dimensions={0} | all-to-all | bytes 1064960 | tf_op jit(solution)/shard_map/all_to_all | solution.py:138
  160.9 0.7 fusion.6
  161.7 0.3 convolution_convert_fusion
  162.0 11.2 %all_to_all.41 = bf16[4,64,1024]{2,1,0:T(8,128)(2,1)S(1)} all-to-all(bf16[4,64,1024]{2,1,0:T(8,128)(2,1)S(1)} %bitcast.75), channel_id=1, replica_groups=mesh['span'=128,'head'=4] {'head'}, dimensions={0} | all-to-all | bytes 1048576 | tf_op jit(solution)/shard_map/all_to_all | solution.py:152
  173.2 0.7 reduce_sum.132
  (48 shorter events, 1.9 us)
Async XLA Ops:
  0.0 161.7 %copy-start = (bf16[256,1024]{1,0:T(8,128)(2,1)S(1)}, bf16[256,1024]{1,0:T(8,128)(2,1)}, u32[]{:S(2)}) copy-start(bf16[256,1024]{1,0:T(8,128)(2,1)} %param.10) | copy-start | bytes 1572868
  62.9 18.6 %all-to-all-start.1 = ((bf16[4,2,256,256]{3,2,1,0:T(8,128)(2,1)}), bf16[4,2,256,256]{3,2,1,0:T(8,128)(2,1)S(1)}, u32[]{:S(2)}, u32[]{:S(2)}) async-start(bf16[4,2,256,256]{3,2,1,0:T(8,128)(2,1)} %broadcast_in_dim.10), calls=%async_computation.1 | async-start | bytes 2097152 | tf_op jit(solution)/shard_map/all_to_all | solution.py:86
  66.4 15.1 %collective-permute-start = (bf16[2,128,256]{2,1,0:T(8,128)(2,1)S(1)}, bf16[2,128,256]{2,1,0:T(8,128)(2,1)S(1)}, u32[]{:S(2)}, u32[]{:S(2)}) collective-permute-start(bf16[2,128,256]{2,1,0:T(8,128)(2,1)S(1)} %slice.40), channel_id=1, source_target_pairs={{508,0},{0,4},{4,8},{8,12},{12,16},{16,20},{20,24},{24,28},{28,32}... | collective-permute-start | bytes 393224 | tf_op jit(solution)/shard_map/ppermute | solution.py:16
  82.5 1.0 copy-start.4
  82.5 1.2 copy-start.6
  86.8 12.3 %all-to-all-start.2 = ((bf16[4,2,128,256]{3,2,1,0:T(8,128)(2,1)}), bf16[4,2,128,256]{3,2,1,0:T(8,128)(2,1)S(1)}, u32[]{:S(2)}, u32[]{:S(2)}) async-start(bf16[4,2,128,256]{3,2,1,0:T(8,128)(2,1)} %broadcast_in_dim.11), calls=%async_computation.2 | async-start | bytes 1048576 | tf_op jit(solution)/shard_map/all_to_all | solution.py:86
  99.3 1.0 copy-start.5
  99.3 1.2 copy-start.7
  101.0 1.1 copy-start.1
  102.2 0.9 slice-start
  102.2 1.1 copy-start.2
  102.2 1.1 copy-start.3
  102.2 1.1 copy-start.8

commit v8 on v7

--- a/solution.py
+++ b/solution.py
@@ -135,7 +135,10 @@
     back = jnp.einsum(
         "rsq,rsw->qw", recv_hot, back_payload, preferred_element_type=jnp.float32
     ).astype(jnp.bfloat16)
+    back_width = back.shape[1]
+    back = lax.optimization_barrier(back).reshape(n_dev, per_peer * back_width)
     home = lax.all_to_all(back, "span", split_axis=0, concat_axis=0, tiled=True)
+    home = lax.optimization_barrier(home.reshape(buffer_rows, back_width))
     token_all = jnp.einsum("rtq,qw->rtw", send_hot, home, preferred_element_type=jnp.float32)
     token_rows = token_all[:, :, :head_cols]
     token_totals = (

time: 175 us -> 178 us (1.017)
  blocking collectives: 124 us -> 116 us
  other arithmetic: 7.15 us -> 14.8 us
  local copies, waits for them, and re-layouts: 9.82 us -> 13.5 us
    all_to_all x1, blocking collectives: 55.2 us -> 47.2 us  [shards(): home = lax.all_to_all(back, 'span', split_axis=0, concat_axis=0, tiled=True)]
    all_to_all x0 -> x2, other arithmetic: none -> 7.63 us  [shards(): home = lax.all_to_all(back, 'span', split_axis=0, concat_axis=0, tiled=True)]
where the time goes in v8:
time: 178 us; the launch traced here: 177 us
  blocking collectives  116 us (65%)
  waiting for transfers between devices  18.4 us (10%)
  other arithmetic  14.8 us (8%)
  local copies, waits for them, and re-layouts  13.5 us (8%)
  starting transfers between devices  9.08 us (5%)
  matrix products  5.54 us (3%)
    all_to_all x1, blocking collectives, shards(): lax.all_to_all(outgoing, 'span', split_axis=0, concat_axis=0, tiled=True)  57.1 us
    all_to_all x1, blocking collectives, shards(): home = lax.all_to_all(back, 'span', split_axis=0, concat_axis=0, tiled=True)  47.2 us
    ppermute x1, waiting for transfers between devices, passed_along(): return lax.ppermute(block, axis, route)  12.5 us
    all_to_all x1, blocking collectives, shards(): lax.all_to_all(group_part.reshape(n_groups, rows_here // n_groups, group_...  11.2 us
    all_to_all x2, other arithmetic, shards(): home = lax.all_to_all(back, 'span', split_axis=0, concat_axis=0, tiled=True)  7.63 us
    all_to_all x2, starting transfers between devices, gather_features(): lax.all_to_all(copies, 'head', split_axis=0, concat_axis=0, tiled=True)  7.16 us
    all_to_all x2, waiting for transfers between devices, gather_features(): lax.all_to_all(copies, 'head', split_axis=0, concat_axis=0, tiled=True)  5.99 us
  transfers between devices with their start and end apart: 3, of which 2 were waited for; matrix products, arithmetic and copies ran while one was open for 2% of the time, Pallas kernels for 0%

profile of v8, /device:TPU:6, one launch (start us, length us, event | category | flops | bytes accessed | tf_op | source)
XLA Modules:
  0.0 177.3 jit_solution(18168970926781109149)
XLA Ops:
  0.0 0.7 and_select_fusion.2
  0.8 0.7 and_select_fusion.1
  1.5 0.5 convert_reduce_fusion.1
  1.9 0.8 add_add_fusion
  3.0 1.3 fusion.12
  4.2 57.1 %all_to_all.37 = bf16[128,8,256]{2,1,0:T(8,128)(2,1)S(1)} all-to-all(bf16[128,8,256]{2,1,0:T(8,128)(2,1)S(1)} %fusion.12), channel_id=1, replica_groups=mesh['span'=128,'head'=4] {'span'}, dimensions={0} | all-to-all | bytes 1048576 | tf_op jit(solution)/shard_map/all_to_all | solution.py:76
  61.3 0.5 fusion.13
  61.8 1.1 broadcast_in_dim.10
  62.9 3.5 %all-to-all-start.1 = ((bf16[4,2,256,256]{3,2,1,0:T(8,128)(2,1)}), bf16[4,2,256,256]{3,2,1,0:T(8,128)(2,1)S(1)}, u32[]{:S(2)}, u32[]{:S(2)}) async-start(bf16[4,2,256,256]{3,2,1,0:T(8,128)(2,1)} %broadcast_in_dim.10), calls=%async_computation.1 | async-start | bytes 2097152 | tf_op jit(solution)/shard_map/all_to_all | solution.py:86
  66.4 1.9 %collective-permute-start = (bf16[2,128,256]{2,1,0:T(8,128)(2,1)S(1)}, bf16[2,128,256]{2,1,0:T(8,128)(2,1)S(1)}, u32[]{:S(2)}, u32[]{:S(2)}) collective-permute-start(bf16[2,128,256]{2,1,0:T(8,128)(2,1)S(1)} %slice.40), channel_id=1, source_target_pairs={{508,0},{0,4},{4,8},{8,12},{12,16},{16,20},{20,24},{24,28},{28,32}... | collective-permute-start | bytes 393224 | tf_op jit(solution)/shard_map/ppermute | solution.py:16
  68.4 0.7 iota_compare_fusion.12
  69.1 12.5 %collective-permute-done = bf16[2,128,256]{2,1,0:T(8,128)(2,1)S(1)} collective-permute-done((bf16[2,128,256]{2,1,0:T(8,128)(2,1)S(1)}, bf16[2,128,256]{2,1,0:T(8,128)(2,1)S(1)}, u32[]{:S(2)}, u32[]{:S(2)}) %collective-permute-start) | collective-permute-done | bytes 131104 | tf_op jit(solution)/shard_map/ppermute | solution.py:16
  81.5 0.5 copy.56
  82.2 0.3 fusion.3
  82.8 0.7 copy-done.4
  83.7 0.7 convolution_convert_fusion.2
  84.6 0.3 reshape.148
  84.9 1.0 reshape.147
  85.9 0.8 broadcast_in_dim.11
  86.7 3.6 %all-to-all-start.2 = ((bf16[4,2,128,256]{3,2,1,0:T(8,128)(2,1)}), bf16[4,2,128,256]{3,2,1,0:T(8,128)(2,1)S(1)}, u32[]{:S(2)}, u32[]{:S(2)}) async-start(bf16[4,2,128,256]{3,2,1,0:T(8,128)(2,1)} %broadcast_in_dim.11), calls=%async_computation.2 | async-start | bytes 1048576 | tf_op jit(solution)/shard_map/all_to_all | solution.py:86
  90.4 0.3 mul.121
  90.7 0.6 reduce_sum.127
  91.6 0.6 mul.129
  92.2 0.4 mul.130
  93.0 6.0 %all-to-all-done.2 = bf16[4,2,128,256]{3,2,1,0:T(8,128)(2,1)S(1)} async-done(((bf16[4,2,128,256]{3,2,1,0:T(8,128)(2,1)}), bf16[4,2,128,256]{3,2,1,0:T(8,128)(2,1)S(1)}, u32[]{:S(2)}, u32[]{:S(2)}) %all-to-all-start.2) | async-done | bytes 524320 | tf_op jit(solution)/shard_map/all_to_all | solution.py:86
  99.0 0.3 copy.54
  99.8 0.5 copy-done.5
  100.5 0.5 convolution_convert_fusion.3
  101.2 0.3 reduce_sum.128
  101.5 0.3 mul.126
  102.3 0.7 slice-done
  103.3 0.5 fusion.52
  103.8 0.4 fusion.14
  104.2 0.3 copy.75
  104.7 0.6 fusion.11
  105.3 0.4 copy.67
  105.7 1.1 all_to_all.31
  106.7 0.5 broadcast.147
  107.3 4.1 %reduce.7 = bf16[128,2080]{1,0:T(8,128)(2,1)S(1)} reduce(bf16[128,1,2080]{2,1,0:T(2,128)(2,1)S(1)} %all_to_all.31, bf16[]{:T(256)} %broadcast.147), dimensions={1}, to_apply=%all_to_all.31.reduce_sub_computation | reduce | bytes 1064962 | tf_op jit(solution)/shard_map/all_to_all | solution.py:140
  111.4 0.6 reshape.155
  112.0 47.2 %all_to_all.38 = bf16[128,2,1040]{2,1,0:T(2,128)(2,1)S(1)} all-to-all(bf16[128,2,1040]{2,1,0:T(2,128)(2,1)S(1)} %reshape.155), channel_id=1, replica_groups=mesh['span'=128,'head'=4] {'span'}, dimensions={0} | all-to-all | bytes 1064960 | tf_op jit(solution)/shard_map/all_to_all | solution.py:140
  159.1 0.6 reshape.156
  159.8 3.5 %reduce.6 = bf16[128,2080]{1,0:T(8,128)(2,1)S(1)} reduce(bf16[128,1,2080]{2,1,0:T(2,128)(2,1)S(1)} %reshape.156, bf16[]{:T(256)} %constant.59), dimensions={1}, to_apply=%all_to_all.29.reduce_sub_computation | reduce | bytes 1064962 | tf_op jit(solution)/shard_map/all_to_all | solution.py:140
  163.3 0.9 reshape.143
  164.2 0.7 fusion.6
  165.0 0.3 convolution_convert_fusion
  165.3 11.2 %all_to_all.39 = bf16[4,64,1024]{2,1,0:T(8,128)(2,1)S(1)} all-to-all(bf16[4,64,1024]{2,1,0:T(8,128)(2,1)S(1)} %bitcast.71), channel_id=1, replica_groups=mesh['span'=128,'head'=4] {'head'}, dimensions={0} | all-to-all | bytes 1048576 | tf_op jit(solution)/shard_map/all_to_all | solution.py:155
  176.6 0.7 reduce_sum.132
  (55 shorter events, 3.3 us)
Async XLA Ops:
  0.0 165.0 %copy-start = (bf16[256,1024]{1,0:T(8,128)(2,1)S(1)}, bf16[256,1024]{1,0:T(8,128)(2,1)}, u32[]{:S(2)}) copy-start(bf16[256,1024]{1,0:T(8,128)(2,1)} %param.10) | copy-start | bytes 1572868
  62.9 18.6 %all-to-all-start.1 = ((bf16[4,2,256,256]{3,2,1,0:T(8,128)(2,1)}), bf16[4,2,256,256]{3,2,1,0:T(8,128)(2,1)S(1)}, u32[]{:S(2)}, u32[]{:S(2)}) async-start(bf16[4,2,256,256]{3,2,1,0:T(8,128)(2,1)} %broadcast_in_dim.10), calls=%async_computation.1 | async-start | bytes 2097152 | tf_op jit(solution)/shard_map/all_to_all | solution.py:86
  66.4 15.1 %collective-permute-start = (bf16[2,128,256]{2,1,0:T(8,128)(2,1)S(1)}, bf16[2,128,256]{2,1,0:T(8,128)(2,1)S(1)}, u32[]{:S(2)}, u32[]{:S(2)}) collective-permute-start(bf16[2,128,256]{2,1,0:T(8,128)(2,1)S(1)} %slice.40), channel_id=1, source_target_pairs={{508,0},{0,4},{4,8},{8,12},{12,16},{16,20},{20,24},{24,28},{28,32}... | collective-permute-start | bytes 393224 | tf_op jit(solution)/shard_map/ppermute | solution.py:16
  82.5 1.0 copy-start.4
  82.5 1.2 copy-start.6
  86.7 12.3 %all-to-all-start.2 = ((bf16[4,2,128,256]{3,2,1,0:T(8,128)(2,1)}), bf16[4,2,128,256]{3,2,1,0:T(8,128)(2,1)S(1)}, u32[]{:S(2)}, u32[]{:S(2)}) async-start(bf16[4,2,128,256]{3,2,1,0:T(8,128)(2,1)} %broadcast_in_dim.11), calls=%async_computation.2 | async-start | bytes 1048576 | tf_op jit(solution)/shard_map/all_to_all | solution.py:86
  99.3 1.0 copy-start.5
  99.3 1.2 copy-start.7
  101.0 1.1 copy-start.1
  102.2 0.9 slice-start
  102.2 1.1 copy-start.2
  102.2 1.1 copy-start.3
  102.2 1.1 copy-start.8

commit v9 on v6

--- a/solution.py
+++ b/solution.py
@@ -77,27 +77,27 @@
     arrived = jnp.einsum(
         "rsq,qf->rsf", recv_hot, incoming, preferred_element_type=jnp.float32
     ).astype(jnp.bfloat16)
-    prior_block = passed_along(arrived[:, rows_here - BLOCK :], "span", 1)
-    with_prior = jnp.concatenate([prior_block, arrived], axis=1)
     n_groups = lax.axis_size("head")
-    copies = jnp.broadcast_to(with_prior[None], (n_groups,) + with_prior.shape)
+    joined = jnp.concatenate([common_lookup_projector, content_projector], axis=1)
+    copies = jnp.broadcast_to(arrived[None], (n_groups,) + arrived.shape)
     gathered = lax.all_to_all(copies, "head", split_axis=0, concat_axis=0, tiled=True)
-    full_rows = jnp.moveaxis(gathered, 0, 2).reshape(
-        with_prior.shape[:2] + (n_groups * with_prior.shape[2],)
-    )
+    full_rows = jnp.moveaxis(gathered, 0, 2).reshape(arrived.shape[:2] + (-1,))
     normed = layer_norm(full_rows)
-    joined = jnp.concatenate([common_lookup_projector, content_projector], axis=1)
     both = jnp.einsum(
         "rsf,fw->rsw", normed, joined, preferred_element_type=jnp.float32
     ).astype(jnp.bfloat16)
-    span_rows = rows_here + BLOCK
-    sorted_shared = both[:, :, :head_cols]
-    sorted_values = both[:, :, head_cols:]
-    spread = sorted_shared.reshape(n_rounds, span_rows, heads_here, HEAD_DIM).astype(jnp.float32)
-    unitlength_address_lines = (
+    spread = both[:, :, :head_cols].reshape(n_rounds, rows_here, heads_here, HEAD_DIM)
+    spread = spread.astype(jnp.float32)
+    keys_here = (
         spread * lax.rsqrt(jnp.sum(spread * spread, axis=-1, keepdims=True) + 1e-06)
-    ).astype(jnp.bfloat16)
-    unitlength_address_lines = unitlength_address_lines.reshape(n_rounds, span_rows, head_cols)
+    ).astype(jnp.bfloat16).reshape(n_rounds, rows_here, head_cols)
+    values_here = both[:, :, head_cols:]
+    last_block = jnp.concatenate(
+        [keys_here[:, rows_here - BLOCK :], values_here[:, rows_here - BLOCK :]], axis=2
+    )
+    prior_block = passed_along(last_block, "span", 1)
+    unitlength_address_lines = jnp.concatenate([prior_block[:, :, :head_cols], keys_here], axis=1)
+    sorted_values = jnp.concatenate([prior_block[:, :, head_cols:], values_here], axis=1)
     keys_cur = unitlength_address_lines[:, BLOCK:].reshape(n_rounds, blocks_here, BLOCK, head_cols)
     key_rows = jnp.stack(
         [unitlength_address_lines[:, b * BLOCK : b * BLOCK + 2 * BLOCK] for b in range(blocks_here)],

time: 176 us -> 169 us (0.960)
  waiting for transfers between devices: 27.4 us -> 23.5 us
    all_to_all x1, waiting for transfers between devices: 20 us -> 14.3 us  [shards(): lax.all_to_all(copies, 'head', split_axis=0, concat_axis=0, tiled=True)]
    ppermute x1, waiting for transfers between devices: 7.34 us -> 9.22 us  [passed_along(): return lax.ppermute(block, axis, route)]
  transfers between devices with their start and end apart: 2 -> 2, of which waited for: 2 -> 2; matrix products, arithmetic and copies ran while one was open for 0% -> 1% of each run, Pallas kernels for 0% -> 0%
where the time goes in v9:
time: 169 us
  blocking collectives  122 us (72%)
  waiting for transfers between devices  23.5 us (14%)
  other arithmetic  6.36 us (4%)
  local copies, waits for them, and re-layouts  6.14 us (4%)
  starting transfers between devices  5.42 us (3%)
  matrix products  5.07 us (3%)
    all_to_all x1, blocking collectives, shards(): lax.all_to_all(outgoing, 'span', split_axis=0, concat_axis=0, tiled=True)  57.1 us
    all_to_all x1, blocking collectives, shards(): home = lax.all_to_all(back, 'span', split_axis=0, concat_axis=0, tiled=True)  53.3 us
    all_to_all x1, waiting for transfers between devices, shards(): lax.all_to_all(copies, 'head', split_axis=0, concat_axis=0, tiled=True)  14.3 us
    all_to_all x1, blocking collectives, shards(): lax.all_to_all(group_part.reshape(n_groups, rows_here // n_groups, group_...  11.2 us
    ppermute x1, waiting for transfers between devices, passed_along(): return lax.ppermute(block, axis, route)  9.22 us
    all_to_all x1, starting transfers between devices, shards(): lax.all_to_all(copies, 'head', split_axis=0, concat_axis=0, tiled=True)  3.51 us
  transfers between devices with their start and end apart: 2, of which 2 were waited for; matrix products, arithmetic and copies ran while one was open for 1% of the time, Pallas kernels for 0%

profile of v9, /device:TPU:6, one launch (start us, length us, event | category | flops | bytes accessed | tf_op | source)
XLA Modules:
  0.0 168.5 jit_solution(1415250479375193761)
XLA Ops:
  0.0 0.7 and_select_fusion.2
  0.8 0.7 and_select_fusion.1
  1.5 0.5 convert_reduce_fusion.1
  1.9 0.8 add_add_fusion
  2.7 0.3 convert_reduce_fusion
  3.0 1.3 fusion.12
  4.2 57.1 %all_to_all.34 = bf16[128,8,256]{2,1,0:T(8,128)(2,1)S(1)} all-to-all(bf16[128,8,256]{2,1,0:T(8,128)(2,1)S(1)} %fusion.12), channel_id=1, replica_groups=mesh['span'=128,'head'=4] {'span'}, dimensions={0} | all-to-all | bytes 1048576 | tf_op jit(solution)/shard_map/all_to_all | solution.py:76
  61.3 0.5 fusion.13
  61.8 1.1 broadcast_in_dim.8
  62.9 3.5 %all-to-all-start.1 = ((bf16[4,2,256,256]{3,2,1,0:T(8,128)(2,1)}), bf16[4,2,256,256]{3,2,1,0:T(8,128)(2,1)S(1)}, u32[]{:S(2)}, u32[]{:S(2)}) async-start(bf16[4,2,256,256]{3,2,1,0:T(8,128)(2,1)} %broadcast_in_dim.8), calls=%async_computation.1 | async-start | bytes 2097152 | tf_op jit(solution)/shard_map/all_to_all | solution.py:83
  66.4 0.1 iota_compare_fusion.12
  66.5 14.3 %all-to-all-done.1 = bf16[4,2,256,256]{3,2,1,0:T(8,128)(2,1)S(1)} async-done(((bf16[4,2,256,256]{3,2,1,0:T(8,128)(2,1)}), bf16[4,2,256,256]{3,2,1,0:T(8,128)(2,1)S(1)}, u32[]{:S(2)}, u32[]{:S(2)}) %all-to-all-start.1) | async-done | bytes 1048608 | tf_op jit(solution)/shard_map/all_to_all | solution.py:83
  80.8 0.5 copy.50
  81.4 0.2 bitcast_reduce_fusion
  81.5 0.3 fusion.3
  81.9 0.3 fusion.1
  82.1 0.7 copy-done.1
  82.9 0.2 copy-done.2
  83.1 0.7 convolution_convert_fusion.2
  83.9 0.3 mul.89
  84.1 0.6 reduce_sum.98
  84.8 0.6 mul.90
  85.4 0.4 mul.91
  85.8 0.1 multiply_convert_fusion
  85.9 0.7 pad_maximum_fusion.2
  86.6 1.9 %collective-permute-start = (bf16[2,128,512]{2,1,0:T(8,128)(2,1)}, bf16[2,128,512]{2,1,0:T(8,128)(2,1)S(1)}, u32[]{:S(2)}, u32[]{:S(2)}) collective-permute-start(bf16[2,128,512]{2,1,0:T(8,128)(2,1)} %pad_maximum_fusion.2), channel_id=1, source_target_pairs={{508,0},{0,4},{4,8},{8,12},{12,16},{16,20},{20,24},{24,28},{28,32}... | collective-permute-start | bytes 786440 | tf_op jit(solution)/shard_map/ppermute | solution.py:16
  88.6 0.1 fusion.47
  88.6 0.1 copy.56
  88.7 0.3 reshape.113
  89.0 0.3 reshape.112
  89.3 0.1 copy.54
  89.4 0.1 copy.66
  89.6 0.2 fusion.29
  89.8 9.2 %collective-permute-done = bf16[2,128,512]{2,1,0:T(8,128)(2,1)S(1)} collective-permute-done((bf16[2,128,512]{2,1,0:T(8,128)(2,1)}, bf16[2,128,512]{2,1,0:T(8,128)(2,1)S(1)}, u32[]{:S(2)}, u32[]{:S(2)}) %collective-permute-start) | collective-permute-done | bytes 262176 | tf_op jit(solution)/shard_map/ppermute | solution.py:16
  99.0 0.1 copy.65
  99.2 0.1 stack.18
  99.3 0.4 copy-done.3
  99.7 0.5 fusion.49
  100.2 0.4 fusion.14
  100.6 0.3 copy.67
  100.9 0.2 reshape.118
  101.1 0.6 fusion.11
  101.7 0.4 copy.61
  102.1 53.3 %all_to_all.35 = bf16[128,8,260]{2,1,0:T(8,128)(2,1)S(1)} all-to-all(bf16[128,8,260]{2,1,0:T(8,128)(2,1)S(1)} %bitcast.58), channel_id=1, replica_groups=mesh['span'=128,'head'=4] {'span'}, dimensions={0} | all-to-all | bytes 1064960 | tf_op jit(solution)/shard_map/all_to_all | solution.py:130
  155.4 0.7 fusion.6
  156.2 0.3 convolution_convert_fusion
  156.5 11.2 %all_to_all.36 = bf16[4,64,1024]{2,1,0:T(8,128)(2,1)S(1)} all-to-all(bf16[4,64,1024]{2,1,0:T(8,128)(2,1)S(1)} %bitcast.59), channel_id=1, replica_groups=mesh['span'=128,'head'=4] {'head'}, dimensions={0} | all-to-all | bytes 1048576 | tf_op jit(solution)/shard_map/all_to_all | solution.py:144
  167.8 0.7 reduce_sum.102
  (22 shorter events, 0.3 us)
Async XLA Ops:
  0.0 156.2 %copy-start = (bf16[256,1024]{1,0:T(8,128)(2,1)S(1)}, bf16[256,1024]{1,0:T(8,128)(2,1)}, u32[]{:S(2)}) copy-start(bf16[256,1024]{1,0:T(8,128)(2,1)} %param.10) | copy-start | bytes 1572868
  62.9 18.0 %all-to-all-start.1 = ((bf16[4,2,256,256]{3,2,1,0:T(8,128)(2,1)}), bf16[4,2,256,256]{3,2,1,0:T(8,128)(2,1)S(1)}, u32[]{:S(2)}, u32[]{:S(2)}) async-start(bf16[4,2,256,256]{3,2,1,0:T(8,128)(2,1)} %broadcast_in_dim.8), calls=%async_computation.1 | async-start | bytes 2097152 | tf_op jit(solution)/shard_map/all_to_all | solution.py:83
  81.8 1.0 copy-start.1
  81.9 1.2 copy-start.2
  86.6 12.3 %collective-permute-start = (bf16[2,128,512]{2,1,0:T(8,128)(2,1)}, bf16[2,128,512]{2,1,0:T(8,128)(2,1)S(1)}, u32[]{:S(2)}, u32[]{:S(2)}) collective-permute-start(bf16[2,128,512]{2,1,0:T(8,128)(2,1)} %pad_maximum_fusion.2), channel_id=1, source_target_pairs={{508,0},{0,4},{4,8},{8,12},{12,16},{16,20},{20,24},{24,28},{28,32}... | collective-permute-start | bytes 786440 | tf_op jit(solution)/shard_map/ppermute | solution.py:16
  99.0 0.7 copy-start.3

commit v10 on v9

--- a/solution.py
+++ b/solution.py
@@ -81,23 +81,32 @@
     joined = jnp.concatenate([common_lookup_projector, content_projector], axis=1)
     copies = jnp.broadcast_to(arrived[None], (n_groups,) + arrived.shape)
     gathered = lax.all_to_all(copies, "head", split_axis=0, concat_axis=0, tiled=True)
-    full_rows = jnp.moveaxis(gathered, 0, 2).reshape(arrived.shape[:2] + (-1,))
+    last_slice = arrived[:, rows_here - BLOCK :]
+    received = []
+    for shift in range(n_groups):
+        route = [
+            (s * n_groups + g, ((s + 1) % n_dev) * n_groups + (g + shift) % n_groups)
+            for s in range(n_dev)
+            for g in range(n_groups)
+        ]
+        received.append(lax.ppermute(last_slice, ("span", "head"), route))
+    received, gathered = lax.optimization_barrier((received, gathered))
+    group_here = lax.axis_index("head")
+    slice_order = (group_here - jnp.arange(n_groups, dtype=jnp.int32)) % n_groups
+    prior_slices = jnp.take(jnp.stack(received), slice_order, axis=0)
+    all_slices = jnp.concatenate([prior_slices, gathered], axis=2)
+    span_rows = rows_here + BLOCK
+    full_rows = jnp.moveaxis(all_slices, 0, 2).reshape(n_rounds, span_rows, -1)
     normed = layer_norm(full_rows)
     both = jnp.einsum(
         "rsf,fw->rsw", normed, joined, preferred_element_type=jnp.float32
     ).astype(jnp.bfloat16)
-    spread = both[:, :, :head_cols].reshape(n_rounds, rows_here, heads_here, HEAD_DIM)
+    spread = both[:, :, :head_cols].reshape(n_rounds, span_rows, heads_here, HEAD_DIM)
     spread = spread.astype(jnp.float32)
-    keys_here = (
+    unitlength_address_lines = (
         spread * lax.rsqrt(jnp.sum(spread * spread, axis=-1, keepdims=True) + 1e-06)
-    ).astype(jnp.bfloat16).reshape(n_rounds, rows_here, head_cols)
-    values_here = both[:, :, head_cols:]
-    last_block = jnp.concatenate(
-        [keys_here[:, rows_here - BLOCK :], values_here[:, rows_here - BLOCK :]], axis=2
-    )
-    prior_block = passed_along(last_block, "span", 1)
-    unitlength_address_lines = jnp.concatenate([prior_block[:, :, :head_cols], keys_here], axis=1)
-    sorted_values = jnp.concatenate([prior_block[:, :, head_cols:], values_here], axis=1)
+    ).astype(jnp.bfloat16).reshape(n_rounds, span_rows, head_cols)
+    sorted_values = both[:, :, head_cols:]
     keys_cur = unitlength_address_lines[:, BLOCK:].reshape(n_rounds, blocks_here, BLOCK, head_cols)
     key_rows = jnp.stack(
         [unitlength_address_lines[:, b * BLOCK : b * BLOCK + 2 * BLOCK] for b in range(blocks_here)],

time: 169 us -> 168 us (level)
  waiting for transfers between devices: 23.5 us -> 5.58 us
  starting transfers between devices: 5.42 us -> 19.9 us
    ppermute x1 -> x4, starting transfers between devices: 1.91 us -> 16.4 us  [shards(): received.append(lax.ppermute(last_slice, ('span', 'head'), route))]
    all_to_all x1, waiting for transfers between devices: 14.3 us -> 0.01 us  [shards(): lax.all_to_all(copies, 'head', split_axis=0, concat_axis=0, tiled=True)]
    ppermute x1 -> x4, waiting for transfers between devices: 9.22 us -> 5.58 us  [shards(): received.append(lax.ppermute(last_slice, ('span', 'head'), route))]
  transfers between devices with their start and end apart: 2 -> 5, of which waited for: 2 -> 2; matrix products, arithmetic and copies ran while one was open for 1% -> 0% of each run, Pallas kernels for 0% -> 0%
where the time goes in v10:
time: 168 us; the launch traced here: 167 us
  blocking collectives  123 us (73%)
  starting transfers between devices  19.9 us (12%)
  local copies, waits for them, and re-layouts  6.85 us (4%)
  other arithmetic  6.27 us (4%)
  waiting for transfers between devices  5.58 us (3%)
  matrix products  5.26 us (3%)
    all_to_all x1, blocking collectives, shards(): lax.all_to_all(outgoing, 'span', split_axis=0, concat_axis=0, tiled=True)  57.1 us
    all_to_all x1, blocking collectives, shards(): home = lax.all_to_all(back, 'span', split_axis=0, concat_axis=0, tiled=True)  54.6 us
    ppermute x4, starting transfers between devices, shards(): received.append(lax.ppermute(last_slice, ('span', 'head'), route))  16.4 us
    all_to_all x1, blocking collectives, shards(): lax.all_to_all(group_part.reshape(n_groups, rows_here // n_groups, group_...  11.2 us
    ppermute x4, waiting for transfers between devices, shards(): received.append(lax.ppermute(last_slice, ('span', 'head'), route))  5.58 us
    all_to_all x1, starting transfers between devices, shards(): lax.all_to_all(copies, 'head', split_axis=0, concat_axis=0, tiled=True)  3.51 us
  transfers between devices with their start and end apart: 5, of which 2 were waited for; matrix products, arithmetic and copies ran while one was open for 0% of the time, Pallas kernels for 0%

profile of v10, /device:TPU:6, one launch (start us, length us, event | category | flops | bytes accessed | tf_op | source)
XLA Modules:
  0.0 167.2 jit_solution(910392794478586996)
XLA Ops:
  0.0 0.7 and_select_fusion.1
  0.8 0.7 and_select_fusion.2
  1.5 0.5 convert_reduce_fusion.1
  1.9 0.8 add_add_fusion
  2.7 0.3 convert_reduce_fusion
  3.0 1.3 fusion.12
  4.2 57.1 %all_to_all.34 = bf16[128,8,256]{2,1,0:T(8,128)(2,1)S(1)} all-to-all(bf16[128,8,256]{2,1,0:T(8,128)(2,1)S(1)} %fusion.12), channel_id=1, replica_groups=mesh['span'=128,'head'=4] {'span'}, dimensions={0} | all-to-all | bytes 1048576 | tf_op jit(solution)/shard_map/all_to_all | solution.py:76
  61.3 0.5 fusion.13
  61.8 1.1 broadcast_in_dim.16
  62.9 3.5 %all-to-all-start.1 = ((bf16[4,2,256,256]{3,2,1,0:T(8,128)(2,1)}), bf16[4,2,256,256]{3,2,1,0:T(8,128)(2,1)S(1)}, u32[]{:S(2)}, u32[]{:S(2)}) async-start(bf16[4,2,256,256]{3,2,1,0:T(8,128)(2,1)} %broadcast_in_dim.16), calls=%async_computation.1 | async-start | bytes 2097152 | tf_op jit(solution)/shard_map/all_to_all | solution.py:83
  66.4 0.1 iota_compare_fusion.12
  66.6 1.9 %collective-permute-start = (bf16[2,128,256]{2,1,0:T(8,128)(2,1)S(1)}, bf16[2,128,256]{2,1,0:T(8,128)(2,1)S(1)}, u32[]{:S(2)}, u32[]{:S(2)}) collective-permute-start(bf16[2,128,256]{2,1,0:T(8,128)(2,1)S(1)} %slice.42), channel_id=1, source_target_pairs={{0,4},{1,5},{2,6},{3,7},{4,8},{5,9},{6,10},{7,11},{8,12},{9,13},{1... | collective-permute-start | bytes 393224 | tf_op jit(solution)/shard_map/ppermute | solution.py:92
  68.5 6.5 %collective-permute-start.1 = (bf16[2,128,256]{2,1,0:T(8,128)(2,1)S(1)}, bf16[2,128,256]{2,1,0:T(8,128)(2,1)S(1)}, u32[]{:S(2)}, u32[]{:S(2)}) collective-permute-start(bf16[2,128,256]{2,1,0:T(8,128)(2,1)S(1)} %slice.42), channel_id=1, source_target_pairs={{0,5},{1,6},{2,7},{3,4},{4,9},{5,10},{6,11},{7,8},{8,13},{9,14},{1... | collective-permute-start | bytes 393224 | tf_op jit(solution)/shard_map/ppermute | solution.py:92
  75.0 3.3 %collective-permute-start.2 = (bf16[2,128,256]{2,1,0:T(8,128)(2,1)S(1)}, bf16[2,128,256]{2,1,0:T(8,128)(2,1)S(1)}, u32[]{:S(2)}, u32[]{:S(2)}) collective-permute-start(bf16[2,128,256]{2,1,0:T(8,128)(2,1)S(1)} %slice.42), channel_id=1, source_target_pairs={{0,6},{1,7},{2,4},{3,5},{4,10},{5,11},{6,8},{7,9},{8,14},{9,15},{1... | collective-permute-start | bytes 393224 | tf_op jit(solution)/shard_map/ppermute | solution.py:92
  78.3 4.7 %collective-permute-start.3 = (bf16[2,128,256]{2,1,0:T(8,128)(2,1)S(1)}, bf16[2,128,256]{2,1,0:T(8,128)(2,1)S(1)}, u32[]{:S(2)}, u32[]{:S(2)}) collective-permute-start(bf16[2,128,256]{2,1,0:T(8,128)(2,1)S(1)} %slice.42), channel_id=1, source_target_pairs={{0,7},{1,4},{2,5},{3,6},{4,11},{5,8},{6,9},{7,10},{8,15},{9,12},{1... | collective-permute-start | bytes 393224 | tf_op jit(solution)/shard_map/ppermute | solution.py:92
  83.0 4.2 %collective-permute-done.2 = bf16[2,128,256]{2,1,0:T(8,128)(2,1)S(1)} collective-permute-done((bf16[2,128,256]{2,1,0:T(8,128)(2,1)S(1)}, bf16[2,128,256]{2,1,0:T(8,128)(2,1)S(1)}, u32[]{:S(2)}, u32[]{:S(2)}) %collective-permute-start.2) | collective-permute-done | bytes 131104 | tf_op jit(solution)/shard_map/ppermute | solution.py:92
  87.2 1.4 collective-permute-done.3
  88.6 0.1 pad_maximum_fusion.1
  88.7 0.6 gather_fusion
  89.3 0.1 broadcast_select_fusion
  89.4 0.3 copy.45
  89.7 0.5 copy.46
  90.2 0.3 bitcast_reduce_fusion
  90.5 0.4 fusion.3
  90.9 0.4 fusion.1
  91.4 0.6 copy-done.1
  92.0 0.2 copy-done.2
  92.1 1.0 convolution_convert_fusion
  93.2 0.4 mul.72
  93.6 0.9 reduce_sum.98
  94.6 1.0 mul.73
  95.5 0.6 mul.74
  96.2 0.1 fusion.20
  96.3 0.1 stack.42
  96.7 0.1 copy.59
  96.8 0.1 copy.60
  97.0 0.2 copy-done.3
  97.2 0.4 fusion.49
  97.6 0.4 fusion.14
  98.0 0.3 copy.61
  98.3 0.2 reshape.148
  98.5 0.6 fusion.11
  99.1 0.4 copy.55
  99.5 54.6 %all_to_all.35 = bf16[128,8,260]{2,1,0:T(8,128)(2,1)S(1)} all-to-all(bf16[128,8,260]{2,1,0:T(8,128)(2,1)S(1)} %bitcast.62), channel_id=1, replica_groups=mesh['span'=128,'head'=4] {'span'}, dimensions={0} | all-to-all | bytes 1064960 | tf_op jit(solution)/shard_map/all_to_all | solution.py:139
  154.1 0.7 fusion.6
  154.9 0.3 convolution_convert_fusion.1
  155.2 11.2 %all_to_all.36 = bf16[4,64,1024]{2,1,0:T(8,128)(2,1)S(1)} all-to-all(bf16[4,64,1024]{2,1,0:T(8,128)(2,1)S(1)} %bitcast.63), channel_id=1, replica_groups=mesh['span'=128,'head'=4] {'head'}, dimensions={0} | all-to-all | bytes 1048576 | tf_op jit(solution)/shard_map/all_to_all | solution.py:153
  166.4 0.7 reduce_sum.102
  (29 shorter events, 0.6 us)
Async XLA Ops:
  0.0 154.9 %copy-start = (bf16[256,1024]{1,0:T(8,128)(2,1)S(1)}, bf16[256,1024]{1,0:T(8,128)(2,1)}, u32[]{:S(2)}) copy-start(bf16[256,1024]{1,0:T(8,128)(2,1)} %param.10) | copy-start | bytes 1572868
  62.9 25.7 %all-to-all-start.1 = ((bf16[4,2,256,256]{3,2,1,0:T(8,128)(2,1)}), bf16[4,2,256,256]{3,2,1,0:T(8,128)(2,1)S(1)}, u32[]{:S(2)}, u32[]{:S(2)}) async-start(bf16[4,2,256,256]{3,2,1,0:T(8,128)(2,1)} %broadcast_in_dim.16), calls=%async_computation.1 | async-start | bytes 2097152 | tf_op jit(solution)/shard_map/all_to_all | solution.py:83
  66.6 16.4 %collective-permute-start = (bf16[2,128,256]{2,1,0:T(8,128)(2,1)S(1)}, bf16[2,128,256]{2,1,0:T(8,128)(2,1)S(1)}, u32[]{:S(2)}, u32[]{:S(2)}) collective-permute-start(bf16[2,128,256]{2,1,0:T(8,128)(2,1)S(1)} %slice.42), channel_id=1, source_target_pairs={{0,4},{1,5},{2,6},{3,7},{4,8},{5,9},{6,10},{7,11},{8,12},{9,13},{1... | collective-permute-start | bytes 393224 | tf_op jit(solution)/shard_map/ppermute | solution.py:92
  68.5 14.5 %collective-permute-start.1 = (bf16[2,128,256]{2,1,0:T(8,128)(2,1)S(1)}, bf16[2,128,256]{2,1,0:T(8,128)(2,1)S(1)}, u32[]{:S(2)}, u32[]{:S(2)}) collective-permute-start(bf16[2,128,256]{2,1,0:T(8,128)(2,1)S(1)} %slice.42), channel_id=1, source_target_pairs={{0,5},{1,6},{2,7},{3,4},{4,9},{5,10},{6,11},{7,8},{8,13},{9,14},{1... | collective-permute-start | bytes 393224 | tf_op jit(solution)/shard_map/ppermute | solution.py:92
  75.0 12.2 %collective-permute-start.2 = (bf16[2,128,256]{2,1,0:T(8,128)(2,1)S(1)}, bf16[2,128,256]{2,1,0:T(8,128)(2,1)S(1)}, u32[]{:S(2)}, u32[]{:S(2)}) collective-permute-start(bf16[2,128,256]{2,1,0:T(8,128)(2,1)S(1)} %slice.42), channel_id=1, source_target_pairs={{0,6},{1,7},{2,4},{3,5},{4,10},{5,11},{6,8},{7,9},{8,14},{9,15},{1... | collective-permute-start | bytes 393224 | tf_op jit(solution)/shard_map/ppermute | solution.py:92
  78.3 10.3 %collective-permute-start.3 = (bf16[2,128,256]{2,1,0:T(8,128)(2,1)S(1)}, bf16[2,128,256]{2,1,0:T(8,128)(2,1)S(1)}, u32[]{:S(2)}, u32[]{:S(2)}) collective-permute-start(bf16[2,128,256]{2,1,0:T(8,128)(2,1)S(1)} %slice.42), channel_id=1, source_target_pairs={{0,7},{1,4},{2,5},{3,6},{4,11},{5,8},{6,9},{7,10},{8,15},{9,12},{1... | collective-permute-start | bytes 393224 | tf_op jit(solution)/shard_map/ppermute | solution.py:92
  90.9 1.0 copy-start.1
  90.9 1.2 copy-start.2
  96.5 0.7 copy-start.3

commit v11 on v10

--- a/solution.py
+++ b/solution.py
@@ -1,6 +1,8 @@
 import jax
 import jax.numpy as jnp
 from jax import lax
+from jax.experimental import pallas as pl
+from jax.experimental.pallas import tpu as pltpu
 from jax.sharding import PartitionSpec as P
 
 HEAD_DIM = 128
@@ -22,6 +24,57 @@
     centred = content_embeddings - row_mean
     row_var = jnp.mean(centred * centred, axis=-1, keepdims=True)
     return (centred * lax.rsqrt(row_var + epsilon)).astype(jnp.bfloat16)
+
+
+def block_attention_kernel(sharp_ref, key_ref, value_ref, out_ref, total_ref):
+    scale = sharp_ref[pl.program_id(1)]
+    n_blocks = out_ref.shape[1] // BLOCK
+    rows = lax.broadcasted_iota(jnp.int32, (BLOCK, 2 * BLOCK), 0)
+    cols = lax.broadcasted_iota(jnp.int32, (BLOCK, 2 * BLOCK), 1)
+    allowed = cols != rows + BLOCK
+    for b in range(n_blocks):
+        queries = key_ref[0, BLOCK * (b + 1) : BLOCK * (b + 2), :]
+        keys = key_ref[0, BLOCK * b : BLOCK * (b + 2), :]
+        values = value_ref[0, BLOCK * b : BLOCK * (b + 2), :]
+        scores = lax.dot_general(
+            queries, keys, (((1,), (1,)), ((), ())), preferred_element_type=jnp.float32
+        ) * scale
+        exp_scores = jnp.where(allowed, jnp.exp(scores), 0.0)
+        totals = jnp.sum(exp_scores, axis=1, keepdims=True)
+        weights = (exp_scores / totals).astype(jnp.bfloat16)
+        mixed = jnp.dot(weights, values, preferred_element_type=jnp.float32)
+        out_ref[0, BLOCK * b : BLOCK * (b + 1), :] = mixed.astype(out_ref.dtype)
+        total_ref[0, 0, BLOCK * b : BLOCK * (b + 1), :] = totals
+
+
+def block_attention(keys_all, values_all, sharpness, head_dim):
+    n_rounds, span_rows, cols = keys_all.shape
+    rows_here = span_rows - BLOCK
+    heads = cols // head_dim
+    n_blocks = rows_here // BLOCK
+    flops = n_rounds * heads * n_blocks * 4 * BLOCK * 2 * BLOCK * head_dim
+    return pl.pallas_call(
+        block_attention_kernel,
+        grid=(n_rounds, heads),
+        in_specs=[
+            pl.BlockSpec(memory_space=pltpu.SMEM),
+            pl.BlockSpec((1, span_rows, head_dim), lambda r, h: (r, 0, h)),
+            pl.BlockSpec((1, span_rows, head_dim), lambda r, h: (r, 0, h)),
+        ],
+        out_specs=[
+            pl.BlockSpec((1, rows_here, head_dim), lambda r, h: (r, 0, h)),
+            pl.BlockSpec((1, 1, rows_here, 1), lambda r, h: (r, h, 0, 0)),
+        ],
+        out_shape=[
+            jax.ShapeDtypeStruct((n_rounds, rows_here, cols), jnp.bfloat16),
+            jax.ShapeDtypeStruct((n_rounds, heads, rows_here, 1), jnp.float32),
+        ],
+        cost_estimate=pl.CostEstimate(
+            flops=flops,
+            transcendentals=n_rounds * heads * n_blocks * BLOCK * 2 * BLOCK,
+            bytes_accessed=2 * keys_all.size * 2 + n_rounds * rows_here * cols * 2,
+        ),
+    )(sharpness, keys_all, values_all)
 
 
 def rank_within_group(group, order):
@@ -107,28 +160,10 @@
         spread * lax.rsqrt(jnp.sum(spread * spread, axis=-1, keepdims=True) + 1e-06)
     ).astype(jnp.bfloat16).reshape(n_rounds, span_rows, head_cols)
     sorted_values = both[:, :, head_cols:]
-    keys_cur = unitlength_address_lines[:, BLOCK:].reshape(n_rounds, blocks_here, BLOCK, head_cols)
-    key_rows = jnp.stack(
-        [unitlength_address_lines[:, b * BLOCK : b * BLOCK + 2 * BLOCK] for b in range(blocks_here)],
-        axis=1,
-    ).reshape(n_rounds, blocks_here, 2 * BLOCK, heads_here, HEAD_DIM)
-    content_projector_lines = jnp.stack(
-        [sorted_values[:, b * BLOCK : b * BLOCK + 2 * BLOCK] for b in range(blocks_here)], axis=1
-    ).reshape(n_rounds, blocks_here, 2 * BLOCK, heads_here, HEAD_DIM)
-    queries = keys_cur.reshape(n_rounds, blocks_here, BLOCK, heads_here, HEAD_DIM)
-    similarity_energies = jnp.einsum(
-        "rbqhd,rbkhd->rbhqk", queries, key_rows, preferred_element_type=jnp.float32
-    )
-    similarity_energies = similarity_energies * lane_sharpness[None, None, :, None, None]
-    allowed = jnp.arange(2 * BLOCK)[None, :] != jnp.arange(BLOCK)[:, None] + BLOCK
-    exp_scores = jnp.where(allowed, jnp.exp(similarity_energies), 0.0)
-    row_totals = jnp.sum(exp_scores, axis=-1)
-    weights = (exp_scores / row_totals[..., None]).astype(jnp.bfloat16)
-    results = jnp.einsum(
-        "rbhqk,rbkhd->rbqhd", weights, content_projector_lines, preferred_element_type=jnp.float32
-    )
-    results = results.astype(jnp.bfloat16).reshape(n_rounds, rows_here, head_cols)
-    slot_totals = jnp.transpose(row_totals, (0, 1, 3, 2)).reshape(n_rounds, rows_here, heads_here)
+    results, block_totals = block_attention(
+        unitlength_address_lines, sorted_values, lane_sharpness, HEAD_DIM
+    )
+    slot_totals = jnp.transpose(block_totals[..., 0], (0, 2, 1))
     totals_high = slot_totals.astype(jnp.bfloat16)
     totals_low = (slot_totals - totals_high.astype(jnp.float32)).astype(jnp.bfloat16)
     back_payload = jnp.concatenate([results, totals_high, totals_low], axis=2)

time: 168 us -> 177 us (1.054)
  Pallas kernels: 0 us -> 4.53 us
  local copies, waits for them, and re-layouts: 6.85 us -> 10.5 us
    pallas_call x0 -> x1, Pallas kernels: none -> 4.53 us  [block_attention(): pl.pallas_call(block_attention_kernel, grid=(n_rounds, heads), in_specs=[...]
    squeeze x0 -> x1, local copies, waits for them, and re-layouts: none -> 4.11 us  [shards(): slot_totals = jnp.transpose(block_totals[..., 0], (0, 2, 1))]
where the time goes in v11:
time: 177 us; the launch traced here: 176 us
  blocking collectives  123 us (69%)
  starting transfers between devices  20.2 us (11%)
  local copies, waits for them, and re-layouts  10.5 us (6%)
  other arithmetic  6.97 us (4%)
  matrix products  5.51 us (3%)
  waiting for transfers between devices  5.08 us (3%)
  Pallas kernels  4.53 us (3%)
    all_to_all x1, blocking collectives, shards(): lax.all_to_all(outgoing, 'span', split_axis=0, concat_axis=0, tiled=True)  57.1 us
    all_to_all x1, blocking collectives, shards(): home = lax.all_to_all(back, 'span', split_axis=0, concat_axis=0, tiled=True)  53.8 us
    ppermute x4, starting transfers between devices, shards(): received.append(lax.ppermute(last_slice, ('span', 'head'), route))  16.7 us
    all_to_all x1, blocking collectives, shards(): lax.all_to_all(group_part.reshape(n_groups, rows_here // n_groups, group_...  11.8 us
    ppermute x4, waiting for transfers between devices, shards(): received.append(lax.ppermute(last_slice, ('span', 'head'), route))  5.08 us
    pallas_call x1, Pallas kernels, block_attention(): pl.pallas_call(block_attention_kernel, grid=(n_rounds, heads), in_specs=[...  4.53 us
    squeeze x1, local copies, waits for them, and re-layouts, shards(): slot_totals = jnp.transpose(block_totals[..., 0], (0, 2, 1))  4.11 us
  transfers between devices with their start and end apart: 5, of which 2 were waited for; matrix products, arithmetic and copies ran while one was open for 0% of the time, Pallas kernels for 0%

profile of v11, /device:TPU:6, one launch (start us, length us, event | category | flops | bytes accessed | tf_op | source)
XLA Modules:
  0.0 175.8 jit_solution(7093633098264957372)
XLA Ops:
  0.0 0.7 and_select_fusion.2
  0.8 0.7 and_select_fusion.1
  1.5 0.5 convert_reduce_fusion.1
  1.9 0.8 add_add_fusion
  2.7 0.3 convert_reduce_fusion
  3.0 1.3 fusion.10
  4.2 57.1 %all_to_all.34 = bf16[128,8,256]{2,1,0:T(8,128)(2,1)S(1)} all-to-all(bf16[128,8,256]{2,1,0:T(8,128)(2,1)S(1)} %fusion.10), channel_id=1, replica_groups=mesh['span'=128,'head'=4] {'span'}, dimensions={0} | all-to-all | bytes 1048576 | tf_op jit(solution)/shard_map/all_to_all | solution.py:129
  61.3 0.5 fusion.11
  61.8 1.1 broadcast_in_dim.10
  62.9 3.5 %all-to-all-start.1 = ((bf16[4,2,256,256]{3,2,1,0:T(8,128)(2,1)}), bf16[4,2,256,256]{3,2,1,0:T(8,128)(2,1)S(1)}, u32[]{:S(2)}, u32[]{:S(2)}) async-start(bf16[4,2,256,256]{3,2,1,0:T(8,128)(2,1)} %broadcast_in_dim.10), calls=%async_computation.1 | async-start | bytes 2097152 | tf_op jit(solution)/shard_map/all_to_all | solution.py:136
  66.4 2.2 %collective-permute-start.3 = (bf16[2,128,256]{2,1,0:T(8,128)(2,1)S(1)}, bf16[2,128,256]{2,1,0:T(8,128)(2,1)S(1)}, u32[]{:S(2)}, u32[]{:S(2)}) collective-permute-start(bf16[2,128,256]{2,1,0:T(8,128)(2,1)S(1)} %slice.26), channel_id=1, source_target_pairs={{0,7},{1,4},{2,5},{3,6},{4,11},{5,8},{6,9},{7,10},{8,15},{9,12},{1... | collective-permute-start | bytes 393224 | tf_op jit(solution)/shard_map/ppermute | solution.py:145
  68.6 6.3 %collective-permute-start.2 = (bf16[2,128,256]{2,1,0:T(8,128)(2,1)S(1)}, bf16[2,128,256]{2,1,0:T(8,128)(2,1)S(1)}, u32[]{:S(2)}, u32[]{:S(2)}) collective-permute-start(bf16[2,128,256]{2,1,0:T(8,128)(2,1)S(1)} %slice.26), channel_id=1, source_target_pairs={{0,6},{1,7},{2,4},{3,5},{4,10},{5,11},{6,8},{7,9},{8,14},{9,15},{1... | collective-permute-start | bytes 393224 | tf_op jit(solution)/shard_map/ppermute | solution.py:145
  74.9 2.1 %collective-permute-start.1 = (bf16[2,128,256]{2,1,0:T(8,128)(2,1)S(1)}, bf16[2,128,256]{2,1,0:T(8,128)(2,1)S(1)}, u32[]{:S(2)}, u32[]{:S(2)}) collective-permute-start(bf16[2,128,256]{2,1,0:T(8,128)(2,1)S(1)} %slice.26), channel_id=1, source_target_pairs={{0,5},{1,6},{2,7},{3,4},{4,9},{5,10},{6,11},{7,8},{8,13},{9,14},{1... | collective-permute-start | bytes 393224 | tf_op jit(solution)/shard_map/ppermute | solution.py:145
  77.0 6.1 %collective-permute-start = (bf16[2,128,256]{2,1,0:T(8,128)(2,1)S(1)}, bf16[2,128,256]{2,1,0:T(8,128)(2,1)S(1)}, u32[]{:S(2)}, u32[]{:S(2)}) collective-permute-start(bf16[2,128,256]{2,1,0:T(8,128)(2,1)S(1)} %slice.26), channel_id=1, source_target_pairs={{0,4},{1,5},{2,6},{3,7},{4,8},{5,9},{6,10},{7,11},{8,12},{9,13},{1... | collective-permute-start | bytes 393224 | tf_op jit(solution)/shard_map/ppermute | solution.py:145
  83.2 0.0 collective-permute-done.3
  83.2 0.0 collective-permute-done.2
  83.2 1.6 collective-permute-done.1
  84.8 3.4 %collective-permute-done = bf16[2,128,256]{2,1,0:T(8,128)(2,1)S(1)} collective-permute-done((bf16[2,128,256]{2,1,0:T(8,128)(2,1)S(1)}, bf16[2,128,256]{2,1,0:T(8,128)(2,1)S(1)}, u32[]{:S(2)}, u32[]{:S(2)}) %collective-permute-start) | collective-permute-done | bytes 131104 | tf_op jit(solution)/shard_map/ppermute | solution.py:145
  88.3 0.1 pad_maximum_fusion.1
  88.4 0.6 gather_fusion
  88.9 0.1 broadcast_select_fusion
  89.1 0.3 copy.35
  89.3 0.5 copy.36
  89.9 0.3 bitcast_reduce_fusion
  90.2 0.4 fusion.3
  90.6 0.0 copy-start.1
  90.6 0.0 copy-start.2
  90.6 0.4 fusion.1
  91.0 0.6 copy-done.1
  91.6 0.2 copy-done.2
  91.8 1.0 convolution_convert_fusion
  92.8 0.8 slice.28.value_ref
  93.6 0.1 convert_multiply_fusion.1
  93.7 0.4 mul.64
  94.1 0.9 reduce_sum.89
  95.0 0.1 add_rsqrt_fusion
  95.0 1.0 mul.65
  96.0 0.6 mul.66
  96.6 0.9 fusion.17.key_ref
  97.5 4.5 %shard_map.73 = (bf16[2,256,256]{2,1,0:T(8,128)(2,1)}, f32[2,2,256,1]{3,2,1,0:T(8,128)}) custom-call(f32[2]{0:T(128)} %sharp_ref.1, bf16[2,384,256]{2,1,0:T(8,128)(2,1)} %fusion.17.key_ref, bf16[2,384,256]{2,1,0:T(8,128)(2,1)} %slice.28.value_ref), custom_call_target="tpu_custom_call" | custom-call | flops 134217728 | bytes 1048576 | tf_op jit(solution)/shard_map/pallas_call | solution.py:56
  102.0 4.1 %copy.45 = f32[2,2,256,1]{1,2,0,3:T(8,128)S(1)} copy(f32[2,2,256,1]{3,2,1,0:T(8,128)} %get-tuple-element.18) | data formatting | bytes 8192 | tf_op jit(solution)/shard_map/squeeze | solution.py:166
  106.2 1.7 fusion.9
  107.9 0.4 copy.40
  108.3 53.8 %all_to_all.35 = bf16[128,8,260]{2,1,0:T(8,128)(2,1)S(1)} all-to-all(bf16[128,8,260]{2,1,0:T(8,128)(2,1)S(1)} %bitcast.56), channel_id=1, replica_groups=mesh['span'=128,'head'=4] {'span'}, dimensions={0} | all-to-all | bytes 1064960 | tf_op jit(solution)/shard_map/all_to_all | solution.py:174
  162.1 0.7 fusion.6
  162.9 0.3 convolution_convert_fusion.1
  163.2 11.8 %all_to_all.36 = bf16[4,64,1024]{2,1,0:T(8,128)(2,1)S(1)} all-to-all(bf16[4,64,1024]{2,1,0:T(8,128)(2,1)S(1)} %bitcast.57), channel_id=1, replica_groups=mesh['span'=128,'head'=4] {'head'}, dimensions={0} | all-to-all | bytes 1048576 | tf_op jit(solution)/shard_map/all_to_all | solution.py:188
  175.0 0.7 reduce_sum.92
  (15 shorter events, 0.2 us)
Async XLA Ops:
  0.0 162.9 %copy-start = (bf16[256,1024]{1,0:T(8,128)(2,1)S(1)}, bf16[256,1024]{1,0:T(8,128)(2,1)}, u32[]{:S(2)}) copy-start(bf16[256,1024]{1,0:T(8,128)(2,1)} %param.10) | copy-start | bytes 1572868
  62.9 25.4 %all-to-all-start.1 = ((bf16[4,2,256,256]{3,2,1,0:T(8,128)(2,1)}), bf16[4,2,256,256]{3,2,1,0:T(8,128)(2,1)S(1)}, u32[]{:S(2)}, u32[]{:S(2)}) async-start(bf16[4,2,256,256]{3,2,1,0:T(8,128)(2,1)} %broadcast_in_dim.10), calls=%async_computation.1 | async-start | bytes 2097152 | tf_op jit(solution)/shard_map/all_to_all | solution.py:136
  66.4 16.7 %collective-permute-start.3 = (bf16[2,128,256]{2,1,0:T(8,128)(2,1)S(1)}, bf16[2,128,256]{2,1,0:T(8,128)(2,1)S(1)}, u32[]{:S(2)}, u32[]{:S(2)}) collective-permute-start(bf16[2,128,256]{2,1,0:T(8,128)(2,1)S(1)} %slice.26), channel_id=1, source_target_pairs={{0,7},{1,4},{2,5},{3,6},{4,11},{5,8},{6,9},{7,10},{8,15},{9,12},{1... | collective-permute-start | bytes 393224 | tf_op jit(solution)/shard_map/ppermute | solution.py:145
  68.6 14.6 %collective-permute-start.2 = (bf16[2,128,256]{2,1,0:T(8,128)(2,1)S(1)}, bf16[2,128,256]{2,1,0:T(8,128)(2,1)S(1)}, u32[]{:S(2)}, u32[]{:S(2)}) collective-permute-start(bf16[2,128,256]{2,1,0:T(8,128)(2,1)S(1)} %slice.26), channel_id=1, source_target_pairs={{0,6},{1,7},{2,4},{3,5},{4,10},{5,11},{6,8},{7,9},{8,14},{9,15},{1... | collective-permute-start | bytes 393224 | tf_op jit(solution)/shard_map/ppermute | solution.py:145
  74.9 10.0 %collective-permute-start.1 = (bf16[2,128,256]{2,1,0:T(8,128)(2,1)S(1)}, bf16[2,128,256]{2,1,0:T(8,128)(2,1)S(1)}, u32[]{:S(2)}, u32[]{:S(2)}) collective-permute-start(bf16[2,128,256]{2,1,0:T(8,128)(2,1)S(1)} %slice.26), channel_id=1, source_target_pairs={{0,5},{1,6},{2,7},{3,4},{4,9},{5,10},{6,11},{7,8},{8,13},{9,14},{1... | collective-permute-start | bytes 393224 | tf_op jit(solution)/shard_map/ppermute | solution.py:145
  77.0 11.2 %collective-permute-start = (bf16[2,128,256]{2,1,0:T(8,128)(2,1)S(1)}, bf16[2,128,256]{2,1,0:T(8,128)(2,1)S(1)}, u32[]{:S(2)}, u32[]{:S(2)}) collective-permute-start(bf16[2,128,256]{2,1,0:T(8,128)(2,1)S(1)} %slice.26), channel_id=1, source_target_pairs={{0,4},{1,5},{2,6},{3,7},{4,8},{5,9},{6,10},{7,11},{8,12},{9,13},{1... | collective-permute-start | bytes 393224 | tf_op jit(solution)/shard_map/ppermute | solution.py:145
  90.6 1.0 copy-start.1
  90.6 1.2 copy-start.2

commit v12 on v11

--- a/solution.py
+++ b/solution.py
@@ -26,15 +26,19 @@
     return (centred * lax.rsqrt(row_var + epsilon)).astype(jnp.bfloat16)
 
 
-def block_attention_kernel(sharp_ref, key_ref, value_ref, out_ref, total_ref):
+def block_attention_kernel(sharp_ref, shared_ref, value_ref, out_ref, total_ref):
     scale = sharp_ref[pl.program_id(1)]
     n_blocks = out_ref.shape[1] // BLOCK
+    spread = shared_ref[0].astype(jnp.float32)
+    unit = (
+        spread * lax.rsqrt(jnp.sum(spread * spread, axis=1, keepdims=True) + 1e-06)
+    ).astype(jnp.bfloat16)
     rows = lax.broadcasted_iota(jnp.int32, (BLOCK, 2 * BLOCK), 0)
     cols = lax.broadcasted_iota(jnp.int32, (BLOCK, 2 * BLOCK), 1)
     allowed = cols != rows + BLOCK
     for b in range(n_blocks):
-        queries = key_ref[0, BLOCK * (b + 1) : BLOCK * (b + 2), :]
-        keys = key_ref[0, BLOCK * b : BLOCK * (b + 2), :]
+        queries = unit[BLOCK * (b + 1) : BLOCK * (b + 2)]
+        keys = unit[BLOCK * b : BLOCK * (b + 2)]
         values = value_ref[0, BLOCK * b : BLOCK * (b + 2), :]
         scores = lax.dot_general(
             queries, keys, (((1,), (1,)), ((), ())), preferred_element_type=jnp.float32
@@ -44,13 +48,13 @@
         weights = (exp_scores / totals).astype(jnp.bfloat16)
         mixed = jnp.dot(weights, values, preferred_element_type=jnp.float32)
         out_ref[0, BLOCK * b : BLOCK * (b + 1), :] = mixed.astype(out_ref.dtype)
-        total_ref[0, 0, BLOCK * b : BLOCK * (b + 1), :] = totals
-
-
-def block_attention(keys_all, values_all, sharpness, head_dim):
-    n_rounds, span_rows, cols = keys_all.shape
+        total_ref[0, 0, b : b + 1, :] = jnp.transpose(jnp.broadcast_to(totals, (BLOCK, BLOCK)))[0:1]
+
+
+def block_attention(both, sharpness, head_dim):
+    n_rounds, span_rows, cols = both.shape
     rows_here = span_rows - BLOCK
-    heads = cols // head_dim
+    heads = cols // (2 * head_dim)
     n_blocks = rows_here // BLOCK
     flops = n_rounds * heads * n_blocks * 4 * BLOCK * 2 * BLOCK * head_dim
     return pl.pallas_call(
@@ -59,22 +63,22 @@
         in_specs=[
             pl.BlockSpec(memory_space=pltpu.SMEM),
             pl.BlockSpec((1, span_rows, head_dim), lambda r, h: (r, 0, h)),
-            pl.BlockSpec((1, span_rows, head_dim), lambda r, h: (r, 0, h)),
+            pl.BlockSpec((1, span_rows, head_dim), lambda r, h: (r, 0, heads + h)),
         ],
         out_specs=[
             pl.BlockSpec((1, rows_here, head_dim), lambda r, h: (r, 0, h)),
-            pl.BlockSpec((1, 1, rows_here, 1), lambda r, h: (r, h, 0, 0)),
+            pl.BlockSpec((1, 1, n_blocks, BLOCK), lambda r, h: (r, h, 0, 0)),
         ],
         out_shape=[
-            jax.ShapeDtypeStruct((n_rounds, rows_here, cols), jnp.bfloat16),
-            jax.ShapeDtypeStruct((n_rounds, heads, rows_here, 1), jnp.float32),
+            jax.ShapeDtypeStruct((n_rounds, rows_here, heads * head_dim), jnp.bfloat16),
+            jax.ShapeDtypeStruct((n_rounds, heads, n_blocks, BLOCK), jnp.float32),
         ],
         cost_estimate=pl.CostEstimate(
             flops=flops,
             transcendentals=n_rounds * heads * n_blocks * BLOCK * 2 * BLOCK,
-            bytes_accessed=2 * keys_all.size * 2 + n_rounds * rows_here * cols * 2,
+            bytes_accessed=both.size * 2 + n_rounds * rows_here * heads * head_dim * 2,
         ),
-    )(sharpness, keys_all, values_all)
+    )(sharpness, both, both)
 
 
 def rank_within_group(group, order):
@@ -154,16 +158,10 @@
     both = jnp.einsum(
         "rsf,fw->rsw", normed, joined, preferred_element_type=jnp.float32
     ).astype(jnp.bfloat16)
-    spread = both[:, :, :head_cols].reshape(n_rounds, span_rows, heads_here, HEAD_DIM)
-    spread = spread.astype(jnp.float32)
-    unitlength_address_lines = (
-        spread * lax.rsqrt(jnp.sum(spread * spread, axis=-1, keepdims=True) + 1e-06)
-    ).astype(jnp.bfloat16).reshape(n_rounds, span_rows, head_cols)
-    sorted_values = both[:, :, head_cols:]
-    results, block_totals = block_attention(
-        unitlength_address_lines, sorted_values, lane_sharpness, HEAD_DIM
-    )
-    slot_totals = jnp.transpose(block_totals[..., 0], (0, 2, 1))
+    results, block_totals = block_attention(both, lane_sharpness, HEAD_DIM)
+    slot_totals = jnp.transpose(
+        block_totals.reshape(n_rounds, heads_here, rows_here), (0, 2, 1)
+    )
     totals_high = slot_totals.astype(jnp.bfloat16)
     totals_low = (slot_totals - totals_high.astype(jnp.float32)).astype(jnp.bfloat16)
     back_payload = jnp.concatenate([results, totals_high, totals_low], axis=2)

time: 177 us -> 170 us (0.960)
  local copies, waits for them, and re-layouts: 10.5 us -> 4.41 us
  other arithmetic: 6.97 us -> 5.12 us
    squeeze x1 -> x0, local copies, waits for them, and re-layouts: 4.11 us -> none  [shards(): slot_totals = jnp.transpose(block_totals[..., 0], (0, 2, 1))]
    mul x3 -> x0, local copies, waits for them, and re-layouts: 2 us -> none  [the longest x2 1.59 us: shards(): spread * lax.rsqrt(jnp.sum(spread * spread, axis=-1, keepdims=True) + 1e-06)]
where the time goes in v12:
time: 170 us; the launch traced here: 169 us
  blocking collectives  123 us (72%)
  starting transfers between devices  20.2 us (12%)
  matrix products  6.39 us (4%)
  other arithmetic  5.12 us (3%)
  waiting for transfers between devices  5.08 us (3%)
  Pallas kernels  4.83 us (3%)
  local copies, waits for them, and re-layouts  4.41 us (3%)
    all_to_all x1, blocking collectives, shards(): lax.all_to_all(outgoing, 'span', split_axis=0, concat_axis=0, tiled=True)  57.1 us
    all_to_all x1, blocking collectives, shards(): home = lax.all_to_all(back, 'span', split_axis=0, concat_axis=0, tiled=True)  53.6 us
    ppermute x4, starting transfers between devices, shards(): received.append(lax.ppermute(last_slice, ('span', 'head'), route))  16.7 us
    all_to_all x1, blocking collectives, shards(): lax.all_to_all(group_part.reshape(n_groups, rows_here // n_groups, group_...  11.8 us
    ppermute x4, waiting for transfers between devices, shards(): received.append(lax.ppermute(last_slice, ('span', 'head'), route))  5.08 us
    pallas_call x1, Pallas kernels, block_attention(): pl.pallas_call(block_attention_kernel, grid=(n_rounds, heads), in_specs=[...  4.83 us
    all_to_all x1, starting transfers between devices, shards(): lax.all_to_all(copies, 'head', split_axis=0, concat_axis=0, tiled=True)  3.51 us
  transfers between devices with their start and end apart: 5, of which 2 were waited for; matrix products, arithmetic and copies ran while one was open for 0% of the time, Pallas kernels for 0%

profile of v12, /device:TPU:6, one launch (start us, length us, event | category | flops | bytes accessed | tf_op | source)
XLA Modules:
  0.0 168.8 jit_solution(7787285170607704333)
XLA Ops:
  0.0 0.0 copy-start
  0.0 0.7 and_select_fusion.2
  0.8 0.7 and_select_fusion.1
  1.5 0.5 convert_reduce_fusion.1
  1.9 0.8 add_add_fusion
  2.7 0.3 convert_reduce_fusion
  3.0 1.3 fusion.10
  4.2 57.1 %all_to_all.34 = bf16[128,8,256]{2,1,0:T(8,128)(2,1)S(1)} all-to-all(bf16[128,8,256]{2,1,0:T(8,128)(2,1)S(1)} %fusion.10), channel_id=1, replica_groups=mesh['span'=128,'head'=4] {'span'}, dimensions={0} | all-to-all | bytes 1048576 | tf_op jit(solution)/shard_map/all_to_all | solution.py:133
  61.3 0.5 fusion.11
  61.8 1.1 broadcast_in_dim.10
  62.9 3.5 %all-to-all-start.1 = ((bf16[4,2,256,256]{3,2,1,0:T(8,128)(2,1)}), bf16[4,2,256,256]{3,2,1,0:T(8,128)(2,1)S(1)}, u32[]{:S(2)}, u32[]{:S(2)}) async-start(bf16[4,2,256,256]{3,2,1,0:T(8,128)(2,1)} %broadcast_in_dim.10), calls=%async_computation.1 | async-start | bytes 2097152 | tf_op jit(solution)/shard_map/all_to_all | solution.py:140
  66.4 2.2 %collective-permute-start.3 = (bf16[2,128,256]{2,1,0:T(8,128)(2,1)S(1)}, bf16[2,128,256]{2,1,0:T(8,128)(2,1)S(1)}, u32[]{:S(2)}, u32[]{:S(2)}) collective-permute-start(bf16[2,128,256]{2,1,0:T(8,128)(2,1)S(1)} %slice.18), channel_id=1, source_target_pairs={{0,7},{1,4},{2,5},{3,6},{4,11},{5,8},{6,9},{7,10},{8,15},{9,12},{1... | collective-permute-start | bytes 393224 | tf_op jit(solution)/shard_map/ppermute | solution.py:149
  68.6 6.3 %collective-permute-start.2 = (bf16[2,128,256]{2,1,0:T(8,128)(2,1)S(1)}, bf16[2,128,256]{2,1,0:T(8,128)(2,1)S(1)}, u32[]{:S(2)}, u32[]{:S(2)}) collective-permute-start(bf16[2,128,256]{2,1,0:T(8,128)(2,1)S(1)} %slice.18), channel_id=1, source_target_pairs={{0,6},{1,7},{2,4},{3,5},{4,10},{5,11},{6,8},{7,9},{8,14},{9,15},{1... | collective-permute-start | bytes 393224 | tf_op jit(solution)/shard_map/ppermute | solution.py:149
  74.9 2.1 %collective-permute-start.1 = (bf16[2,128,256]{2,1,0:T(8,128)(2,1)S(1)}, bf16[2,128,256]{2,1,0:T(8,128)(2,1)S(1)}, u32[]{:S(2)}, u32[]{:S(2)}) collective-permute-start(bf16[2,128,256]{2,1,0:T(8,128)(2,1)S(1)} %slice.18), channel_id=1, source_target_pairs={{0,5},{1,6},{2,7},{3,4},{4,9},{5,10},{6,11},{7,8},{8,13},{9,14},{1... | collective-permute-start | bytes 393224 | tf_op jit(solution)/shard_map/ppermute | solution.py:149
  77.0 6.1 %collective-permute-start = (bf16[2,128,256]{2,1,0:T(8,128)(2,1)S(1)}, bf16[2,128,256]{2,1,0:T(8,128)(2,1)S(1)}, u32[]{:S(2)}, u32[]{:S(2)}) collective-permute-start(bf16[2,128,256]{2,1,0:T(8,128)(2,1)S(1)} %slice.18), channel_id=1, source_target_pairs={{0,4},{1,5},{2,6},{3,7},{4,8},{5,9},{6,10},{7,11},{8,12},{9,13},{1... | collective-permute-start | bytes 393224 | tf_op jit(solution)/shard_map/ppermute | solution.py:149
  83.2 0.0 collective-permute-done.3
  83.2 0.0 collective-permute-done.2
  83.2 1.6 collective-permute-done.1
  84.8 3.4 %collective-permute-done = bf16[2,128,256]{2,1,0:T(8,128)(2,1)S(1)} collective-permute-done((bf16[2,128,256]{2,1,0:T(8,128)(2,1)S(1)}, bf16[2,128,256]{2,1,0:T(8,128)(2,1)S(1)}, u32[]{:S(2)}, u32[]{:S(2)}) %collective-permute-start) | collective-permute-done | bytes 131104 | tf_op jit(solution)/shard_map/ppermute | solution.py:149
  88.3 0.0 all-to-all-done.1
  88.3 0.1 pad_maximum_fusion.1
  88.4 0.6 gather_fusion
  88.9 0.1 broadcast_select_fusion
  89.1 0.3 copy.34
  89.3 0.5 copy.35
  89.9 0.3 bitcast_reduce_fusion
  90.2 0.4 fusion.3
  90.6 0.0 copy-start.1
  90.6 0.0 copy-start.2
  90.6 0.4 fusion.1
  91.0 0.6 copy-done.1
  91.6 0.2 copy-done.2
  91.8 1.9 %convolution_convert_fusion.shared_ref.value_ref = bf16[2,384,512]{2,1,0:T(8,128)(2,1)} fusion(bf16[2,384,1024]{1,2,0:T(8,128)(2,1)S(1)} %fusion.1, bf16[1024,256]{1,0:T(8,128)(2,1)S(1)} %copy-done.1, bf16[1024,256]{1,0:T(8,128)(2,1)S(1)} %copy-done.2), kind=kOutput, calls=%fused_computation.16 | convolution fusion | flops 807796736 | bytes 3407872 | tf_op jit(solution)/shard_map/rsf,fw->rsw/dot_general | solution.py:158
  93.7 4.8 %shard_map.73 = (bf16[2,256,256]{2,1,0:T(8,128)(2,1)}, f32[2,2,2,128]{3,2,1,0:T(2,128)}) custom-call(f32[2]{0:T(128)} %sharp_ref.1, bf16[2,384,512]{2,1,0:T(8,128)(2,1)} %convolution_convert_fusion.shared_ref.value_ref, bf16[2,384,512]{2,1,0:T(8,128)(2,1)} %convolution_convert_fusion.shared_ref.value_ref), custom_call_target="tpu_custom_call" | custom-call | flops 134217728 | bytes 1048576 | tf_op jit(solution)/shard_map/pallas_call | solution.py:60
  98.5 0.8 copy.44
  99.4 1.7 %fusion.9 = bf16[1024,260]{0,1:T(8,128)(2,1)S(1)} fusion(s32[2,256]{1,0:T(2,128)S(1)} %get-tuple-element.23, bf16[2,256,2]{2,1,0:T(8,128)(2,1)S(1)} %get-tuple-element.19, bf16[2,256,2]{2,1,0:T(8,128)(2,1)S(1)} %get-tuple-element.20, bf16[2,256,256]{2,1,0:T(8,128)(2,1)} %get-tuple-element.17), kind=kOutput, calls=%fused_computation.18 | convolution fusion | flops 274219008 | bytes 800768 | tf_op jit(solution)/shard_map/rsq,rsw->qw/dot_general | solution.py:169
  101.1 0.4 copy.39
  101.5 53.6 %all_to_all.35 = bf16[128,8,260]{2,1,0:T(8,128)(2,1)S(1)} all-to-all(bf16[128,8,260]{2,1,0:T(8,128)(2,1)S(1)} %bitcast.56), channel_id=1, replica_groups=mesh['span'=128,'head'=4] {'span'}, dimensions={0} | all-to-all | bytes 1064960 | tf_op jit(solution)/shard_map/all_to_all | solution.py:172
  155.1 0.7 fusion.6
  155.9 0.0 copy-done
  155.9 0.3 convolution_convert_fusion.1
  156.3 11.8 %all_to_all.36 = bf16[4,64,1024]{2,1,0:T(8,128)(2,1)S(1)} all-to-all(bf16[4,64,1024]{2,1,0:T(8,128)(2,1)S(1)} %bitcast.57), channel_id=1, replica_groups=mesh['span'=128,'head'=4] {'head'}, dimensions={0} | all-to-all | bytes 1048576 | tf_op jit(solution)/shard_map/all_to_all | solution.py:186
  168.1 0.7 reduce_sum.82
  (12 shorter events, 0.2 us)
Async XLA Ops:
  0.0 155.9 %copy-start = (bf16[256,1024]{1,0:T(8,128)(2,1)S(1)}, bf16[256,1024]{1,0:T(8,128)(2,1)}, u32[]{:S(2)}) copy-start(bf16[256,1024]{1,0:T(8,128)(2,1)} %param.10) | copy-start | bytes 1572868
  62.9 25.4 %all-to-all-start.1 = ((bf16[4,2,256,256]{3,2,1,0:T(8,128)(2,1)}), bf16[4,2,256,256]{3,2,1,0:T(8,128)(2,1)S(1)}, u32[]{:S(2)}, u32[]{:S(2)}) async-start(bf16[4,2,256,256]{3,2,1,0:T(8,128)(2,1)} %broadcast_in_dim.10), calls=%async_computation.1 | async-start | bytes 2097152 | tf_op jit(solution)/shard_map/all_to_all | solution.py:140
  66.4 16.7 %collective-permute-start.3 = (bf16[2,128,256]{2,1,0:T(8,128)(2,1)S(1)}, bf16[2,128,256]{2,1,0:T(8,128)(2,1)S(1)}, u32[]{:S(2)}, u32[]{:S(2)}) collective-permute-start(bf16[2,128,256]{2,1,0:T(8,128)(2,1)S(1)} %slice.18), channel_id=1, source_target_pairs={{0,7},{1,4},{2,5},{3,6},{4,11},{5,8},{6,9},{7,10},{8,15},{9,12},{1... | collective-permute-start | bytes 393224 | tf_op jit(solution)/shard_map/ppermute | solution.py:149
  68.6 14.6 %collective-permute-start.2 = (bf16[2,128,256]{2,1,0:T(8,128)(2,1)S(1)}, bf16[2,128,256]{2,1,0:T(8,128)(2,1)S(1)}, u32[]{:S(2)}, u32[]{:S(2)}) collective-permute-start(bf16[2,128,256]{2,1,0:T(8,128)(2,1)S(1)} %slice.18), channel_id=1, source_target_pairs={{0,6},{1,7},{2,4},{3,5},{4,10},{5,11},{6,8},{7,9},{8,14},{9,15},{1... | collective-permute-start | bytes 393224 | tf_op jit(solution)/shard_map/ppermute | solution.py:149
  74.9 10.0 %collective-permute-start.1 = (bf16[2,128,256]{2,1,0:T(8,128)(2,1)S(1)}, bf16[2,128,256]{2,1,0:T(8,128)(2,1)S(1)}, u32[]{:S(2)}, u32[]{:S(2)}) collective-permute-start(bf16[2,128,256]{2,1,0:T(8,128)(2,1)S(1)} %slice.18), channel_id=1, source_target_pairs={{0,5},{1,6},{2,7},{3,4},{4,9},{5,10},{6,11},{7,8},{8,13},{9,14},{1... | collective-permute-start | bytes 393224 | tf_op jit(solution)/shard_map/ppermute | solution.py:149
  77.0 11.2 %collective-permute-start = (bf16[2,128,256]{2,1,0:T(8,128)(2,1)S(1)}, bf16[2,128,256]{2,1,0:T(8,128)(2,1)S(1)}, u32[]{:S(2)}, u32[]{:S(2)}) collective-permute-start(bf16[2,128,256]{2,1,0:T(8,128)(2,1)S(1)} %slice.18), channel_id=1, source_target_pairs={{0,4},{1,5},{2,6},{3,7},{4,8},{5,9},{6,10},{7,11},{8,12},{9,13},{1... | collective-permute-start | bytes 393224 | tf_op jit(solution)/shard_map/ppermute | solution.py:149
  90.6 1.0 copy-start.1
  90.6 1.2 copy-start.2

commit v13 on v12

--- a/solution.py
+++ b/solution.py
@@ -26,29 +26,38 @@
     return (centred * lax.rsqrt(row_var + epsilon)).astype(jnp.bfloat16)
 
 
-def block_attention_kernel(sharp_ref, shared_ref, value_ref, out_ref, total_ref):
-    scale = sharp_ref[pl.program_id(1)]
+def block_attention_kernel(sharp_ref, both_ref, out_ref, total_ref):
+    n_rounds, span_rows, cols = both_ref.shape
+    heads = out_ref.shape[2] // HEAD_DIM
     n_blocks = out_ref.shape[1] // BLOCK
-    spread = shared_ref[0].astype(jnp.float32)
-    unit = (
-        spread * lax.rsqrt(jnp.sum(spread * spread, axis=1, keepdims=True) + 1e-06)
-    ).astype(jnp.bfloat16)
     rows = lax.broadcasted_iota(jnp.int32, (BLOCK, 2 * BLOCK), 0)
-    cols = lax.broadcasted_iota(jnp.int32, (BLOCK, 2 * BLOCK), 1)
-    allowed = cols != rows + BLOCK
-    for b in range(n_blocks):
-        queries = unit[BLOCK * (b + 1) : BLOCK * (b + 2)]
-        keys = unit[BLOCK * b : BLOCK * (b + 2)]
-        values = value_ref[0, BLOCK * b : BLOCK * (b + 2), :]
-        scores = lax.dot_general(
-            queries, keys, (((1,), (1,)), ((), ())), preferred_element_type=jnp.float32
-        ) * scale
-        exp_scores = jnp.where(allowed, jnp.exp(scores), 0.0)
-        totals = jnp.sum(exp_scores, axis=1, keepdims=True)
-        weights = (exp_scores / totals).astype(jnp.bfloat16)
-        mixed = jnp.dot(weights, values, preferred_element_type=jnp.float32)
-        out_ref[0, BLOCK * b : BLOCK * (b + 1), :] = mixed.astype(out_ref.dtype)
-        total_ref[0, 0, b : b + 1, :] = jnp.transpose(jnp.broadcast_to(totals, (BLOCK, BLOCK)))[0:1]
+    key_cols = lax.broadcasted_iota(jnp.int32, (BLOCK, 2 * BLOCK), 1)
+    allowed = key_cols != rows + BLOCK
+    for r in range(n_rounds):
+        for h in range(heads):
+            scale = sharp_ref[h]
+            spread = both_ref[r, :, HEAD_DIM * h : HEAD_DIM * (h + 1)].astype(jnp.float32)
+            unit = (
+                spread * lax.rsqrt(jnp.sum(spread * spread, axis=1, keepdims=True) + 1e-06)
+            ).astype(jnp.bfloat16)
+            value_col = HEAD_DIM * (heads + h)
+            for b in range(n_blocks):
+                queries = unit[BLOCK * (b + 1) : BLOCK * (b + 2)]
+                keys = unit[BLOCK * b : BLOCK * (b + 2)]
+                values = both_ref[r, BLOCK * b : BLOCK * (b + 2), value_col : value_col + HEAD_DIM]
+                scores = lax.dot_general(
+                    queries, keys, (((1,), (1,)), ((), ())), preferred_element_type=jnp.float32
+                ) * scale
+                exp_scores = jnp.where(allowed, jnp.exp(scores), 0.0)
+                totals = jnp.sum(exp_scores, axis=1, keepdims=True)
+                weights = (exp_scores / totals).astype(jnp.bfloat16)
+                mixed = jnp.dot(weights, values, preferred_element_type=jnp.float32)
+                out_ref[r, BLOCK * b : BLOCK * (b + 1), HEAD_DIM * h : HEAD_DIM * (h + 1)] = (
+                    mixed.astype(out_ref.dtype)
+                )
+                total_ref[r, h, b : b + 1, :] = jnp.transpose(
+                    jnp.broadcast_to(totals, (BLOCK, BLOCK))
+                )[0:1]
 
 
 def block_attention(both, sharpness, head_dim):
@@ -59,15 +68,13 @@
     flops = n_rounds * heads * n_blocks * 4 * BLOCK * 2 * BLOCK * head_dim
     return pl.pallas_call(
         block_attention_kernel,
-        grid=(n_rounds, heads),
         in_specs=[
             pl.BlockSpec(memory_space=pltpu.SMEM),
-            pl.BlockSpec((1, span_rows, head_dim), lambda r, h: (r, 0, h)),
-            pl.BlockSpec((1, span_rows, head_dim), lambda r, h: (r, 0, heads + h)),
+            pl.BlockSpec(memory_space=pltpu.VMEM),
         ],
         out_specs=[
-            pl.BlockSpec((1, rows_here, head_dim), lambda r, h: (r, 0, h)),
-            pl.BlockSpec((1, 1, n_blocks, BLOCK), lambda r, h: (r, h, 0, 0)),
+            pl.BlockSpec(memory_space=pltpu.VMEM),
+            pl.BlockSpec(memory_space=pltpu.VMEM),
         ],
         out_shape=[
             jax.ShapeDtypeStruct((n_rounds, rows_here, heads * head_dim), jnp.bfloat16),
@@ -78,7 +85,7 @@
             transcendentals=n_rounds * heads * n_blocks * BLOCK * 2 * BLOCK,
             bytes_accessed=both.size * 2 + n_rounds * rows_here * heads * head_dim * 2,
         ),
-    )(sharpness, both, both)
+    )(sharpness, both)
 
 
 def rank_within_group(group, order):

time: 170 us -> 168 us (0.988)
  Pallas kernels: 4.83 us -> 2.87 us
    pallas_call x1, Pallas kernels: 4.83 us -> 2.87 us  [block_attention(): pl.pallas_call(block_attention_kernel, in_specs=[pl.BlockSpec(memory_spac...]
where the time goes in v13:
time: 168 us; the launch traced here: 167 us
  blocking collectives  123 us (73%)
  starting transfers between devices  20.2 us (12%)
  matrix products  6.41 us (4%)
  other arithmetic  5.12 us (3%)
  waiting for transfers between devices  5.08 us (3%)
  local copies, waits for them, and re-layouts  4.41 us (3%)
  Pallas kernels  2.87 us (2%)
    all_to_all x1, blocking collectives, shards(): lax.all_to_all(outgoing, 'span', split_axis=0, concat_axis=0, tiled=True)  57.1 us
    all_to_all x1, blocking collectives, shards(): home = lax.all_to_all(back, 'span', split_axis=0, concat_axis=0, tiled=True)  53.6 us
    ppermute x4, starting transfers between devices, shards(): received.append(lax.ppermute(last_slice, ('span', 'head'), route))  16.7 us
    all_to_all x1, blocking collectives, shards(): lax.all_to_all(group_part.reshape(n_groups, rows_here // n_groups, group_...  11.8 us
    ppermute x4, waiting for transfers between devices, shards(): received.append(lax.ppermute(last_slice, ('span', 'head'), route))  5.08 us
    all_to_all x1, starting transfers between devices, shards(): lax.all_to_all(copies, 'head', split_axis=0, concat_axis=0, tiled=True)  3.51 us
  transfers between devices with their start and end apart: 5, of which 2 were waited for; matrix products, arithmetic and copies ran while one was open for 0% of the time, Pallas kernels for 0%

profile of v13, /device:TPU:6, one launch (start us, length us, event | category | flops | bytes accessed | tf_op | source)
XLA Modules:
  0.0 166.9 jit_solution(188929015846819562)
XLA Ops:
  0.0 0.0 copy-start
  0.0 0.7 and_select_fusion.2
  0.8 0.7 and_select_fusion.1
  1.5 0.5 convert_reduce_fusion.1
  1.9 0.8 add_add_fusion
  2.7 0.3 convert_reduce_fusion
  3.0 1.3 fusion.10
  4.2 57.1 %all_to_all.34 = bf16[128,8,256]{2,1,0:T(8,128)(2,1)S(1)} all-to-all(bf16[128,8,256]{2,1,0:T(8,128)(2,1)S(1)} %fusion.10), channel_id=1, replica_groups=mesh['span'=128,'head'=4] {'span'}, dimensions={0} | all-to-all | bytes 1048576 | tf_op jit(solution)/shard_map/all_to_all | solution.py:140
  61.3 0.5 fusion.11
  61.8 1.1 broadcast_in_dim.10
  62.9 3.5 %all-to-all-start.1 = ((bf16[4,2,256,256]{3,2,1,0:T(8,128)(2,1)}), bf16[4,2,256,256]{3,2,1,0:T(8,128)(2,1)S(1)}, u32[]{:S(2)}, u32[]{:S(2)}) async-start(bf16[4,2,256,256]{3,2,1,0:T(8,128)(2,1)} %broadcast_in_dim.10), calls=%async_computation.1 | async-start | bytes 2097152 | tf_op jit(solution)/shard_map/all_to_all | solution.py:147
  66.4 2.2 %collective-permute-start.3 = (bf16[2,128,256]{2,1,0:T(8,128)(2,1)S(1)}, bf16[2,128,256]{2,1,0:T(8,128)(2,1)S(1)}, u32[]{:S(2)}, u32[]{:S(2)}) collective-permute-start(bf16[2,128,256]{2,1,0:T(8,128)(2,1)S(1)} %slice.18), channel_id=1, source_target_pairs={{0,7},{1,4},{2,5},{3,6},{4,11},{5,8},{6,9},{7,10},{8,15},{9,12},{1... | collective-permute-start | bytes 393224 | tf_op jit(solution)/shard_map/ppermute | solution.py:156
  68.6 6.3 %collective-permute-start.2 = (bf16[2,128,256]{2,1,0:T(8,128)(2,1)S(1)}, bf16[2,128,256]{2,1,0:T(8,128)(2,1)S(1)}, u32[]{:S(2)}, u32[]{:S(2)}) collective-permute-start(bf16[2,128,256]{2,1,0:T(8,128)(2,1)S(1)} %slice.18), channel_id=1, source_target_pairs={{0,6},{1,7},{2,4},{3,5},{4,10},{5,11},{6,8},{7,9},{8,14},{9,15},{1... | collective-permute-start | bytes 393224 | tf_op jit(solution)/shard_map/ppermute | solution.py:156
  74.9 2.1 %collective-permute-start.1 = (bf16[2,128,256]{2,1,0:T(8,128)(2,1)S(1)}, bf16[2,128,256]{2,1,0:T(8,128)(2,1)S(1)}, u32[]{:S(2)}, u32[]{:S(2)}) collective-permute-start(bf16[2,128,256]{2,1,0:T(8,128)(2,1)S(1)} %slice.18), channel_id=1, source_target_pairs={{0,5},{1,6},{2,7},{3,4},{4,9},{5,10},{6,11},{7,8},{8,13},{9,14},{1... | collective-permute-start | bytes 393224 | tf_op jit(solution)/shard_map/ppermute | solution.py:156
  77.0 6.1 %collective-permute-start = (bf16[2,128,256]{2,1,0:T(8,128)(2,1)S(1)}, bf16[2,128,256]{2,1,0:T(8,128)(2,1)S(1)}, u32[]{:S(2)}, u32[]{:S(2)}) collective-permute-start(bf16[2,128,256]{2,1,0:T(8,128)(2,1)S(1)} %slice.18), channel_id=1, source_target_pairs={{0,4},{1,5},{2,6},{3,7},{4,8},{5,9},{6,10},{7,11},{8,12},{9,13},{1... | collective-permute-start | bytes 393224 | tf_op jit(solution)/shard_map/ppermute | solution.py:156
  83.2 0.0 collective-permute-done.3
  83.2 0.0 collective-permute-done.2
  83.2 1.6 collective-permute-done.1
  84.8 3.4 %collective-permute-done = bf16[2,128,256]{2,1,0:T(8,128)(2,1)S(1)} collective-permute-done((bf16[2,128,256]{2,1,0:T(8,128)(2,1)S(1)}, bf16[2,128,256]{2,1,0:T(8,128)(2,1)S(1)}, u32[]{:S(2)}, u32[]{:S(2)}) %collective-permute-start) | collective-permute-done | bytes 131104 | tf_op jit(solution)/shard_map/ppermute | solution.py:156
  88.3 0.0 all-to-all-done.1
  88.3 0.1 pad_maximum_fusion.1
  88.4 0.6 gather_fusion
  88.9 0.1 broadcast_select_fusion
  89.1 0.3 copy.34
  89.3 0.5 copy.35
  89.9 0.3 bitcast_reduce_fusion
  90.2 0.4 fusion.3
  90.6 0.0 copy-start.1
  90.6 0.0 copy-start.2
  90.6 0.4 fusion.1
  91.0 0.6 copy-done.1
  91.6 0.2 copy-done.2
  91.8 1.9 %convolution_convert_fusion.both_ref = bf16[2,384,512]{2,1,0:T(8,128)(2,1)} fusion(bf16[2,384,1024]{1,2,0:T(8,128)(2,1)S(1)} %fusion.1, bf16[1024,256]{1,0:T(8,128)(2,1)S(1)} %copy-done.1, bf16[1024,256]{1,0:T(8,128)(2,1)S(1)} %copy-done.2), kind=kOutput, calls=%fused_computation.16 | convolution fusion | flops 807796736 | bytes 3407872 | tf_op jit(solution)/shard_map/rsf,fw->rsw/dot_general | solution.py:165
  93.7 2.9 %shard_map.73 = (bf16[2,256,256]{2,1,0:T(8,128)(2,1)}, f32[2,2,2,128]{3,2,1,0:T(2,128)}) custom-call(f32[2]{0:T(128)} %sharp_ref.1, bf16[2,384,512]{2,1,0:T(8,128)(2,1)} %convolution_convert_fusion.both_ref), custom_call_target="tpu_custom_call" | custom-call | flops 134217728 | bytes 1048576 | tf_op jit(solution)/shard_map/pallas_call | solution.py:69
  96.6 0.8 copy.44
  97.5 1.7 %fusion.9 = bf16[1024,260]{0,1:T(8,128)(2,1)S(1)} fusion(s32[2,256]{1,0:T(2,128)S(1)} %get-tuple-element.23, bf16[2,256,2]{2,1,0:T(8,128)(2,1)S(1)} %get-tuple-element.19, bf16[2,256,2]{2,1,0:T(8,128)(2,1)S(1)} %get-tuple-element.20, bf16[2,256,256]{2,1,0:T(8,128)(2,1)} %get-tuple-element.17), kind=kOutput, calls=%fused_computation.18 | convolution fusion | flops 274219008 | bytes 800768 | tf_op jit(solution)/shard_map/rsq,rsw->qw/dot_general | solution.py:176
  99.2 0.4 copy.39
  99.6 53.6 %all_to_all.35 = bf16[128,8,260]{2,1,0:T(8,128)(2,1)S(1)} all-to-all(bf16[128,8,260]{2,1,0:T(8,128)(2,1)S(1)} %bitcast.56), channel_id=1, replica_groups=mesh['span'=128,'head'=4] {'span'}, dimensions={0} | all-to-all | bytes 1064960 | tf_op jit(solution)/shard_map/all_to_all | solution.py:179
  153.2 0.7 fusion.6
  154.0 0.0 copy-done
  154.0 0.3 convolution_convert_fusion.1
  154.3 11.8 %all_to_all.36 = bf16[4,64,1024]{2,1,0:T(8,128)(2,1)S(1)} all-to-all(bf16[4,64,1024]{2,1,0:T(8,128)(2,1)S(1)} %bitcast.57), channel_id=1, replica_groups=mesh['span'=128,'head'=4] {'head'}, dimensions={0} | all-to-all | bytes 1048576 | tf_op jit(solution)/shard_map/all_to_all | solution.py:193
  166.1 0.7 reduce_sum.82
  (12 shorter events, 0.2 us)
Async XLA Ops:
  0.0 154.0 %copy-start = (bf16[256,1024]{1,0:T(8,128)(2,1)S(1)}, bf16[256,1024]{1,0:T(8,128)(2,1)}, u32[]{:S(2)}) copy-start(bf16[256,1024]{1,0:T(8,128)(2,1)} %param.10) | copy-start | bytes 1572868
  62.9 25.4 %all-to-all-start.1 = ((bf16[4,2,256,256]{3,2,1,0:T(8,128)(2,1)}), bf16[4,2,256,256]{3,2,1,0:T(8,128)(2,1)S(1)}, u32[]{:S(2)}, u32[]{:S(2)}) async-start(bf16[4,2,256,256]{3,2,1,0:T(8,128)(2,1)} %broadcast_in_dim.10), calls=%async_computation.1 | async-start | bytes 2097152 | tf_op jit(solution)/shard_map/all_to_all | solution.py:147
  66.4 16.7 %collective-permute-start.3 = (bf16[2,128,256]{2,1,0:T(8,128)(2,1)S(1)}, bf16[2,128,256]{2,1,0:T(8,128)(2,1)S(1)}, u32[]{:S(2)}, u32[]{:S(2)}) collective-permute-start(bf16[2,128,256]{2,1,0:T(8,128)(2,1)S(1)} %slice.18), channel_id=1, source_target_pairs={{0,7},{1,4},{2,5},{3,6},{4,11},{5,8},{6,9},{7,10},{8,15},{9,12},{1... | collective-permute-start | bytes 393224 | tf_op jit(solution)/shard_map/ppermute | solution.py:156
  68.6 14.6 %collective-permute-start.2 = (bf16[2,128,256]{2,1,0:T(8,128)(2,1)S(1)}, bf16[2,128,256]{2,1,0:T(8,128)(2,1)S(1)}, u32[]{:S(2)}, u32[]{:S(2)}) collective-permute-start(bf16[2,128,256]{2,1,0:T(8,128)(2,1)S(1)} %slice.18), channel_id=1, source_target_pairs={{0,6},{1,7},{2,4},{3,5},{4,10},{5,11},{6,8},{7,9},{8,14},{9,15},{1... | collective-permute-start | bytes 393224 | tf_op jit(solution)/shard_map/ppermute | solution.py:156
  74.9 10.0 %collective-permute-start.1 = (bf16[2,128,256]{2,1,0:T(8,128)(2,1)S(1)}, bf16[2,128,256]{2,1,0:T(8,128)(2,1)S(1)}, u32[]{:S(2)}, u32[]{:S(2)}) collective-permute-start(bf16[2,128,256]{2,1,0:T(8,128)(2,1)S(1)} %slice.18), channel_id=1, source_target_pairs={{0,5},{1,6},{2,7},{3,4},{4,9},{5,10},{6,11},{7,8},{8,13},{9,14},{1... | collective-permute-start | bytes 393224 | tf_op jit(solution)/shard_map/ppermute | solution.py:156
  77.0 11.2 %collective-permute-start = (bf16[2,128,256]{2,1,0:T(8,128)(2,1)S(1)}, bf16[2,128,256]{2,1,0:T(8,128)(2,1)S(1)}, u32[]{:S(2)}, u32[]{:S(2)}) collective-permute-start(bf16[2,128,256]{2,1,0:T(8,128)(2,1)S(1)} %slice.18), channel_id=1, source_target_pairs={{0,4},{1,5},{2,6},{3,7},{4,8},{5,9},{6,10},{7,11},{8,12},{9,13},{1... | collective-permute-start | bytes 393224 | tf_op jit(solution)/shard_map/ppermute | solution.py:156
  90.6 1.0 copy-start.1
  90.6 1.2 copy-start.2

commit v14 on v13

--- a/solution.py
+++ b/solution.py
@@ -26,25 +26,45 @@
     return (centred * lax.rsqrt(row_var + epsilon)).astype(jnp.bfloat16)
 
 
-def block_attention_kernel(sharp_ref, both_ref, out_ref, total_ref):
-    n_rounds, span_rows, cols = both_ref.shape
+def block_attention_kernel(
+    sharp_ref, slices_ref, shared_proj_ref, value_proj_ref, out_ref, total_ref
+):
+    n_groups, n_rounds, span_rows, group_cols = slices_ref.shape
     heads = out_ref.shape[2] // HEAD_DIM
     n_blocks = out_ref.shape[1] // BLOCK
+    features = n_groups * group_cols
     rows = lax.broadcasted_iota(jnp.int32, (BLOCK, 2 * BLOCK), 0)
     key_cols = lax.broadcasted_iota(jnp.int32, (BLOCK, 2 * BLOCK), 1)
     allowed = key_cols != rows + BLOCK
     for r in range(n_rounds):
+        parts = [slices_ref[g, r].astype(jnp.float32) for g in range(n_groups)]
+        row_mean = sum(jnp.sum(p, axis=1, keepdims=True) for p in parts) / features
+        centred = [p - row_mean for p in parts]
+        row_var = sum(jnp.sum(c * c, axis=1, keepdims=True) for c in centred) / features
+        inv = lax.rsqrt(row_var + epsilon)
+        normed = [(c * inv).astype(jnp.bfloat16) for c in centred]
+        projected = []
+        for proj_ref in (shared_proj_ref, value_proj_ref):
+            acc = None
+            for g in range(n_groups):
+                term = jnp.dot(
+                    normed[g],
+                    proj_ref[group_cols * g : group_cols * (g + 1), :],
+                    preferred_element_type=jnp.float32,
+                )
+                acc = term if acc is None else acc + term
+            projected.append(acc.astype(jnp.bfloat16))
+        shared, values_all = projected
         for h in range(heads):
             scale = sharp_ref[h]
-            spread = both_ref[r, :, HEAD_DIM * h : HEAD_DIM * (h + 1)].astype(jnp.float32)
+            spread = shared[:, HEAD_DIM * h : HEAD_DIM * (h + 1)].astype(jnp.float32)
             unit = (
                 spread * lax.rsqrt(jnp.sum(spread * spread, axis=1, keepdims=True) + 1e-06)
             ).astype(jnp.bfloat16)
-            value_col = HEAD_DIM * (heads + h)
             for b in range(n_blocks):
                 queries = unit[BLOCK * (b + 1) : BLOCK * (b + 2)]
                 keys = unit[BLOCK * b : BLOCK * (b + 2)]
-                values = both_ref[r, BLOCK * b : BLOCK * (b + 2), value_col : value_col + HEAD_DIM]
+                values = values_all[BLOCK * b : BLOCK * (b + 2), HEAD_DIM * h : HEAD_DIM * (h + 1)]
                 scores = lax.dot_general(
                     queries, keys, (((1,), (1,)), ((), ())), preferred_element_type=jnp.float32
                 ) * scale
@@ -60,32 +80,29 @@
                 )[0:1]
 
 
-def block_attention(both, sharpness, head_dim):
-    n_rounds, span_rows, cols = both.shape
+def block_attention(slices, shared_proj, value_proj, sharpness):
+    n_groups, n_rounds, span_rows, group_cols = slices.shape
     rows_here = span_rows - BLOCK
-    heads = cols // (2 * head_dim)
+    cols = shared_proj.shape[1]
+    heads = cols // HEAD_DIM
     n_blocks = rows_here // BLOCK
-    flops = n_rounds * heads * n_blocks * 4 * BLOCK * 2 * BLOCK * head_dim
+    flops = n_rounds * heads * n_blocks * 4 * BLOCK * 2 * BLOCK * HEAD_DIM
+    flops += n_rounds * span_rows * n_groups * group_cols * 2 * cols * 2
+    vmem = pl.BlockSpec(memory_space=pltpu.VMEM)
     return pl.pallas_call(
         block_attention_kernel,
-        in_specs=[
-            pl.BlockSpec(memory_space=pltpu.SMEM),
-            pl.BlockSpec(memory_space=pltpu.VMEM),
-        ],
-        out_specs=[
-            pl.BlockSpec(memory_space=pltpu.VMEM),
-            pl.BlockSpec(memory_space=pltpu.VMEM),
-        ],
+        in_specs=[pl.BlockSpec(memory_space=pltpu.SMEM), vmem, vmem, vmem],
+        out_specs=[vmem, vmem],
         out_shape=[
-            jax.ShapeDtypeStruct((n_rounds, rows_here, heads * head_dim), jnp.bfloat16),
+            jax.ShapeDtypeStruct((n_rounds, rows_here, cols), jnp.bfloat16),
             jax.ShapeDtypeStruct((n_rounds, heads, n_blocks, BLOCK), jnp.float32),
         ],
         cost_estimate=pl.CostEstimate(
             flops=flops,
             transcendentals=n_rounds * heads * n_blocks * BLOCK * 2 * BLOCK,
-            bytes_accessed=both.size * 2 + n_rounds * rows_here * heads * head_dim * 2,
+            bytes_accessed=slices.size * 2 + 4 * shared_proj.size + n_rounds * rows_here * cols * 2,
         ),
-    )(sharpness, both)
+    )(sharpness, slices, shared_proj, value_proj)
 
 
 def rank_within_group(group, order):
@@ -142,7 +159,6 @@
         "rsq,qf->rsf", recv_hot, incoming, preferred_element_type=jnp.float32
     ).astype(jnp.bfloat16)
     n_groups = lax.axis_size("head")
-    joined = jnp.concatenate([common_lookup_projector, content_projector], axis=1)
     copies = jnp.broadcast_to(arrived[None], (n_groups,) + arrived.shape)
     gathered = lax.all_to_all(copies, "head", split_axis=0, concat_axis=0, tiled=True)
     last_slice = arrived[:, rows_here - BLOCK :]
@@ -159,13 +175,9 @@
     slice_order = (group_here - jnp.arange(n_groups, dtype=jnp.int32)) % n_groups
     prior_slices = jnp.take(jnp.stack(received), slice_order, axis=0)
     all_slices = jnp.concatenate([prior_slices, gathered], axis=2)
-    span_rows = rows_here + BLOCK
-    full_rows = jnp.moveaxis(all_slices, 0, 2).reshape(n_rounds, span_rows, -1)
-    normed = layer_norm(full_rows)
-    both = jnp.einsum(
-        "rsf,fw->rsw", normed, joined, preferred_element_type=jnp.float32
-    ).astype(jnp.bfloat16)
-    results, block_totals = block_attention(both, lane_sharpness, HEAD_DIM)
+    results, block_totals = block_attention(
+        all_slices, common_lookup_projector, content_projector, lane_sharpness
+    )
     slot_totals = jnp.transpose(
         block_totals.reshape(n_rounds, heads_here, rows_here), (0, 2, 1)
     )

time: 168 us -> 166 us (0.988)
  matrix products: 6.41 us -> 4.5 us
  Pallas kernels: 2.87 us -> 4.74 us
    dot_general x1 -> x0, matrix products: 1.9 us -> none  [shards(): jnp.einsum('rsf,fw->rsw', normed, joined, preferred_element_type=jnp.floa...]
    pallas_call x1, Pallas kernels: 2.87 us -> 4.74 us  [block_attention(): pl.pallas_call(block_attention_kernel, in_specs=[pl.BlockSpec(memory_spac...]
where the time goes in v14:
time: 166 us; the launch traced here: 165 us
  blocking collectives  123 us (74%)
  starting transfers between devices  20.2 us (12%)
  other arithmetic  5.26 us (3%)
  waiting for transfers between devices  5.08 us (3%)
  Pallas kernels  4.74 us (3%)
  matrix products  4.5 us (3%)
  local copies, waits for them, and re-layouts  2.83 us (2%)
    all_to_all x1, blocking collectives, shards(): lax.all_to_all(outgoing, 'span', split_axis=0, concat_axis=0, tiled=True)  57.1 us
    all_to_all x1, blocking collectives, shards(): home = lax.all_to_all(back, 'span', split_axis=0, concat_axis=0, tiled=True)  53.6 us
    ppermute x4, starting transfers between devices, shards(): received.append(lax.ppermute(last_slice, ('span', 'head'), route))  16.7 us
    all_to_all x1, blocking collectives, shards(): lax.all_to_all(group_part.reshape(n_groups, rows_here // n_groups, group_...  11.8 us
    ppermute x4, waiting for transfers between devices, shards(): received.append(lax.ppermute(last_slice, ('span', 'head'), route))  5.08 us
    pallas_call x1, Pallas kernels, block_attention(): pl.pallas_call(block_attention_kernel, in_specs=[pl.BlockSpec(memory_spac...  4.74 us
    all_to_all x1, starting transfers between devices, shards(): lax.all_to_all(copies, 'head', split_axis=0, concat_axis=0, tiled=True)  3.51 us
  transfers between devices with their start and end apart: 5, of which 2 were waited for; matrix products, arithmetic and copies ran while one was open for 0% of the time, Pallas kernels for 0%

profile of v14, /device:TPU:6, one launch (start us, length us, event | category | flops | bytes accessed | tf_op | source)
XLA Modules:
  0.0 165.3 jit_solution(341245346744343725)
XLA Ops:
  0.0 0.0 copy-start
  0.0 0.7 and_select_fusion.2
  0.8 0.7 and_select_fusion.1
  1.5 0.5 convert_reduce_fusion.1
  1.9 0.8 add_add_fusion
  2.7 0.3 convert_reduce_fusion
  3.0 1.3 fusion.6
  4.2 57.1 %all_to_all.34 = bf16[128,8,256]{2,1,0:T(8,128)(2,1)S(1)} all-to-all(bf16[128,8,256]{2,1,0:T(8,128)(2,1)S(1)} %fusion.6), channel_id=1, replica_groups=mesh['span'=128,'head'=4] {'span'}, dimensions={0} | all-to-all | bytes 1048576 | tf_op jit(solution)/shard_map/all_to_all | solution.py:157
  61.3 0.5 fusion.7
  61.8 1.1 broadcast_in_dim.10
  62.9 3.5 %all-to-all-start.1 = ((bf16[4,2,256,256]{3,2,1,0:T(8,128)(2,1)}), bf16[4,2,256,256]{3,2,1,0:T(8,128)(2,1)S(1)}, u32[]{:S(2)}, u32[]{:S(2)}) async-start(bf16[4,2,256,256]{3,2,1,0:T(8,128)(2,1)} %broadcast_in_dim.10), calls=%async_computation.1 | async-start | bytes 2097152 | tf_op jit(solution)/shard_map/all_to_all | solution.py:163
  66.4 2.2 %collective-permute-start.3 = (bf16[2,128,256]{2,1,0:T(8,128)(2,1)S(1)}, bf16[2,128,256]{2,1,0:T(8,128)(2,1)S(1)}, u32[]{:S(2)}, u32[]{:S(2)}) collective-permute-start(bf16[2,128,256]{2,1,0:T(8,128)(2,1)S(1)} %slice.18), channel_id=1, source_target_pairs={{0,7},{1,4},{2,5},{3,6},{4,11},{5,8},{6,9},{7,10},{8,15},{9,12},{1... | collective-permute-start | bytes 393224 | tf_op jit(solution)/shard_map/ppermute | solution.py:172
  68.6 6.3 %collective-permute-start.2 = (bf16[2,128,256]{2,1,0:T(8,128)(2,1)S(1)}, bf16[2,128,256]{2,1,0:T(8,128)(2,1)S(1)}, u32[]{:S(2)}, u32[]{:S(2)}) collective-permute-start(bf16[2,128,256]{2,1,0:T(8,128)(2,1)S(1)} %slice.18), channel_id=1, source_target_pairs={{0,6},{1,7},{2,4},{3,5},{4,10},{5,11},{6,8},{7,9},{8,14},{9,15},{1... | collective-permute-start | bytes 393224 | tf_op jit(solution)/shard_map/ppermute | solution.py:172
  74.9 2.1 %collective-permute-start.1 = (bf16[2,128,256]{2,1,0:T(8,128)(2,1)S(1)}, bf16[2,128,256]{2,1,0:T(8,128)(2,1)S(1)}, u32[]{:S(2)}, u32[]{:S(2)}) collective-permute-start(bf16[2,128,256]{2,1,0:T(8,128)(2,1)S(1)} %slice.18), channel_id=1, source_target_pairs={{0,5},{1,6},{2,7},{3,4},{4,9},{5,10},{6,11},{7,8},{8,13},{9,14},{1... | collective-permute-start | bytes 393224 | tf_op jit(solution)/shard_map/ppermute | solution.py:172
  77.0 6.1 %collective-permute-start = (bf16[2,128,256]{2,1,0:T(8,128)(2,1)S(1)}, bf16[2,128,256]{2,1,0:T(8,128)(2,1)S(1)}, u32[]{:S(2)}, u32[]{:S(2)}) collective-permute-start(bf16[2,128,256]{2,1,0:T(8,128)(2,1)S(1)} %slice.18), channel_id=1, source_target_pairs={{0,4},{1,5},{2,6},{3,7},{4,8},{5,9},{6,10},{7,11},{8,12},{9,13},{1... | collective-permute-start | bytes 393224 | tf_op jit(solution)/shard_map/ppermute | solution.py:172
  83.2 0.0 collective-permute-done.3
  83.2 0.0 collective-permute-done.2
  83.2 1.6 collective-permute-done.1
  84.8 3.4 %collective-permute-done = bf16[2,128,256]{2,1,0:T(8,128)(2,1)S(1)} collective-permute-done((bf16[2,128,256]{2,1,0:T(8,128)(2,1)S(1)}, bf16[2,128,256]{2,1,0:T(8,128)(2,1)S(1)}, u32[]{:S(2)}, u32[]{:S(2)}) %collective-permute-start) | collective-permute-done | bytes 131104 | tf_op jit(solution)/shard_map/ppermute | solution.py:172
  88.3 0.0 all-to-all-done.1
  88.3 0.1 pad_maximum_fusion.1
  88.4 0.6 gather_fusion
  88.9 0.1 broadcast_select_fusion
  89.1 1.3 pad_maximum_fusion.slices_ref
  90.3 4.7 %shard_map.73 = (bf16[2,256,256]{2,1,0:T(8,128)(2,1)}, f32[2,2,2,128]{3,2,1,0:T(2,128)}) custom-call(f32[2]{0:T(128)} %sharp_ref.1, bf16[4,2,384,256]{3,2,1,0:T(8,128)(2,1)} %pad_maximum_fusion.slices_ref, bf16[1024,256]{1,0:T(8,128)(2,1)} %shared_proj_ref.1, bf16[1024,256]{1,0:T(8,128)(2,1)} %value_proj_ref.1), custom_call_target="tpu_custom_call" | custom-call | flops 939524096 | bytes 2883584 | tf_op jit(solution)/shard_map/pallas_call | solution.py:92
  95.1 0.8 copy.28
  95.9 1.7 %fusion.5 = bf16[1024,260]{0,1:T(8,128)(2,1)S(1)} fusion(s32[2,256]{1,0:T(2,128)S(1)} %get-tuple-element.23, bf16[2,256,2]{2,1,0:T(8,128)(2,1)S(1)} %get-tuple-element.19, bf16[2,256,2]{2,1,0:T(8,128)(2,1)S(1)} %get-tuple-element.20, bf16[2,256,256]{2,1,0:T(8,128)(2,1)} %get-tuple-element.17), kind=kOutput, calls=%fused_computation.10 | convolution fusion | flops 274219008 | bytes 800768 | tf_op jit(solution)/shard_map/rsq,rsw->qw/dot_general | solution.py:188
  97.7 0.4 copy.24
  98.0 53.6 %all_to_all.35 = bf16[128,8,260]{2,1,0:T(8,128)(2,1)S(1)} all-to-all(bf16[128,8,260]{2,1,0:T(8,128)(2,1)S(1)} %bitcast.38), channel_id=1, replica_groups=mesh['span'=128,'head'=4] {'span'}, dimensions={0} | all-to-all | bytes 1064960 | tf_op jit(solution)/shard_map/all_to_all | solution.py:191
  151.6 0.7 fusion.2
  152.4 0.0 copy-done
  152.4 0.3 convolution_convert_fusion
  152.8 11.8 %all_to_all.36 = bf16[4,64,1024]{2,1,0:T(8,128)(2,1)S(1)} all-to-all(bf16[4,64,1024]{2,1,0:T(8,128)(2,1)S(1)} %bitcast.39), channel_id=1, replica_groups=mesh['span'=128,'head'=4] {'head'}, dimensions={0} | all-to-all | bytes 1048576 | tf_op jit(solution)/shard_map/all_to_all | solution.py:205
  164.6 0.7 reduce_sum.62
  (10 shorter events, 0.2 us)
Async XLA Ops:
  0.0 152.4 %copy-start = (bf16[256,1024]{1,0:T(8,128)(2,1)S(1)}, bf16[256,1024]{1,0:T(8,128)(2,1)}, u32[]{:S(2)}) copy-start(bf16[256,1024]{1,0:T(8,128)(2,1)} %param.10) | copy-start | bytes 1572868
  62.9 25.4 %all-to-all-start.1 = ((bf16[4,2,256,256]{3,2,1,0:T(8,128)(2,1)}), bf16[4,2,256,256]{3,2,1,0:T(8,128)(2,1)S(1)}, u32[]{:S(2)}, u32[]{:S(2)}) async-start(bf16[4,2,256,256]{3,2,1,0:T(8,128)(2,1)} %broadcast_in_dim.10), calls=%async_computation.1 | async-start | bytes 2097152 | tf_op jit(solution)/shard_map/all_to_all | solution.py:163
  66.4 16.7 %collective-permute-start.3 = (bf16[2,128,256]{2,1,0:T(8,128)(2,1)S(1)}, bf16[2,128,256]{2,1,0:T(8,128)(2,1)S(1)}, u32[]{:S(2)}, u32[]{:S(2)}) collective-permute-start(bf16[2,128,256]{2,1,0:T(8,128)(2,1)S(1)} %slice.18), channel_id=1, source_target_pairs={{0,7},{1,4},{2,5},{3,6},{4,11},{5,8},{6,9},{7,10},{8,15},{9,12},{1... | collective-permute-start | bytes 393224 | tf_op jit(solution)/shard_map/ppermute | solution.py:172
  68.6 14.6 %collective-permute-start.2 = (bf16[2,128,256]{2,1,0:T(8,128)(2,1)S(1)}, bf16[2,128,256]{2,1,0:T(8,128)(2,1)S(1)}, u32[]{:S(2)}, u32[]{:S(2)}) collective-permute-start(bf16[2,128,256]{2,1,0:T(8,128)(2,1)S(1)} %slice.18), channel_id=1, source_target_pairs={{0,6},{1,7},{2,4},{3,5},{4,10},{5,11},{6,8},{7,9},{8,14},{9,15},{1... | collective-permute-start | bytes 393224 | tf_op jit(solution)/shard_map/ppermute | solution.py:172
  74.9 10.0 %collective-permute-start.1 = (bf16[2,128,256]{2,1,0:T(8,128)(2,1)S(1)}, bf16[2,128,256]{2,1,0:T(8,128)(2,1)S(1)}, u32[]{:S(2)}, u32[]{:S(2)}) collective-permute-start(bf16[2,128,256]{2,1,0:T(8,128)(2,1)S(1)} %slice.18), channel_id=1, source_target_pairs={{0,5},{1,6},{2,7},{3,4},{4,9},{5,10},{6,11},{7,8},{8,13},{9,14},{1... | collective-permute-start | bytes 393224 | tf_op jit(solution)/shard_map/ppermute | solution.py:172
  77.0 11.2 %collective-permute-start = (bf16[2,128,256]{2,1,0:T(8,128)(2,1)S(1)}, bf16[2,128,256]{2,1,0:T(8,128)(2,1)S(1)}, u32[]{:S(2)}, u32[]{:S(2)}) collective-permute-start(bf16[2,128,256]{2,1,0:T(8,128)(2,1)S(1)} %slice.18), channel_id=1, source_target_pairs={{0,4},{1,5},{2,6},{3,7},{4,8},{5,9},{6,10},{7,11},{8,12},{9,13},{1... | collective-permute-start | bytes 393224 | tf_op jit(solution)/shard_map/ppermute | solution.py:172

commit v15 on v14

--- a/solution.py
+++ b/solution.py
@@ -27,9 +27,9 @@
 
 
 def block_attention_kernel(
-    sharp_ref, slices_ref, shared_proj_ref, value_proj_ref, out_ref, total_ref
+    sharp_ref, order_ref, prior_ref, here_ref, shared_proj_ref, value_proj_ref, out_ref, total_ref
 ):
-    n_groups, n_rounds, span_rows, group_cols = slices_ref.shape
+    n_groups, n_rounds, rows_here, group_cols = here_ref.shape
     heads = out_ref.shape[2] // HEAD_DIM
     n_blocks = out_ref.shape[1] // BLOCK
     features = n_groups * group_cols
@@ -37,7 +37,10 @@
     key_cols = lax.broadcasted_iota(jnp.int32, (BLOCK, 2 * BLOCK), 1)
     allowed = key_cols != rows + BLOCK
     for r in range(n_rounds):
-        parts = [slices_ref[g, r].astype(jnp.float32) for g in range(n_groups)]
+        parts = [
+            jnp.concatenate([prior_ref[order_ref[g], r], here_ref[g, r]], axis=0).astype(jnp.float32)
+            for g in range(n_groups)
+        ]
         row_mean = sum(jnp.sum(p, axis=1, keepdims=True) for p in parts) / features
         centred = [p - row_mean for p in parts]
         row_var = sum(jnp.sum(c * c, axis=1, keepdims=True) for c in centred) / features
@@ -80,18 +83,19 @@
                 )[0:1]
 
 
-def block_attention(slices, shared_proj, value_proj, sharpness):
-    n_groups, n_rounds, span_rows, group_cols = slices.shape
-    rows_here = span_rows - BLOCK
+def block_attention(prior, order, here, shared_proj, value_proj, sharpness):
+    n_groups, n_rounds, rows_here, group_cols = here.shape
+    span_rows = rows_here + BLOCK
     cols = shared_proj.shape[1]
     heads = cols // HEAD_DIM
     n_blocks = rows_here // BLOCK
     flops = n_rounds * heads * n_blocks * 4 * BLOCK * 2 * BLOCK * HEAD_DIM
     flops += n_rounds * span_rows * n_groups * group_cols * 2 * cols * 2
     vmem = pl.BlockSpec(memory_space=pltpu.VMEM)
+    smem = pl.BlockSpec(memory_space=pltpu.SMEM)
     return pl.pallas_call(
         block_attention_kernel,
-        in_specs=[pl.BlockSpec(memory_space=pltpu.SMEM), vmem, vmem, vmem],
+        in_specs=[smem, smem, vmem, vmem, vmem, vmem],
         out_specs=[vmem, vmem],
         out_shape=[
             jax.ShapeDtypeStruct((n_rounds, rows_here, cols), jnp.bfloat16),
@@ -100,9 +104,10 @@
         cost_estimate=pl.CostEstimate(
             flops=flops,
             transcendentals=n_rounds * heads * n_blocks * BLOCK * 2 * BLOCK,
-            bytes_accessed=slices.size * 2 + 4 * shared_proj.size + n_rounds * rows_here * cols * 2,
+            bytes_accessed=(prior.size + here.size) * 2 + 4 * shared_proj.size
+            + n_rounds * rows_here * cols * 2,
         ),
-    )(sharpness, slices, shared_proj, value_proj)
+    )(sharpness, order, prior, here, shared_proj, value_proj)
 
 
 def rank_within_group(group, order):
@@ -173,10 +178,9 @@
     received, gathered = lax.optimization_barrier((received, gathered))
     group_here = lax.axis_index("head")
     slice_order = (group_here - jnp.arange(n_groups, dtype=jnp.int32)) % n_groups
-    prior_slices = jnp.take(jnp.stack(received), slice_order, axis=0)
-    all_slices = jnp.concatenate([prior_slices, gathered], axis=2)
+    prior_stack = jnp.stack(received)
     results, block_totals = block_attention(
-        all_slices, common_lookup_projector, content_projector, lane_sharpness
+        prior_stack, slice_order, gathered, common_lookup_projector, content_projector, lane_sharpness
     )
     slot_totals = jnp.transpose(
         block_totals.reshape(n_rounds, heads_here, rows_here), (0, 2, 1)

time: 166 us -> 166 us (level)
  no operation moved by 1% of the time
where the time goes in v15:
time: 166 us; the launch traced here: 165 us
  blocking collectives  123 us (74%)
  starting transfers between devices  19.9 us (12%)
  other arithmetic  5.26 us (3%)
  waiting for transfers between devices  5.1 us (3%)
  Pallas kernels  4.72 us (3%)
  matrix products  4.5 us (3%)
  local copies, waits for them, and re-layouts  2.47 us (1%)
    all_to_all x1, blocking collectives, shards(): lax.all_to_all(outgoing, 'span', split_axis=0, concat_axis=0, tiled=True)  57.1 us
    all_to_all x1, blocking collectives, shards(): home = lax.all_to_all(back, 'span', split_axis=0, concat_axis=0, tiled=True)  54.6 us
    ppermute x4, starting transfers between devices, shards(): received.append(lax.ppermute(last_slice, ('span', 'head'), route))  16.4 us
    all_to_all x1, blocking collectives, shards(): lax.all_to_all(group_part.reshape(n_groups, rows_here // n_groups, group_...  11.2 us
    ppermute x4, waiting for transfers between devices, shards(): received.append(lax.ppermute(last_slice, ('span', 'head'), route))  5.09 us
    pallas_call x1, Pallas kernels, block_attention(): pl.pallas_call(block_attention_kernel, in_specs=[smem, smem, vmem, vmem,...  4.72 us
    all_to_all x1, starting transfers between devices, shards(): lax.all_to_all(copies, 'head', split_axis=0, concat_axis=0, tiled=True)  3.51 us
  transfers between devices with their start and end apart: 5, of which 2 were waited for; matrix products, arithmetic and copies ran while one was open for 0% of the time, Pallas kernels for 0%

profile of v15, /device:TPU:6, one launch (start us, length us, event | category | flops | bytes accessed | tf_op | source)
XLA Modules:
  0.0 165.0 jit_solution(5962661042937391437)
XLA Ops:
  0.0 0.0 copy-start
  0.0 0.7 and_select_fusion.1
  0.8 0.7 and_select_fusion.2
  1.5 0.5 convert_reduce_fusion.1
  1.9 0.8 add_add_fusion
  2.7 0.3 convert_reduce_fusion
  3.0 1.3 fusion.6
  4.2 57.1 %all_to_all.34 = bf16[128,8,256]{2,1,0:T(8,128)(2,1)S(1)} all-to-all(bf16[128,8,256]{2,1,0:T(8,128)(2,1)S(1)} %fusion.6), channel_id=1, replica_groups=mesh['span'=128,'head'=4] {'span'}, dimensions={0} | all-to-all | bytes 1048576 | tf_op jit(solution)/shard_map/all_to_all | solution.py:162
  61.3 0.5 fusion.7
  61.8 1.1 broadcast_in_dim.2
  62.9 3.5 %all-to-all-start.1 = ((bf16[4,2,256,256]{3,2,1,0:T(8,128)(2,1)}), bf16[4,2,256,256]{3,2,1,0:T(8,128)(2,1)S(1)}, u32[]{:S(2)}, u32[]{:S(2)}) async-start(bf16[4,2,256,256]{3,2,1,0:T(8,128)(2,1)} %broadcast_in_dim.2), calls=%async_computation.1 | async-start | bytes 2097152 | tf_op jit(solution)/shard_map/all_to_all | solution.py:168
  66.4 1.9 %collective-permute-start = (bf16[2,128,256]{2,1,0:T(8,128)(2,1)S(1)}, bf16[2,128,256]{2,1,0:T(8,128)(2,1)S(1)}, u32[]{:S(2)}, u32[]{:S(2)}) collective-permute-start(bf16[2,128,256]{2,1,0:T(8,128)(2,1)S(1)} %slice.16), channel_id=1, source_target_pairs={{0,4},{1,5},{2,6},{3,7},{4,8},{5,9},{6,10},{7,11},{8,12},{9,13},{1... | collective-permute-start | bytes 393224 | tf_op jit(solution)/shard_map/ppermute | solution.py:177
  68.4 6.5 %collective-permute-start.1 = (bf16[2,128,256]{2,1,0:T(8,128)(2,1)S(1)}, bf16[2,128,256]{2,1,0:T(8,128)(2,1)S(1)}, u32[]{:S(2)}, u32[]{:S(2)}) collective-permute-start(bf16[2,128,256]{2,1,0:T(8,128)(2,1)S(1)} %slice.16), channel_id=1, source_target_pairs={{0,5},{1,6},{2,7},{3,4},{4,9},{5,10},{6,11},{7,8},{8,13},{9,14},{1... | collective-permute-start | bytes 393224 | tf_op jit(solution)/shard_map/ppermute | solution.py:177
  74.9 3.3 %collective-permute-start.2 = (bf16[2,128,256]{2,1,0:T(8,128)(2,1)S(1)}, bf16[2,128,256]{2,1,0:T(8,128)(2,1)S(1)}, u32[]{:S(2)}, u32[]{:S(2)}) collective-permute-start(bf16[2,128,256]{2,1,0:T(8,128)(2,1)S(1)} %slice.16), channel_id=1, source_target_pairs={{0,6},{1,7},{2,4},{3,5},{4,10},{5,11},{6,8},{7,9},{8,14},{9,15},{1... | collective-permute-start | bytes 393224 | tf_op jit(solution)/shard_map/ppermute | solution.py:177
  78.2 4.7 %collective-permute-start.3 = (bf16[2,128,256]{2,1,0:T(8,128)(2,1)S(1)}, bf16[2,128,256]{2,1,0:T(8,128)(2,1)S(1)}, u32[]{:S(2)}, u32[]{:S(2)}) collective-permute-start(bf16[2,128,256]{2,1,0:T(8,128)(2,1)S(1)} %slice.16), channel_id=1, source_target_pairs={{0,7},{1,4},{2,5},{3,6},{4,11},{5,8},{6,9},{7,10},{8,15},{9,12},{1... | collective-permute-start | bytes 393224 | tf_op jit(solution)/shard_map/ppermute | solution.py:177
  82.8 0.5 and_select_fusion.3.order_ref
  83.4 0.0 collective-permute-done
  83.4 0.0 collective-permute-done.1
  83.4 3.7 %collective-permute-done.2 = bf16[2,128,256]{2,1,0:T(8,128)(2,1)S(1)} collective-permute-done((bf16[2,128,256]{2,1,0:T(8,128)(2,1)S(1)}, bf16[2,128,256]{2,1,0:T(8,128)(2,1)S(1)}, u32[]{:S(2)}, u32[]{:S(2)}) %collective-permute-start.2) | collective-permute-done | bytes 131104 | tf_op jit(solution)/shard_map/ppermute | solution.py:177
  87.1 1.4 collective-permute-done.3
  88.5 0.0 all-to-all-done.1.here_ref
  88.5 0.0 copy-start.1
  88.5 0.9 pad_maximum_fusion.prior_ref
  89.4 0.2 copy-done.1
  89.6 4.7 %shard_map.73 = (bf16[2,256,256]{2,1,0:T(8,128)(2,1)}, f32[2,2,2,128]{3,2,1,0:T(2,128)}) custom-call(f32[2]{0:T(128)} %sharp_ref.1, s32[4]{0:T(128)} %and_select_fusion.3.order_ref, bf16[4,2,128,256]{3,2,1,0:T(8,128)(2,1)} %pad_maximum_fusion.prior_ref, bf16[4,2,256,256]{3,2,1,0:T(8,128)(2,1)} %copy-done.1, bf16[1024,256]{1,0:T(8,128)(2,1)} %shared_proj_ref.1, ...), custom_call_target="tpu_custom_call" | custom-call | flops 939524096 | bytes 2883584 | tf_op jit(solution)/shard_map/pallas_call | solution.py:96
  94.4 0.8 copy.28
  95.2 1.7 %fusion.5 = bf16[1024,260]{0,1:T(8,128)(2,1)S(1)} fusion(s32[2,256]{1,0:T(2,128)S(1)} %get-tuple-element.23, bf16[2,256,2]{2,1,0:T(8,128)(2,1)S(1)} %get-tuple-element.19, bf16[2,256,2]{2,1,0:T(8,128)(2,1)S(1)} %get-tuple-element.20, bf16[2,256,256]{2,1,0:T(8,128)(2,1)} %get-tuple-element.17), kind=kOutput, calls=%fused_computation.8 | convolution fusion | flops 274219008 | bytes 800768 | tf_op jit(solution)/shard_map/rsq,rsw->qw/dot_general | solution.py:192
  97.0 0.4 copy.24
  97.3 54.6 %all_to_all.35 = bf16[128,8,260]{2,1,0:T(8,128)(2,1)S(1)} all-to-all(bf16[128,8,260]{2,1,0:T(8,128)(2,1)S(1)} %bitcast.36), channel_id=1, replica_groups=mesh['span'=128,'head'=4] {'span'}, dimensions={0} | all-to-all | bytes 1064960 | tf_op jit(solution)/shard_map/all_to_all | solution.py:195
  151.9 0.7 fusion.2
  152.7 0.0 copy-done
  152.7 0.3 convolution_convert_fusion
  153.0 11.2 %all_to_all.36 = bf16[4,64,1024]{2,1,0:T(8,128)(2,1)S(1)} all-to-all(bf16[4,64,1024]{2,1,0:T(8,128)(2,1)S(1)} %bitcast.37), channel_id=1, replica_groups=mesh['span'=128,'head'=4] {'head'}, dimensions={0} | all-to-all | bytes 1048576 | tf_op jit(solution)/shard_map/all_to_all | solution.py:209
  164.3 0.7 reduce_sum.62
  (7 shorter events, 0.1 us)
Async XLA Ops:
  0.0 152.7 %copy-start = (bf16[256,1024]{1,0:T(8,128)(2,1)S(1)}, bf16[256,1024]{1,0:T(8,128)(2,1)}, u32[]{:S(2)}) copy-start(bf16[256,1024]{1,0:T(8,128)(2,1)} %param.10) | copy-start | bytes 1572868
  62.9 25.6 %all-to-all-start.1 = ((bf16[4,2,256,256]{3,2,1,0:T(8,128)(2,1)}), bf16[4,2,256,256]{3,2,1,0:T(8,128)(2,1)S(1)}, u32[]{:S(2)}, u32[]{:S(2)}) async-start(bf16[4,2,256,256]{3,2,1,0:T(8,128)(2,1)} %broadcast_in_dim.2), calls=%async_computation.1 | async-start | bytes 2097152 | tf_op jit(solution)/shard_map/all_to_all | solution.py:168
  66.4 17.0 %collective-permute-start = (bf16[2,128,256]{2,1,0:T(8,128)(2,1)S(1)}, bf16[2,128,256]{2,1,0:T(8,128)(2,1)S(1)}, u32[]{:S(2)}, u32[]{:S(2)}) collective-permute-start(bf16[2,128,256]{2,1,0:T(8,128)(2,1)S(1)} %slice.16), channel_id=1, source_target_pairs={{0,4},{1,5},{2,6},{3,7},{4,8},{5,9},{6,10},{7,11},{8,12},{9,13},{1... | collective-permute-start | bytes 393224 | tf_op jit(solution)/shard_map/ppermute | solution.py:177
  68.4 15.0 %collective-permute-start.1 = (bf16[2,128,256]{2,1,0:T(8,128)(2,1)S(1)}, bf16[2,128,256]{2,1,0:T(8,128)(2,1)S(1)}, u32[]{:S(2)}, u32[]{:S(2)}) collective-permute-start(bf16[2,128,256]{2,1,0:T(8,128)(2,1)S(1)} %slice.16), channel_id=1, source_target_pairs={{0,5},{1,6},{2,7},{3,4},{4,9},{5,10},{6,11},{7,8},{8,13},{9,14},{1... | collective-permute-start | bytes 393224 | tf_op jit(solution)/shard_map/ppermute | solution.py:177
  74.9 12.2 %collective-permute-start.2 = (bf16[2,128,256]{2,1,0:T(8,128)(2,1)S(1)}, bf16[2,128,256]{2,1,0:T(8,128)(2,1)S(1)}, u32[]{:S(2)}, u32[]{:S(2)}) collective-permute-start(bf16[2,128,256]{2,1,0:T(8,128)(2,1)S(1)} %slice.16), channel_id=1, source_target_pairs={{0,6},{1,7},{2,4},{3,5},{4,10},{5,11},{6,8},{7,9},{8,14},{9,15},{1... | collective-permute-start | bytes 393224 | tf_op jit(solution)/shard_map/ppermute | solution.py:177
  78.2 10.3 %collective-permute-start.3 = (bf16[2,128,256]{2,1,0:T(8,128)(2,1)S(1)}, bf16[2,128,256]{2,1,0:T(8,128)(2,1)S(1)}, u32[]{:S(2)}, u32[]{:S(2)}) collective-permute-start(bf16[2,128,256]{2,1,0:T(8,128)(2,1)S(1)} %slice.16), channel_id=1, source_target_pairs={{0,7},{1,4},{2,5},{3,6},{4,11},{5,8},{6,9},{7,10},{8,15},{9,12},{1... | collective-permute-start | bytes 393224 | tf_op jit(solution)/shard_map/ppermute | solution.py:177
  88.5 1.2 copy-start.1

commit v16 on v15

--- a/solution.py
+++ b/solution.py
@@ -27,11 +27,13 @@
 
 
 def block_attention_kernel(
-    sharp_ref, order_ref, prior_ref, here_ref, shared_proj_ref, value_proj_ref, out_ref, total_ref
+    sharp_ref, order_ref, prior_ref, here_ref, shared_proj_ref, value_proj_ref, place_ref,
+    back_ref, out_ref, total_ref,
 ):
     n_groups, n_rounds, rows_here, group_cols = here_ref.shape
     heads = out_ref.shape[2] // HEAD_DIM
     n_blocks = out_ref.shape[1] // BLOCK
+    total_ref[...] = jnp.zeros_like(total_ref)
     features = n_groups * group_cols
     rows = lax.broadcasted_iota(jnp.int32, (BLOCK, 2 * BLOCK), 0)
     key_cols = lax.broadcasted_iota(jnp.int32, (BLOCK, 2 * BLOCK), 1)
@@ -78,12 +80,26 @@
                 out_ref[r, BLOCK * b : BLOCK * (b + 1), HEAD_DIM * h : HEAD_DIM * (h + 1)] = (
                     mixed.astype(out_ref.dtype)
                 )
-                total_ref[r, h, b : b + 1, :] = jnp.transpose(
-                    jnp.broadcast_to(totals, (BLOCK, BLOCK))
-                )[0:1]
-
-
-def block_attention(prior, order, here, shared_proj, value_proj, sharpness):
+                high = totals.astype(jnp.bfloat16)
+                low = (totals - high.astype(jnp.float32)).astype(jnp.bfloat16)
+                total_ref[r, BLOCK * b : BLOCK * (b + 1), h : h + 1] = high
+                total_ref[r, BLOCK * b : BLOCK * (b + 1), heads + h : heads + h + 1] = low
+    buffer_rows = back_ref.shape[0]
+    cols = out_ref.shape[2]
+    row_ids = lax.broadcasted_iota(jnp.int32, (buffer_rows, rows_here), 0)
+    back_rows = None
+    back_totals = None
+    for r in range(n_rounds):
+        hot = jnp.where(row_ids == place_ref[r : r + 1, :], 1.0, 0.0).astype(jnp.bfloat16)
+        rows_part = jnp.dot(hot, out_ref[r], preferred_element_type=jnp.float32)
+        totals_part = jnp.dot(hot, total_ref[r], preferred_element_type=jnp.float32)
+        back_rows = rows_part if back_rows is None else back_rows + rows_part
+        back_totals = totals_part if back_totals is None else back_totals + totals_part
+    back_ref[:, :cols] = back_rows.astype(back_ref.dtype)
+    back_ref[:, cols:] = back_totals[:, : back_ref.shape[1] - cols].astype(back_ref.dtype)
+
+
+def block_attention(prior, order, here, shared_proj, value_proj, sharpness, place, buffer_rows):
     n_groups, n_rounds, rows_here, group_cols = here.shape
     span_rows = rows_here + BLOCK
     cols = shared_proj.shape[1]
@@ -91,23 +107,26 @@
     n_blocks = rows_here // BLOCK
     flops = n_rounds * heads * n_blocks * 4 * BLOCK * 2 * BLOCK * HEAD_DIM
     flops += n_rounds * span_rows * n_groups * group_cols * 2 * cols * 2
+    flops += n_rounds * buffer_rows * rows_here * 2 * (cols + BLOCK)
     vmem = pl.BlockSpec(memory_space=pltpu.VMEM)
     smem = pl.BlockSpec(memory_space=pltpu.SMEM)
-    return pl.pallas_call(
+    back, _, _ = pl.pallas_call(
         block_attention_kernel,
-        in_specs=[smem, smem, vmem, vmem, vmem, vmem],
-        out_specs=[vmem, vmem],
+        in_specs=[smem, smem, vmem, vmem, vmem, vmem, vmem],
+        out_specs=[vmem, vmem, vmem],
         out_shape=[
+            jax.ShapeDtypeStruct((buffer_rows, cols + 2 * heads), jnp.bfloat16),
             jax.ShapeDtypeStruct((n_rounds, rows_here, cols), jnp.bfloat16),
-            jax.ShapeDtypeStruct((n_rounds, heads, n_blocks, BLOCK), jnp.float32),
+            jax.ShapeDtypeStruct((n_rounds, rows_here, BLOCK), jnp.bfloat16),
         ],
         cost_estimate=pl.CostEstimate(
             flops=flops,
             transcendentals=n_rounds * heads * n_blocks * BLOCK * 2 * BLOCK,
             bytes_accessed=(prior.size + here.size) * 2 + 4 * shared_proj.size
-            + n_rounds * rows_here * cols * 2,
+            + buffer_rows * (cols + 2 * heads) * 2,
         ),
-    )(sharpness, order, prior, here, shared_proj, value_proj)
+    )(sharpness, order, prior, here, shared_proj, value_proj, place)
+    return back
 
 
 def rank_within_group(group, order):
@@ -179,19 +198,16 @@
     group_here = lax.axis_index("head")
     slice_order = (group_here - jnp.arange(n_groups, dtype=jnp.int32)) % n_groups
     prior_stack = jnp.stack(received)
-    results, block_totals = block_attention(
-        prior_stack, slice_order, gathered, common_lookup_projector, content_projector, lane_sharpness
-    )
-    slot_totals = jnp.transpose(
-        block_totals.reshape(n_rounds, heads_here, rows_here), (0, 2, 1)
-    )
-    totals_high = slot_totals.astype(jnp.bfloat16)
-    totals_low = (slot_totals - totals_high.astype(jnp.float32)).astype(jnp.bfloat16)
-    back_payload = jnp.concatenate([results, totals_high, totals_low], axis=2)
-
-    back = jnp.einsum(
-        "rsq,rsw->qw", recv_hot, back_payload, preferred_element_type=jnp.float32
-    ).astype(jnp.bfloat16)
+    back = block_attention(
+        prior_stack,
+        slice_order,
+        gathered,
+        common_lookup_projector,
+        content_projector,
+        lane_sharpness,
+        recv_row,
+        buffer_rows,
+    )
     home = lax.all_to_all(back, "span", split_axis=0, concat_axis=0, tiled=True)
     token_all = jnp.einsum("rtq,qw->rtw", send_hot, home, preferred_element_type=jnp.float32)
     token_rows = token_all[:, :, :head_cols]

time: 166 us -> 163 us (0.982)
  matrix products: 4.5 us -> 2.79 us
    dot_general x1 -> x0, matrix products: 1.71 us -> none  [shards(): jnp.einsum('rsq,rsw->qw', recv_hot, back_payload, preferred_element_type=...]
where the time goes in v16:
time: 163 us
  blocking collectives  123 us (75%)
  starting transfers between devices  20.2 us (12%)
  Pallas kernels  5.68 us (3%)
  other arithmetic  5.27 us (3%)
  waiting for transfers between devices  4.53 us (3%)
  matrix products  2.79 us (2%)
    all_to_all x1, blocking collectives, shards(): lax.all_to_all(outgoing, 'span', split_axis=0, concat_axis=0, tiled=True)  57.1 us
    all_to_all x1, blocking collectives, shards(): home = lax.all_to_all(back, 'span', split_axis=0, concat_axis=0, tiled=True)  53.8 us
    ppermute x4, starting transfers between devices, shards(): received.append(lax.ppermute(last_slice, ('span', 'head'), route))  16.7 us
    all_to_all x1, blocking collectives, shards(): lax.all_to_all(group_part.reshape(n_groups, rows_here // n_groups, group_...  11.8 us
    pallas_call x1, Pallas kernels, block_attention(): pl.pallas_call(block_attention_kernel, in_specs=[smem, smem, vmem, vmem,...  5.68 us
    ppermute x4, waiting for transfers between devices, shards(): received.append(lax.ppermute(last_slice, ('span', 'head'), route))  4.53 us
    all_to_all x1, starting transfers between devices, shards(): lax.all_to_all(copies, 'head', split_axis=0, concat_axis=0, tiled=True)  3.51 us
  transfers between devices with their start and end apart: 5, of which 2 were waited for; matrix products, arithmetic and copies ran while one was open for 0% of the time, Pallas kernels for 0%

profile of v16, /device:TPU:6, one launch (start us, length us, event | category | flops | bytes accessed | tf_op | source)
XLA Modules:
  0.0 162.6 jit_solution(14046553621832413365)
XLA Ops:
  0.0 0.0 copy-start
  0.0 0.7 and_select_fusion.2
  0.8 0.7 and_select_fusion.1
  1.5 0.5 convert_reduce_fusion.1
  1.9 0.8 add_add_fusion
  2.7 0.0 copy-start.2
  2.7 0.3 convert_reduce_fusion
  3.0 1.3 fusion.3
  4.2 57.1 %all_to_all.34 = bf16[128,8,256]{2,1,0:T(8,128)(2,1)S(1)} all-to-all(bf16[128,8,256]{2,1,0:T(8,128)(2,1)S(1)} %fusion.3), channel_id=1, replica_groups=mesh['span'=128,'head'=4] {'span'}, dimensions={0} | all-to-all | bytes 1048576 | tf_op jit(solution)/shard_map/all_to_all | solution.py:181
  61.3 0.0 copy-done.2
  61.3 0.5 fusion.4
  61.8 1.1 broadcast_in_dim.2
  62.9 3.5 %all-to-all-start.1 = ((bf16[4,2,256,256]{3,2,1,0:T(8,128)(2,1)}), bf16[4,2,256,256]{3,2,1,0:T(8,128)(2,1)S(1)}, u32[]{:S(2)}, u32[]{:S(2)}) async-start(bf16[4,2,256,256]{3,2,1,0:T(8,128)(2,1)} %broadcast_in_dim.2), calls=%async_computation.1 | async-start | bytes 2097152 | tf_op jit(solution)/shard_map/all_to_all | solution.py:187
  66.4 2.2 %collective-permute-start.3 = (bf16[2,128,256]{2,1,0:T(8,128)(2,1)S(1)}, bf16[2,128,256]{2,1,0:T(8,128)(2,1)S(1)}, u32[]{:S(2)}, u32[]{:S(2)}) collective-permute-start(bf16[2,128,256]{2,1,0:T(8,128)(2,1)S(1)} %slice.16), channel_id=1, source_target_pairs={{0,7},{1,4},{2,5},{3,6},{4,11},{5,8},{6,9},{7,10},{8,15},{9,12},{1... | collective-permute-start | bytes 393224 | tf_op jit(solution)/shard_map/ppermute | solution.py:196
  68.6 6.3 %collective-permute-start.2 = (bf16[2,128,256]{2,1,0:T(8,128)(2,1)S(1)}, bf16[2,128,256]{2,1,0:T(8,128)(2,1)S(1)}, u32[]{:S(2)}, u32[]{:S(2)}) collective-permute-start(bf16[2,128,256]{2,1,0:T(8,128)(2,1)S(1)} %slice.16), channel_id=1, source_target_pairs={{0,6},{1,7},{2,4},{3,5},{4,10},{5,11},{6,8},{7,9},{8,14},{9,15},{1... | collective-permute-start | bytes 393224 | tf_op jit(solution)/shard_map/ppermute | solution.py:196
  74.9 2.1 %collective-permute-start.1 = (bf16[2,128,256]{2,1,0:T(8,128)(2,1)S(1)}, bf16[2,128,256]{2,1,0:T(8,128)(2,1)S(1)}, u32[]{:S(2)}, u32[]{:S(2)}) collective-permute-start(bf16[2,128,256]{2,1,0:T(8,128)(2,1)S(1)} %slice.16), channel_id=1, source_target_pairs={{0,5},{1,6},{2,7},{3,4},{4,9},{5,10},{6,11},{7,8},{8,13},{9,14},{1... | collective-permute-start | bytes 393224 | tf_op jit(solution)/shard_map/ppermute | solution.py:196
  77.0 6.1 %collective-permute-start = (bf16[2,128,256]{2,1,0:T(8,128)(2,1)S(1)}, bf16[2,128,256]{2,1,0:T(8,128)(2,1)S(1)}, u32[]{:S(2)}, u32[]{:S(2)}) collective-permute-start(bf16[2,128,256]{2,1,0:T(8,128)(2,1)S(1)} %slice.16), channel_id=1, source_target_pairs={{0,4},{1,5},{2,6},{3,7},{4,8},{5,9},{6,10},{7,11},{8,12},{9,13},{1... | collective-permute-start | bytes 393224 | tf_op jit(solution)/shard_map/ppermute | solution.py:196
  83.1 0.6 and_select_fusion.3.order_ref
  83.7 0.0 collective-permute-done.3
  83.7 0.0 collective-permute-done.2
  83.7 1.1 collective-permute-done.1
  84.8 3.4 %collective-permute-done = bf16[2,128,256]{2,1,0:T(8,128)(2,1)S(1)} collective-permute-done((bf16[2,128,256]{2,1,0:T(8,128)(2,1)S(1)}, bf16[2,128,256]{2,1,0:T(8,128)(2,1)S(1)}, u32[]{:S(2)}, u32[]{:S(2)}) %collective-permute-start) | collective-permute-done | bytes 131104 | tf_op jit(solution)/shard_map/ppermute | solution.py:196
  88.3 0.0 all-to-all-done.1.here_ref
  88.3 0.0 copy-start.1
  88.3 0.9 pad_maximum_fusion.prior_ref
  89.2 0.2 copy-done.1
  89.4 5.7 %shard_map.73 = (bf16[1024,260]{1,0:T(8,128)(2,1)}, bf16[2,256,256]{2,1,0:T(8,128)(2,1)}, bf16[2,256,128]{2,1,0:T(8,128)(2,1)}) custom-call(f32[2]{0:T(128)} %sharp_ref.1, s32[4]{0:T(128)} %and_select_fusion.3.order_ref, bf16[4,2,128,256]{3,2,1,0:T(8,128)(2,1)} %pad_maximum_fusion.prior_ref, bf16[4,2,256,256]{3,2,1,0:T(8,128)(2,1)} %copy-done.1, ...), custom_call_target="tpu_custom_call" | custom-call | flops 1342177280 | bytes 3153920 | tf_op jit(solution)/shard_map/pallas_call | solution.py:113
  95.1 53.8 %all_to_all.35 = bf16[128,8,260]{2,1,0:T(8,128)(2,1)S(1)} all-to-all(bf16[128,8,260]{2,1,0:T(8,128)(2,1)} %bitcast.25), channel_id=1, replica_groups=mesh['span'=128,'head'=4] {'span'}, dimensions={0} | all-to-all | bytes 1064960 | tf_op jit(solution)/shard_map/all_to_all | solution.py:211
  148.9 0.7 fusion
  149.7 0.0 copy-done
  149.7 0.3 convolution_convert_fusion
  150.1 11.8 %all_to_all.36 = bf16[4,64,1024]{2,1,0:T(8,128)(2,1)S(1)} all-to-all(bf16[4,64,1024]{2,1,0:T(8,128)(2,1)S(1)} %bitcast.24), channel_id=1, replica_groups=mesh['span'=128,'head'=4] {'head'}, dimensions={0} | all-to-all | bytes 1048576 | tf_op jit(solution)/shard_map/all_to_all | solution.py:225
  161.9 0.7 reduce_sum.62
  (6 shorter events, 0.1 us)
Async XLA Ops:
  0.0 149.7 %copy-start = (bf16[256,1024]{1,0:T(8,128)(2,1)S(1)}, bf16[256,1024]{1,0:T(8,128)(2,1)}, u32[]{:S(2)}) copy-start(bf16[256,1024]{1,0:T(8,128)(2,1)} %param.10) | copy-start | bytes 1572868
  2.7 58.6 %copy-start.2 = (s32[2,256]{1,0:T(2,128)}, s32[2,256]{1,0:T(2,128)S(1)}, u32[]{:S(2)}) copy-start(s32[2,256]{1,0:T(2,128)S(1)} %get-tuple-element.19.place_ref) | copy-start | bytes 6148
  62.9 25.4 %all-to-all-start.1 = ((bf16[4,2,256,256]{3,2,1,0:T(8,128)(2,1)}), bf16[4,2,256,256]{3,2,1,0:T(8,128)(2,1)S(1)}, u32[]{:S(2)}, u32[]{:S(2)}) async-start(bf16[4,2,256,256]{3,2,1,0:T(8,128)(2,1)} %broadcast_in_dim.2), calls=%async_computation.1 | async-start | bytes 2097152 | tf_op jit(solution)/shard_map/all_to_all | solution.py:187
  66.4 17.3 %collective-permute-start.3 = (bf16[2,128,256]{2,1,0:T(8,128)(2,1)S(1)}, bf16[2,128,256]{2,1,0:T(8,128)(2,1)S(1)}, u32[]{:S(2)}, u32[]{:S(2)}) collective-permute-start(bf16[2,128,256]{2,1,0:T(8,128)(2,1)S(1)} %slice.16), channel_id=1, source_target_pairs={{0,7},{1,4},{2,5},{3,6},{4,11},{5,8},{6,9},{7,10},{8,15},{9,12},{1... | collective-permute-start | bytes 393224 | tf_op jit(solution)/shard_map/ppermute | solution.py:196
  68.6 15.2 %collective-permute-start.2 = (bf16[2,128,256]{2,1,0:T(8,128)(2,1)S(1)}, bf16[2,128,256]{2,1,0:T(8,128)(2,1)S(1)}, u32[]{:S(2)}, u32[]{:S(2)}) collective-permute-start(bf16[2,128,256]{2,1,0:T(8,128)(2,1)S(1)} %slice.16), channel_id=1, source_target_pairs={{0,6},{1,7},{2,4},{3,5},{4,10},{5,11},{6,8},{7,9},{8,14},{9,15},{1... | collective-permute-start | bytes 393224 | tf_op jit(solution)/shard_map/ppermute | solution.py:196
  74.9 10.0 %collective-permute-start.1 = (bf16[2,128,256]{2,1,0:T(8,128)(2,1)S(1)}, bf16[2,128,256]{2,1,0:T(8,128)(2,1)S(1)}, u32[]{:S(2)}, u32[]{:S(2)}) collective-permute-start(bf16[2,128,256]{2,1,0:T(8,128)(2,1)S(1)} %slice.16), channel_id=1, source_target_pairs={{0,5},{1,6},{2,7},{3,4},{4,9},{5,10},{6,11},{7,8},{8,13},{9,14},{1... | collective-permute-start | bytes 393224 | tf_op jit(solution)/shard_map/ppermute | solution.py:196
  77.0 11.2 %collective-permute-start = (bf16[2,128,256]{2,1,0:T(8,128)(2,1)S(1)}, bf16[2,128,256]{2,1,0:T(8,128)(2,1)S(1)}, u32[]{:S(2)}, u32[]{:S(2)}) collective-permute-start(bf16[2,128,256]{2,1,0:T(8,128)(2,1)S(1)} %slice.16), channel_id=1, source_target_pairs={{0,4},{1,5},{2,6},{3,7},{4,8},{5,9},{6,10},{7,11},{8,12},{9,13},{1... | collective-permute-start | bytes 393224 | tf_op jit(solution)/shard_map/ppermute | solution.py:196
  88.3 1.2 copy-start.1

commit v17 on v16

--- a/solution.py
+++ b/solution.py
@@ -26,10 +26,12 @@
     return (centred * lax.rsqrt(row_var + epsilon)).astype(jnp.bfloat16)
 
 
-def block_attention_kernel(
-    sharp_ref, order_ref, prior_ref, here_ref, shared_proj_ref, value_proj_ref, place_ref,
-    back_ref, out_ref, total_ref,
-):
+def block_attention_kernel(sharp_ref, order_ref, *refs):
+    n_groups = len(refs) - 7
+    prior_refs = refs[:n_groups]
+    here_ref, shared_proj_ref, value_proj_ref, place_ref, back_ref, out_ref, total_ref = refs[
+        n_groups:
+    ]
     n_groups, n_rounds, rows_here, group_cols = here_ref.shape
     heads = out_ref.shape[2] // HEAD_DIM
     n_blocks = out_ref.shape[1] // BLOCK
@@ -39,10 +41,14 @@
     key_cols = lax.broadcasted_iota(jnp.int32, (BLOCK, 2 * BLOCK), 1)
     allowed = key_cols != rows + BLOCK
     for r in range(n_rounds):
-        parts = [
-            jnp.concatenate([prior_ref[order_ref[g], r], here_ref[g, r]], axis=0).astype(jnp.float32)
-            for g in range(n_groups)
-        ]
+        parts = []
+        for g in range(n_groups):
+            prior = prior_refs[0][r]
+            for k in range(1, n_groups):
+                prior = jnp.where(order_ref[g] == k, prior_refs[k][r], prior)
+            parts.append(
+                jnp.concatenate([prior, here_ref[g, r]], axis=0).astype(jnp.float32)
+            )
         row_mean = sum(jnp.sum(p, axis=1, keepdims=True) for p in parts) / features
         centred = [p - row_mean for p in parts]
         row_var = sum(jnp.sum(c * c, axis=1, keepdims=True) for c in centred) / features
@@ -112,7 +118,7 @@
     smem = pl.BlockSpec(memory_space=pltpu.SMEM)
     back, _, _ = pl.pallas_call(
         block_attention_kernel,
-        in_specs=[smem, smem, vmem, vmem, vmem, vmem, vmem],
+        in_specs=[smem, smem] + [vmem] * (len(prior) + 4),
         out_specs=[vmem, vmem, vmem],
         out_shape=[
             jax.ShapeDtypeStruct((buffer_rows, cols + 2 * heads), jnp.bfloat16),
@@ -122,10 +128,10 @@
         cost_estimate=pl.CostEstimate(
             flops=flops,
             transcendentals=n_rounds * heads * n_blocks * BLOCK * 2 * BLOCK,
-            bytes_accessed=(prior.size + here.size) * 2 + 4 * shared_proj.size
+            bytes_accessed=(sum(p.size for p in prior) + here.size) * 2 + 4 * shared_proj.size
             + buffer_rows * (cols + 2 * heads) * 2,
         ),
-    )(sharpness, order, prior, here, shared_proj, value_proj, place)
+    )(sharpness, order, *prior, here, shared_proj, value_proj, place)
     return back
 
 
@@ -197,9 +203,8 @@
     received, gathered = lax.optimization_barrier((received, gathered))
     group_here = lax.axis_index("head")
     slice_order = (group_here - jnp.arange(n_groups, dtype=jnp.int32)) % n_groups
-    prior_stack = jnp.stack(received)
     back = block_attention(
-        prior_stack,
+        list(received),
         slice_order,
         gathered,
         common_lookup_projector,

time: 163 us -> 164 us (level)
  no operation moved by 1% of the time
where the time goes in v17:
time: 164 us; the launch traced here: 163 us
  blocking collectives  123 us (75%)
  starting transfers between devices  20.2 us (12%)
  Pallas kernels  5.74 us (4%)
  waiting for transfers between devices  4.52 us (3%)
  other arithmetic  4.33 us (3%)
  matrix products  2.78 us (2%)
  local copies, waits for them, and re-layouts  2.7 us (2%)
    all_to_all x1, blocking collectives, shards(): lax.all_to_all(outgoing, 'span', split_axis=0, concat_axis=0, tiled=True)  57.1 us
    all_to_all x1, blocking collectives, shards(): home = lax.all_to_all(back, 'span', split_axis=0, concat_axis=0, tiled=True)  53.8 us
    ppermute x4, starting transfers between devices, shards(): received.append(lax.ppermute(last_slice, ('span', 'head'), route))  16.7 us
    all_to_all x1, blocking collectives, shards(): lax.all_to_all(group_part.reshape(n_groups, rows_here // n_groups, group_...  11.8 us
    pallas_call x1, Pallas kernels, block_attention(): pl.pallas_call(block_attention_kernel, in_specs=[smem, smem] + [vmem] * (...  5.74 us
    ppermute x4, waiting for transfers between devices, shards(): received.append(lax.ppermute(last_slice, ('span', 'head'), route))  4.52 us
    all_to_all x1, starting transfers between devices, shards(): lax.all_to_all(copies, 'head', split_axis=0, concat_axis=0, tiled=True)  3.51 us
  transfers between devices with their start and end apart: 5, of which 2 were waited for; matrix products, arithmetic and copies ran while one was open for 0% of the time, Pallas kernels for 0%

profile of v17, /device:TPU:6, one launch (start us, length us, event | category | flops | bytes accessed | tf_op | source)
XLA Modules:
  0.0 163.2 jit_solution(4403845457596776248)
XLA Ops:
  0.0 0.0 copy-start
  0.0 0.7 and_select_fusion.2
  0.8 0.7 and_select_fusion.1
  1.5 0.5 convert_reduce_fusion.1
  1.9 0.8 add_add_fusion
  2.7 0.0 copy-start.2
  2.7 0.3 convert_reduce_fusion
  3.0 1.3 fusion.3
  4.2 57.1 %all_to_all.34 = bf16[128,8,256]{2,1,0:T(8,128)(2,1)S(1)} all-to-all(bf16[128,8,256]{2,1,0:T(8,128)(2,1)S(1)} %fusion.3), channel_id=1, replica_groups=mesh['span'=128,'head'=4] {'span'}, dimensions={0} | all-to-all | bytes 1048576 | tf_op jit(solution)/shard_map/all_to_all | solution.py:187
  61.3 0.0 copy-done.2
  61.3 0.5 fusion.4
  61.8 1.1 broadcast_in_dim.2
  62.9 3.5 %all-to-all-start.1 = ((bf16[4,2,256,256]{3,2,1,0:T(8,128)(2,1)}), bf16[4,2,256,256]{3,2,1,0:T(8,128)(2,1)S(1)}, u32[]{:S(2)}, u32[]{:S(2)}) async-start(bf16[4,2,256,256]{3,2,1,0:T(8,128)(2,1)} %broadcast_in_dim.2), calls=%async_computation.1 | async-start | bytes 2097152 | tf_op jit(solution)/shard_map/all_to_all | solution.py:193
  66.4 2.2 %collective-permute-start.3 = (bf16[2,128,256]{2,1,0:T(8,128)(2,1)S(1)}, bf16[2,128,256]{2,1,0:T(8,128)(2,1)S(1)}, u32[]{:S(2)}, u32[]{:S(2)}) collective-permute-start(bf16[2,128,256]{2,1,0:T(8,128)(2,1)S(1)} %slice.16), channel_id=1, source_target_pairs={{0,7},{1,4},{2,5},{3,6},{4,11},{5,8},{6,9},{7,10},{8,15},{9,12},{1... | collective-permute-start | bytes 393224 | tf_op jit(solution)/shard_map/ppermute | solution.py:202
  68.6 6.3 %collective-permute-start.2 = (bf16[2,128,256]{2,1,0:T(8,128)(2,1)S(1)}, bf16[2,128,256]{2,1,0:T(8,128)(2,1)S(1)}, u32[]{:S(2)}, u32[]{:S(2)}) collective-permute-start(bf16[2,128,256]{2,1,0:T(8,128)(2,1)S(1)} %slice.16), channel_id=1, source_target_pairs={{0,6},{1,7},{2,4},{3,5},{4,10},{5,11},{6,8},{7,9},{8,14},{9,15},{1... | collective-permute-start | bytes 393224 | tf_op jit(solution)/shard_map/ppermute | solution.py:202
  74.9 2.1 %collective-permute-start.1 = (bf16[2,128,256]{2,1,0:T(8,128)(2,1)S(1)}, bf16[2,128,256]{2,1,0:T(8,128)(2,1)S(1)}, u32[]{:S(2)}, u32[]{:S(2)}) collective-permute-start(bf16[2,128,256]{2,1,0:T(8,128)(2,1)S(1)} %slice.16), channel_id=1, source_target_pairs={{0,5},{1,6},{2,7},{3,4},{4,9},{5,10},{6,11},{7,8},{8,13},{9,14},{1... | collective-permute-start | bytes 393224 | tf_op jit(solution)/shard_map/ppermute | solution.py:202
  77.0 6.1 %collective-permute-start = (bf16[2,128,256]{2,1,0:T(8,128)(2,1)S(1)}, bf16[2,128,256]{2,1,0:T(8,128)(2,1)S(1)}, u32[]{:S(2)}, u32[]{:S(2)}) collective-permute-start(bf16[2,128,256]{2,1,0:T(8,128)(2,1)S(1)} %slice.16), channel_id=1, source_target_pairs={{0,4},{1,5},{2,6},{3,7},{4,8},{5,9},{6,10},{7,11},{8,12},{9,13},{1... | collective-permute-start | bytes 393224 | tf_op jit(solution)/shard_map/ppermute | solution.py:202
  83.1 0.6 and_select_fusion.3.order_ref
  83.7 0.0 collective-permute-done.3.refs_3_
  83.7 0.0 copy-start.3
  83.7 0.0 collective-permute-done.2.refs_2_
  83.7 0.0 copy-start.4
  83.8 1.1 collective-permute-done.1.refs_1_
  84.8 0.0 copy-start.5
  84.8 3.4 %collective-permute-done.refs_0_ = bf16[2,128,256]{2,1,0:T(8,128)(2,1)S(1)} collective-permute-done((bf16[2,128,256]{2,1,0:T(8,128)(2,1)S(1)}, bf16[2,128,256]{2,1,0:T(8,128)(2,1)S(1)}, u32[]{:S(2)}, u32[]{:S(2)}) %collective-permute-start) | collective-permute-done | bytes 131104 | tf_op jit(solution)/shard_map/ppermute | solution.py:202
  88.3 0.0 copy-start.6
  88.3 0.0 all-to-all-done.1.refs_4_
  88.3 0.0 copy-done.3
  88.3 0.0 copy-done.4
  88.3 0.0 copy-done.5
  88.3 0.6 copy-done.6
  88.9 0.0 copy-start.1
  88.9 1.0 copy-done.1
  89.9 5.7 %shard_map.73 = (bf16[1024,260]{1,0:T(8,128)(2,1)}, bf16[2,256,256]{2,1,0:T(8,128)(2,1)}, bf16[2,256,128]{2,1,0:T(8,128)(2,1)}) custom-call(f32[2]{0:T(128)} %sharp_ref.1, s32[4]{0:T(128)} %and_select_fusion.3.order_ref, bf16[2,128,256]{2,1,0:T(8,128)(2,1)} %copy-done.6, bf16[2,128,256]{2,1,0:T(8,128)(2,1)} %copy-done.5, bf16[2,128,256]{2,1,0:T(8,128)(2,1)} %copy-done.4, ...), custom_call_target="tpu_custom_call" | custom-call | flops 1342177280 | bytes 3153920 | tf_op jit(solution)/shard_map/pallas_call | solution.py:119
  95.6 53.8 %all_to_all.35 = bf16[128,8,260]{2,1,0:T(8,128)(2,1)S(1)} all-to-all(bf16[128,8,260]{2,1,0:T(8,128)(2,1)} %bitcast.21), channel_id=1, replica_groups=mesh['span'=128,'head'=4] {'span'}, dimensions={0} | all-to-all | bytes 1064960 | tf_op jit(solution)/shard_map/all_to_all | solution.py:216
  149.5 0.7 fusion
  150.3 0.0 copy-done
  150.3 0.3 convolution_convert_fusion
  150.6 11.8 %all_to_all.36 = bf16[4,64,1024]{2,1,0:T(8,128)(2,1)S(1)} all-to-all(bf16[4,64,1024]{2,1,0:T(8,128)(2,1)S(1)} %bitcast.20), channel_id=1, replica_groups=mesh['span'=128,'head'=4] {'head'}, dimensions={0} | all-to-all | bytes 1048576 | tf_op jit(solution)/shard_map/all_to_all | solution.py:230
  162.4 0.7 reduce_sum.62
  (6 shorter events, 0.1 us)
Async XLA Ops:
  0.0 150.3 %copy-start = (bf16[256,1024]{1,0:T(8,128)(2,1)S(1)}, bf16[256,1024]{1,0:T(8,128)(2,1)}, u32[]{:S(2)}) copy-start(bf16[256,1024]{1,0:T(8,128)(2,1)} %param.10) | copy-start | bytes 1572868
  2.7 58.6 %copy-start.2 = (s32[2,256]{1,0:T(2,128)}, s32[2,256]{1,0:T(2,128)S(1)}, u32[]{:S(2)}) copy-start(s32[2,256]{1,0:T(2,128)S(1)} %get-tuple-element.19.refs_7_) | copy-start | bytes 6148
  62.9 25.4 %all-to-all-start.1 = ((bf16[4,2,256,256]{3,2,1,0:T(8,128)(2,1)}), bf16[4,2,256,256]{3,2,1,0:T(8,128)(2,1)S(1)}, u32[]{:S(2)}, u32[]{:S(2)}) async-start(bf16[4,2,256,256]{3,2,1,0:T(8,128)(2,1)} %broadcast_in_dim.2), calls=%async_computation.1 | async-start | bytes 2097152 | tf_op jit(solution)/shard_map/all_to_all | solution.py:193
  66.4 17.3 %collective-permute-start.3 = (bf16[2,128,256]{2,1,0:T(8,128)(2,1)S(1)}, bf16[2,128,256]{2,1,0:T(8,128)(2,1)S(1)}, u32[]{:S(2)}, u32[]{:S(2)}) collective-permute-start(bf16[2,128,256]{2,1,0:T(8,128)(2,1)S(1)} %slice.16), channel_id=1, source_target_pairs={{0,7},{1,4},{2,5},{3,6},{4,11},{5,8},{6,9},{7,10},{8,15},{9,12},{1... | collective-permute-start | bytes 393224 | tf_op jit(solution)/shard_map/ppermute | solution.py:202
  68.6 15.2 %collective-permute-start.2 = (bf16[2,128,256]{2,1,0:T(8,128)(2,1)S(1)}, bf16[2,128,256]{2,1,0:T(8,128)(2,1)S(1)}, u32[]{:S(2)}, u32[]{:S(2)}) collective-permute-start(bf16[2,128,256]{2,1,0:T(8,128)(2,1)S(1)} %slice.16), channel_id=1, source_target_pairs={{0,6},{1,7},{2,4},{3,5},{4,10},{5,11},{6,8},{7,9},{8,14},{9,15},{1... | collective-permute-start | bytes 393224 | tf_op jit(solution)/shard_map/ppermute | solution.py:202
  74.9 10.0 %collective-permute-start.1 = (bf16[2,128,256]{2,1,0:T(8,128)(2,1)S(1)}, bf16[2,128,256]{2,1,0:T(8,128)(2,1)S(1)}, u32[]{:S(2)}, u32[]{:S(2)}) collective-permute-start(bf16[2,128,256]{2,1,0:T(8,128)(2,1)S(1)} %slice.16), channel_id=1, source_target_pairs={{0,5},{1,6},{2,7},{3,4},{4,9},{5,10},{6,11},{7,8},{8,13},{9,14},{1... | collective-permute-start | bytes 393224 | tf_op jit(solution)/shard_map/ppermute | solution.py:202
  77.0 11.2 %collective-permute-start = (bf16[2,128,256]{2,1,0:T(8,128)(2,1)S(1)}, bf16[2,128,256]{2,1,0:T(8,128)(2,1)S(1)}, u32[]{:S(2)}, u32[]{:S(2)}) collective-permute-start(bf16[2,128,256]{2,1,0:T(8,128)(2,1)S(1)} %slice.16), channel_id=1, source_target_pairs={{0,4},{1,5},{2,6},{3,7},{4,8},{5,9},{6,10},{7,11},{8,12},{9,13},{1... | collective-permute-start | bytes 393224 | tf_op jit(solution)/shard_map/ppermute | solution.py:202
  83.7 4.5 %copy-start.3 = (bf16[2,128,256]{2,1,0:T(8,128)(2,1)}, bf16[2,128,256]{2,1,0:T(8,128)(2,1)S(1)}, u32[]{:S(2)}) copy-start(bf16[2,128,256]{2,1,0:T(8,128)(2,1)S(1)} %collective-permute-done.3.refs_3_) | copy-start | bytes 393220
  83.7 4.5 %copy-start.4 = (bf16[2,128,256]{2,1,0:T(8,128)(2,1)}, bf16[2,128,256]{2,1,0:T(8,128)(2,1)S(1)}, u32[]{:S(2)}) copy-start(bf16[2,128,256]{2,1,0:T(8,128)(2,1)S(1)} %collective-permute-done.2.refs_2_) | copy-start | bytes 393220
  84.8 3.5 %copy-start.5 = (bf16[2,128,256]{2,1,0:T(8,128)(2,1)}, bf16[2,128,256]{2,1,0:T(8,128)(2,1)S(1)}, u32[]{:S(2)}) copy-start(bf16[2,128,256]{2,1,0:T(8,128)(2,1)S(1)} %collective-permute-done.1.refs_1_) | copy-start | bytes 393220
  88.3 0.7 copy-start.6
  88.9 1.0 copy-start.1

commit v18 on v16

--- a/solution.py
+++ b/solution.py
@@ -165,13 +165,16 @@
     )
 
     target = sorted_place_per_element // rows_here
-    send_rank = rank_within_group(target, local_ids)
+
+    source = element_per_sorted_place // rows_here
+    within = element_per_sorted_place % rows_here
+
+    ranks = rank_within_group(
+        jnp.concatenate([target, source], axis=0), jnp.concatenate([local_ids, within], axis=0)
+    )
+    send_rank, recv_rank = ranks[:n_rounds], ranks[n_rounds:]
     send_row = target * per_peer + round_ids * capacity + send_rank
     send_hot = one_hot_rows(send_row, buffer_rows)
-
-    source = element_per_sorted_place // rows_here
-    within = element_per_sorted_place % rows_here
-    recv_rank = rank_within_group(source, within)
     recv_row = source * per_peer + round_ids * capacity + recv_rank
     recv_hot = one_hot_rows(recv_row, buffer_rows)
 

time: 163 us -> 163 us (level)
  no operation moved by 1% of the time
where the time goes in v18:
time: 163 us
  blocking collectives  123 us (75%)
  starting transfers between devices  20.2 us (12%)
  Pallas kernels  5.69 us (3%)
  other arithmetic  5.32 us (3%)
  waiting for transfers between devices  4.54 us (3%)
  matrix products  2.78 us (2%)
    all_to_all x1, blocking collectives, shards(): lax.all_to_all(outgoing, 'span', split_axis=0, concat_axis=0, tiled=True)  57.1 us
    all_to_all x1, blocking collectives, shards(): home = lax.all_to_all(back, 'span', split_axis=0, concat_axis=0, tiled=True)  53.8 us
    ppermute x4, starting transfers between devices, shards(): received.append(lax.ppermute(last_slice, ('span', 'head'), route))  16.7 us
    all_to_all x1, blocking collectives, shards(): lax.all_to_all(group_part.reshape(n_groups, rows_here // n_groups, group_...  11.8 us
    pallas_call x1, Pallas kernels, block_attention(): pl.pallas_call(block_attention_kernel, in_specs=[smem, smem, vmem, vmem,...  5.69 us
    ppermute x4, waiting for transfers between devices, shards(): received.append(lax.ppermute(last_slice, ('span', 'head'), route))  4.54 us
    all_to_all x1, starting transfers between devices, shards(): lax.all_to_all(copies, 'head', split_axis=0, concat_axis=0, tiled=True)  3.51 us
  transfers between devices with their start and end apart: 5, of which 2 were waited for; matrix products, arithmetic and copies ran while one was open for 0% of the time, Pallas kernels for 0%

profile of v18, /device:TPU:6, one launch (start us, length us, event | category | flops | bytes accessed | tf_op | source)
XLA Modules:
  0.0 162.7 jit_solution(15260187241283974162)
XLA Ops:
  0.0 0.0 copy-start
  0.0 0.7 and_select_fusion.2
  0.8 0.7 and_select_fusion.1
  1.5 0.5 convert_reduce_fusion.1
  2.0 0.8 slice_add_fusion.1
  2.8 0.0 copy-start.2
  2.8 0.3 convert_reduce_fusion
  3.0 1.3 fusion.3
  4.3 57.1 %all_to_all.34 = bf16[128,8,256]{2,1,0:T(8,128)(2,1)S(1)} all-to-all(bf16[128,8,256]{2,1,0:T(8,128)(2,1)S(1)} %fusion.3), channel_id=1, replica_groups=mesh['span'=128,'head'=4] {'span'}, dimensions={0} | all-to-all | bytes 1048576 | tf_op jit(solution)/shard_map/all_to_all | solution.py:184
  61.4 0.0 copy-done.2
  61.4 0.5 fusion.4
  61.9 1.1 broadcast_in_dim.5
  62.9 3.5 %all-to-all-start.1 = ((bf16[4,2,256,256]{3,2,1,0:T(8,128)(2,1)}), bf16[4,2,256,256]{3,2,1,0:T(8,128)(2,1)S(1)}, u32[]{:S(2)}, u32[]{:S(2)}) async-start(bf16[4,2,256,256]{3,2,1,0:T(8,128)(2,1)} %broadcast_in_dim.5), calls=%async_computation.1 | async-start | bytes 2097152 | tf_op jit(solution)/shard_map/all_to_all | solution.py:190
  66.5 2.2 %collective-permute-start.3 = (bf16[2,128,256]{2,1,0:T(8,128)(2,1)S(1)}, bf16[2,128,256]{2,1,0:T(8,128)(2,1)S(1)}, u32[]{:S(2)}, u32[]{:S(2)}) collective-permute-start(bf16[2,128,256]{2,1,0:T(8,128)(2,1)S(1)} %slice.26), channel_id=1, source_target_pairs={{0,7},{1,4},{2,5},{3,6},{4,11},{5,8},{6,9},{7,10},{8,15},{9,12},{1... | collective-permute-start | bytes 393224 | tf_op jit(solution)/shard_map/ppermute | solution.py:199
  68.7 6.3 %collective-permute-start.2 = (bf16[2,128,256]{2,1,0:T(8,128)(2,1)S(1)}, bf16[2,128,256]{2,1,0:T(8,128)(2,1)S(1)}, u32[]{:S(2)}, u32[]{:S(2)}) collective-permute-start(bf16[2,128,256]{2,1,0:T(8,128)(2,1)S(1)} %slice.26), channel_id=1, source_target_pairs={{0,6},{1,7},{2,4},{3,5},{4,10},{5,11},{6,8},{7,9},{8,14},{9,15},{1... | collective-permute-start | bytes 393224 | tf_op jit(solution)/shard_map/ppermute | solution.py:199
  74.9 2.1 %collective-permute-start.1 = (bf16[2,128,256]{2,1,0:T(8,128)(2,1)S(1)}, bf16[2,128,256]{2,1,0:T(8,128)(2,1)S(1)}, u32[]{:S(2)}, u32[]{:S(2)}) collective-permute-start(bf16[2,128,256]{2,1,0:T(8,128)(2,1)S(1)} %slice.26), channel_id=1, source_target_pairs={{0,5},{1,6},{2,7},{3,4},{4,9},{5,10},{6,11},{7,8},{8,13},{9,14},{1... | collective-permute-start | bytes 393224 | tf_op jit(solution)/shard_map/ppermute | solution.py:199
  77.1 6.1 %collective-permute-start = (bf16[2,128,256]{2,1,0:T(8,128)(2,1)S(1)}, bf16[2,128,256]{2,1,0:T(8,128)(2,1)S(1)}, u32[]{:S(2)}, u32[]{:S(2)}) collective-permute-start(bf16[2,128,256]{2,1,0:T(8,128)(2,1)S(1)} %slice.26), channel_id=1, source_target_pairs={{0,4},{1,5},{2,6},{3,7},{4,8},{5,9},{6,10},{7,11},{8,12},{9,13},{1... | collective-permute-start | bytes 393224 | tf_op jit(solution)/shard_map/ppermute | solution.py:199
  83.2 0.6 and_select_fusion.3.order_ref
  83.8 0.0 collective-permute-done.3
  83.8 0.0 collective-permute-done.2
  83.8 1.1 collective-permute-done.1
  84.9 3.4 %collective-permute-done = bf16[2,128,256]{2,1,0:T(8,128)(2,1)S(1)} collective-permute-done((bf16[2,128,256]{2,1,0:T(8,128)(2,1)S(1)}, bf16[2,128,256]{2,1,0:T(8,128)(2,1)S(1)}, u32[]{:S(2)}, u32[]{:S(2)}) %collective-permute-start) | collective-permute-done | bytes 131104 | tf_op jit(solution)/shard_map/ppermute | solution.py:199
  88.3 0.0 all-to-all-done.1.here_ref
  88.3 0.0 copy-start.1
  88.3 0.9 pad_maximum_fusion.prior_ref
  89.3 0.2 copy-done.1
  89.5 5.7 %shard_map.73 = (bf16[1024,260]{1,0:T(8,128)(2,1)}, bf16[2,256,256]{2,1,0:T(8,128)(2,1)}, bf16[2,256,128]{2,1,0:T(8,128)(2,1)}) custom-call(f32[2]{0:T(128)} %sharp_ref.1, s32[4]{0:T(128)} %and_select_fusion.3.order_ref, bf16[4,2,128,256]{3,2,1,0:T(8,128)(2,1)} %pad_maximum_fusion.prior_ref, bf16[4,2,256,256]{3,2,1,0:T(8,128)(2,1)} %copy-done.1, ...), custom_call_target="tpu_custom_call" | custom-call | flops 1342177280 | bytes 3153920 | tf_op jit(solution)/shard_map/pallas_call | solution.py:113
  95.2 53.8 %all_to_all.35 = bf16[128,8,260]{2,1,0:T(8,128)(2,1)S(1)} all-to-all(bf16[128,8,260]{2,1,0:T(8,128)(2,1)} %bitcast.25), channel_id=1, replica_groups=mesh['span'=128,'head'=4] {'span'}, dimensions={0} | all-to-all | bytes 1064960 | tf_op jit(solution)/shard_map/all_to_all | solution.py:214
  149.0 0.7 fusion
  149.8 0.0 copy-done
  149.8 0.3 convolution_convert_fusion
  150.1 11.8 %all_to_all.36 = bf16[4,64,1024]{2,1,0:T(8,128)(2,1)S(1)} all-to-all(bf16[4,64,1024]{2,1,0:T(8,128)(2,1)S(1)} %bitcast.24), channel_id=1, replica_groups=mesh['span'=128,'head'=4] {'head'}, dimensions={0} | all-to-all | bytes 1048576 | tf_op jit(solution)/shard_map/all_to_all | solution.py:228
  161.9 0.7 reduce_sum.52
  (7 shorter events, 0.1 us)
Async XLA Ops:
  0.0 149.8 %copy-start = (bf16[256,1024]{1,0:T(8,128)(2,1)S(1)}, bf16[256,1024]{1,0:T(8,128)(2,1)}, u32[]{:S(2)}) copy-start(bf16[256,1024]{1,0:T(8,128)(2,1)} %param.10) | copy-start | bytes 1572868
  2.8 58.6 %copy-start.2 = (s32[2,256]{1,0:T(2,128)}, s32[2,256]{1,0:T(2,128)S(1)}, u32[]{:S(2)}) copy-start(s32[2,256]{1,0:T(2,128)S(1)} %get-tuple-element.17.place_ref) | copy-start | bytes 6148
  62.9 25.4 %all-to-all-start.1 = ((bf16[4,2,256,256]{3,2,1,0:T(8,128)(2,1)}), bf16[4,2,256,256]{3,2,1,0:T(8,128)(2,1)S(1)}, u32[]{:S(2)}, u32[]{:S(2)}) async-start(bf16[4,2,256,256]{3,2,1,0:T(8,128)(2,1)} %broadcast_in_dim.5), calls=%async_computation.1 | async-start | bytes 2097152 | tf_op jit(solution)/shard_map/all_to_all | solution.py:190
  66.5 17.3 %collective-permute-start.3 = (bf16[2,128,256]{2,1,0:T(8,128)(2,1)S(1)}, bf16[2,128,256]{2,1,0:T(8,128)(2,1)S(1)}, u32[]{:S(2)}, u32[]{:S(2)}) collective-permute-start(bf16[2,128,256]{2,1,0:T(8,128)(2,1)S(1)} %slice.26), channel_id=1, source_target_pairs={{0,7},{1,4},{2,5},{3,6},{4,11},{5,8},{6,9},{7,10},{8,15},{9,12},{1... | collective-permute-start | bytes 393224 | tf_op jit(solution)/shard_map/ppermute | solution.py:199
  68.7 15.1 %collective-permute-start.2 = (bf16[2,128,256]{2,1,0:T(8,128)(2,1)S(1)}, bf16[2,128,256]{2,1,0:T(8,128)(2,1)S(1)}, u32[]{:S(2)}, u32[]{:S(2)}) collective-permute-start(bf16[2,128,256]{2,1,0:T(8,128)(2,1)S(1)} %slice.26), channel_id=1, source_target_pairs={{0,6},{1,7},{2,4},{3,5},{4,10},{5,11},{6,8},{7,9},{8,14},{9,15},{1... | collective-permute-start | bytes 393224 | tf_op jit(solution)/shard_map/ppermute | solution.py:199
  74.9 10.0 %collective-permute-start.1 = (bf16[2,128,256]{2,1,0:T(8,128)(2,1)S(1)}, bf16[2,128,256]{2,1,0:T(8,128)(2,1)S(1)}, u32[]{:S(2)}, u32[]{:S(2)}) collective-permute-start(bf16[2,128,256]{2,1,0:T(8,128)(2,1)S(1)} %slice.26), channel_id=1, source_target_pairs={{0,5},{1,6},{2,7},{3,4},{4,9},{5,10},{6,11},{7,8},{8,13},{9,14},{1... | collective-permute-start | bytes 393224 | tf_op jit(solution)/shard_map/ppermute | solution.py:199
  77.1 11.2 %collective-permute-start = (bf16[2,128,256]{2,1,0:T(8,128)(2,1)S(1)}, bf16[2,128,256]{2,1,0:T(8,128)(2,1)S(1)}, u32[]{:S(2)}, u32[]{:S(2)}) collective-permute-start(bf16[2,128,256]{2,1,0:T(8,128)(2,1)S(1)} %slice.26), channel_id=1, source_target_pairs={{0,4},{1,5},{2,6},{3,7},{4,8},{5,9},{6,10},{7,11},{8,12},{9,13},{1... | collective-permute-start | bytes 393224 | tf_op jit(solution)/shard_map/ppermute | solution.py:199
  88.3 1.2 copy-start.1

commit v19 on v16

--- a/solution.py
+++ b/solution.py
@@ -183,7 +183,12 @@
         "rsq,qf->rsf", recv_hot, incoming, preferred_element_type=jnp.float32
     ).astype(jnp.bfloat16)
     n_groups = lax.axis_size("head")
-    copies = jnp.broadcast_to(arrived[None], (n_groups,) + arrived.shape)
+    copies = jnp.einsum(
+        "grsq,qf->grsf",
+        jnp.broadcast_to(recv_hot[None], (n_groups,) + recv_hot.shape),
+        incoming,
+        preferred_element_type=jnp.float32,
+    ).astype(jnp.bfloat16)
     gathered = lax.all_to_all(copies, "head", split_axis=0, concat_axis=0, tiled=True)
     last_slice = arrived[:, rows_here - BLOCK :]
     received = []

time: 163 us -> 166 us (1.018)
  blocking collectives: 123 us -> 65.8 us
  waiting for transfers between devices: 4.53 us -> 40.1 us
  starting transfers between devices: 20.2 us -> 41.9 us
  matrix products: 2.79 us -> 5.82 us
    all_to_all x1 -> x0, blocking collectives: 57.1 us -> none  [shards(): lax.all_to_all(outgoing, 'span', split_axis=0, concat_axis=0, tiled=True)]
    all_to_all x0 -> x1, waiting for transfers between devices: none -> 35 us  [shards(): lax.all_to_all(outgoing, 'span', split_axis=0, concat_axis=0, tiled=True)]
    all_to_all x0 -> x1, starting transfers between devices: none -> 22 us  [shards(): lax.all_to_all(outgoing, 'span', split_axis=0, concat_axis=0, tiled=True)]
    dot_general x0 -> x1, matrix products: none -> 2.25 us  [shards(): jnp.einsum('grsq,qf->grsf', jnp.broadcast_to(recv_hot[None], (n_groups,)...]
  transfers between devices with their start and end apart: 5 -> 6, of which waited for: 2 -> 3; matrix products, arithmetic and copies ran while one was open for 0% -> 1% of each run, Pallas kernels for 0% -> 0%
where the time goes in v19:
time: 166 us; the launch traced here: 165 us
  blocking collectives  65.8 us (40%)
  starting transfers between devices  41.9 us (25%)
  waiting for transfers between devices  40.1 us (24%)
  matrix products  5.82 us (4%)
  Pallas kernels  5.68 us (3%)
  other arithmetic  5.51 us (3%)
    all_to_all x1, blocking collectives, shards(): home = lax.all_to_all(back, 'span', split_axis=0, concat_axis=0, tiled=True)  54.4 us
    all_to_all x1, waiting for transfers between devices, shards(): lax.all_to_all(outgoing, 'span', split_axis=0, concat_axis=0, tiled=True)  35 us
    all_to_all x1, starting transfers between devices, shards(): lax.all_to_all(outgoing, 'span', split_axis=0, concat_axis=0, tiled=True)  22 us
    ppermute x4, starting transfers between devices, shards(): received.append(lax.ppermute(last_slice, ('span', 'head'), route))  16.4 us
    all_to_all x1, blocking collectives, shards(): lax.all_to_all(group_part.reshape(n_groups, rows_here // n_groups, group_...  11.4 us
    pallas_call x1, Pallas kernels, block_attention(): pl.pallas_call(block_attention_kernel, in_specs=[smem, smem, vmem, vmem,...  5.68 us
    ppermute x4, waiting for transfers between devices, shards(): received.append(lax.ppermute(last_slice, ('span', 'head'), route))  5.03 us
    all_to_all x1, starting transfers between devices, shards(): lax.all_to_all(copies, 'head', split_axis=0, concat_axis=0, tiled=True)  3.51 us
  transfers between devices with their start and end apart: 6, of which 3 were waited for; matrix products, arithmetic and copies ran while one was open for 1% of the time, Pallas kernels for 0%

profile of v19, /device:TPU:6, one launch (start us, length us, event | category | flops | bytes accessed | tf_op | source)
XLA Modules:
  0.0 165.2 jit_solution(14845648630786528432)
XLA Ops:
  0.0 0.0 copy-start
  0.0 0.7 and_select_fusion.1
  0.8 0.7 and_select_fusion.2
  1.5 0.5 convert_reduce_fusion.1
  1.9 0.8 add_add_fusion
  2.7 0.0 copy-start.2
  2.7 0.3 convert_reduce_fusion
  3.0 2.0 %fusion.9 = bf16[128,8,256]{2,1,0:T(8,128)(2,1)} fusion(bf16[256,1024]{1,0:T(8,128)(2,1)S(1)} %convert_reduce_fusion, bf16[256,256]{1,0:T(8,128)(2,1)} %param.7), kind=kOutput, calls=%fused_computation.12 | convolution fusion | flops 134217728 | bytes 1179648 | tf_op jit(solution)/shard_map/rtq,tf->qf/dot_general | solution.py:178
  5.0 22.0 %all-to-all-start = ((bf16[128,8,256]{2,1,0:T(8,128)(2,1)}), bf16[128,8,256]{2,1,0:T(8,128)(2,1)S(1)}, u32[]{:S(2)}, u32[]{:S(2)}) async-start(bf16[128,8,256]{2,1,0:T(8,128)(2,1)} %fusion.9), calls=%async_computation | async-start | bytes 1048576 | tf_op jit(solution)/shard_map/all_to_all | solution.py:181
  27.0 0.2 fusion
  27.3 35.0 %all-to-all-done = bf16[128,8,256]{2,1,0:T(8,128)(2,1)S(1)} async-done(((bf16[128,8,256]{2,1,0:T(8,128)(2,1)}), bf16[128,8,256]{2,1,0:T(8,128)(2,1)S(1)}, u32[]{:S(2)}, u32[]{:S(2)}) %all-to-all-start) | async-done | bytes 524320 | tf_op jit(solution)/shard_map/all_to_all | solution.py:181
  62.3 2.2 %fusion.6 = bf16[4,2,256,256]{3,2,1,0:T(8,128)(2,1)} fusion(bf16[2,256,1024]{2,1,0:T(8,128)(2,1)S(1)} %fusion, bf16[128,8,256]{2,1,0:T(8,128)(2,1)S(1)} %all-to-all-done), kind=kOutput, calls=%fused_computation.9 | convolution fusion | flops 1074266112 | bytes 2621440 | tf_op jit(solution)/shard_map/grsq,qf->grsf/dot_general | solution.py:186
  64.6 3.5 %all-to-all-start.1 = ((bf16[4,2,256,256]{3,2,1,0:T(8,128)(2,1)}), bf16[4,2,256,256]{3,2,1,0:T(8,128)(2,1)S(1)}, u32[]{:S(2)}, u32[]{:S(2)}) async-start(bf16[4,2,256,256]{3,2,1,0:T(8,128)(2,1)} %fusion.6), calls=%async_computation.1 | async-start | bytes 2097152 | tf_op jit(solution)/shard_map/all_to_all | solution.py:192
  68.1 0.0 copy-done.2
  68.1 0.5 fusion.1
  68.6 1.9 %collective-permute-start = (bf16[2,128,256]{2,1,0:T(8,128)(2,1)S(1)}, bf16[2,128,256]{2,1,0:T(8,128)(2,1)S(1)}, u32[]{:S(2)}, u32[]{:S(2)}) collective-permute-start(bf16[2,128,256]{2,1,0:T(8,128)(2,1)S(1)} %slice.34), channel_id=1, source_target_pairs={{0,4},{1,5},{2,6},{3,7},{4,8},{5,9},{6,10},{7,11},{8,12},{9,13},{1... | collective-permute-start | bytes 393224 | tf_op jit(solution)/shard_map/ppermute | solution.py:201
  70.5 6.5 %collective-permute-start.1 = (bf16[2,128,256]{2,1,0:T(8,128)(2,1)S(1)}, bf16[2,128,256]{2,1,0:T(8,128)(2,1)S(1)}, u32[]{:S(2)}, u32[]{:S(2)}) collective-permute-start(bf16[2,128,256]{2,1,0:T(8,128)(2,1)S(1)} %slice.34), channel_id=1, source_target_pairs={{0,5},{1,6},{2,7},{3,4},{4,9},{5,10},{6,11},{7,8},{8,13},{9,14},{1... | collective-permute-start | bytes 393224 | tf_op jit(solution)/shard_map/ppermute | solution.py:201
  77.1 3.3 %collective-permute-start.2 = (bf16[2,128,256]{2,1,0:T(8,128)(2,1)S(1)}, bf16[2,128,256]{2,1,0:T(8,128)(2,1)S(1)}, u32[]{:S(2)}, u32[]{:S(2)}) collective-permute-start(bf16[2,128,256]{2,1,0:T(8,128)(2,1)S(1)} %slice.34), channel_id=1, source_target_pairs={{0,6},{1,7},{2,4},{3,5},{4,10},{5,11},{6,8},{7,9},{8,14},{9,15},{1... | collective-permute-start | bytes 393224 | tf_op jit(solution)/shard_map/ppermute | solution.py:201
  80.3 4.7 %collective-permute-start.3 = (bf16[2,128,256]{2,1,0:T(8,128)(2,1)S(1)}, bf16[2,128,256]{2,1,0:T(8,128)(2,1)S(1)}, u32[]{:S(2)}, u32[]{:S(2)}) collective-permute-start(bf16[2,128,256]{2,1,0:T(8,128)(2,1)S(1)} %slice.34), channel_id=1, source_target_pairs={{0,7},{1,4},{2,5},{3,6},{4,11},{5,8},{6,9},{7,10},{8,15},{9,12},{1... | collective-permute-start | bytes 393224 | tf_op jit(solution)/shard_map/ppermute | solution.py:201
  85.0 0.6 and_select_fusion.3.order_ref
  85.6 0.0 collective-permute-done
  85.6 0.0 collective-permute-done.1
  85.6 3.6 %collective-permute-done.2 = bf16[2,128,256]{2,1,0:T(8,128)(2,1)S(1)} collective-permute-done((bf16[2,128,256]{2,1,0:T(8,128)(2,1)S(1)}, bf16[2,128,256]{2,1,0:T(8,128)(2,1)S(1)}, u32[]{:S(2)}, u32[]{:S(2)}) %collective-permute-start.2) | collective-permute-done | bytes 131104 | tf_op jit(solution)/shard_map/ppermute | solution.py:201
  89.2 1.4 collective-permute-done.3
  90.7 0.0 all-to-all-done.1.here_ref
  90.7 0.0 copy-start.1
  90.7 0.9 pad_maximum_fusion.prior_ref
  91.6 0.2 copy-done.1
  91.8 5.7 %shard_map.73 = (bf16[1024,260]{1,0:T(8,128)(2,1)}, bf16[2,256,256]{2,1,0:T(8,128)(2,1)}, bf16[2,256,128]{2,1,0:T(8,128)(2,1)}) custom-call(f32[2]{0:T(128)} %sharp_ref.1, s32[4]{0:T(128)} %and_select_fusion.3.order_ref, bf16[4,2,128,256]{3,2,1,0:T(8,128)(2,1)} %pad_maximum_fusion.prior_ref, bf16[4,2,256,256]{3,2,1,0:T(8,128)(2,1)} %copy-done.1, ...), custom_call_target="tpu_custom_call" | custom-call | flops 1342177280 | bytes 3153920 | tf_op jit(solution)/shard_map/pallas_call | solution.py:113
  97.5 54.4 %all_to_all.34 = bf16[128,8,260]{2,1,0:T(8,128)(2,1)S(1)} all-to-all(bf16[128,8,260]{2,1,0:T(8,128)(2,1)} %bitcast.31), channel_id=1, replica_groups=mesh['span'=128,'head'=4] {'span'}, dimensions={0} | all-to-all | bytes 1064960 | tf_op jit(solution)/shard_map/all_to_all | solution.py:216
  151.9 0.7 fusion.2
  152.7 0.0 copy-done
  152.7 0.3 convolution_convert_fusion
  153.0 11.4 %all_to_all.35 = bf16[4,64,1024]{2,1,0:T(8,128)(2,1)S(1)} all-to-all(bf16[4,64,1024]{2,1,0:T(8,128)(2,1)S(1)} %bitcast.30), channel_id=1, replica_groups=mesh['span'=128,'head'=4] {'head'}, dimensions={0} | all-to-all | bytes 1048576 | tf_op jit(solution)/shard_map/all_to_all | solution.py:230
  164.4 0.7 reduce_sum.62
  (6 shorter events, 0.1 us)
Async XLA Ops:
  0.0 152.7 %copy-start = (bf16[256,1024]{1,0:T(8,128)(2,1)S(1)}, bf16[256,1024]{1,0:T(8,128)(2,1)}, u32[]{:S(2)}) copy-start(bf16[256,1024]{1,0:T(8,128)(2,1)} %param.10) | copy-start | bytes 1572868
  2.7 65.4 %copy-start.2 = (s32[2,256]{1,0:T(2,128)}, s32[2,256]{1,0:T(2,128)S(1)}, u32[]{:S(2)}) copy-start(s32[2,256]{1,0:T(2,128)S(1)} %get-tuple-element.19.place_ref) | copy-start | bytes 6148
  5.0 57.3 %all-to-all-start = ((bf16[128,8,256]{2,1,0:T(8,128)(2,1)}), bf16[128,8,256]{2,1,0:T(8,128)(2,1)S(1)}, u32[]{:S(2)}, u32[]{:S(2)}) async-start(bf16[128,8,256]{2,1,0:T(8,128)(2,1)} %fusion.9), calls=%async_computation | async-start | bytes 1048576 | tf_op jit(solution)/shard_map/all_to_all | solution.py:181
  64.6 26.1 %all-to-all-start.1 = ((bf16[4,2,256,256]{3,2,1,0:T(8,128)(2,1)}), bf16[4,2,256,256]{3,2,1,0:T(8,128)(2,1)S(1)}, u32[]{:S(2)}, u32[]{:S(2)}) async-start(bf16[4,2,256,256]{3,2,1,0:T(8,128)(2,1)} %fusion.6), calls=%async_computation.1 | async-start | bytes 2097152 | tf_op jit(solution)/shard_map/all_to_all | solution.py:192
  68.6 17.0 %collective-permute-start = (bf16[2,128,256]{2,1,0:T(8,128)(2,1)S(1)}, bf16[2,128,256]{2,1,0:T(8,128)(2,1)S(1)}, u32[]{:S(2)}, u32[]{:S(2)}) collective-permute-start(bf16[2,128,256]{2,1,0:T(8,128)(2,1)S(1)} %slice.34), channel_id=1, source_target_pairs={{0,4},{1,5},{2,6},{3,7},{4,8},{5,9},{6,10},{7,11},{8,12},{9,13},{1... | collective-permute-start | bytes 393224 | tf_op jit(solution)/shard_map/ppermute | solution.py:201
  70.5 15.1 %collective-permute-start.1 = (bf16[2,128,256]{2,1,0:T(8,128)(2,1)S(1)}, bf16[2,128,256]{2,1,0:T(8,128)(2,1)S(1)}, u32[]{:S(2)}, u32[]{:S(2)}) collective-permute-start(bf16[2,128,256]{2,1,0:T(8,128)(2,1)S(1)} %slice.34), channel_id=1, source_target_pairs={{0,5},{1,6},{2,7},{3,4},{4,9},{5,10},{6,11},{7,8},{8,13},{9,14},{1... | collective-permute-start | bytes 393224 | tf_op jit(solution)/shard_map/ppermute | solution.py:201
  77.1 12.2 %collective-permute-start.2 = (bf16[2,128,256]{2,1,0:T(8,128)(2,1)S(1)}, bf16[2,128,256]{2,1,0:T(8,128)(2,1)S(1)}, u32[]{:S(2)}, u32[]{:S(2)}) collective-permute-start(bf16[2,128,256]{2,1,0:T(8,128)(2,1)S(1)} %slice.34), channel_id=1, source_target_pairs={{0,6},{1,7},{2,4},{3,5},{4,10},{5,11},{6,8},{7,9},{8,14},{9,15},{1... | collective-permute-start | bytes 393224 | tf_op jit(solution)/shard_map/ppermute | solution.py:201
  80.3 10.3 %collective-permute-start.3 = (bf16[2,128,256]{2,1,0:T(8,128)(2,1)S(1)}, bf16[2,128,256]{2,1,0:T(8,128)(2,1)S(1)}, u32[]{:S(2)}, u32[]{:S(2)}) collective-permute-start(bf16[2,128,256]{2,1,0:T(8,128)(2,1)S(1)} %slice.34), channel_id=1, source_target_pairs={{0,7},{1,4},{2,5},{3,6},{4,11},{5,8},{6,9},{7,10},{8,15},{9,12},{1... | collective-permute-start | bytes 393224 | tf_op jit(solution)/shard_map/ppermute | solution.py:201
  90.7 1.2 copy-start.1
